TPU v7x, 512 devices: a whole 4x8x8 slice. The times are simulated.
512 devices in a mesh: space: 32 (over y_lo, z), field: 16 (over x, y_hi, core).
Axes of the slice: x: 4, y: 8 (y_hi: 2, y_lo: 4; y = y_hi * 4 + y_lo), z: 8, core: 2. Of those that a mesh axis runs over, the one named last changes fastest.
Arguments:
- fields: float32 [16, 1024, 6144], P('field', 'space'), may hold values from -6 to 6
- zone_ids: int32 [1024, 6144], P('space'), may hold values from 0 to 7
- diffusivity: float32 [16, 8], P('field'), may hold values from 0.3 to 3
- heat_rate: float32 [15], replicated, may hold values from 0.3 to 1.5
- weight_in: bfloat16 [384, 16], replicated, may hold values from -1.5 to 1.5
- bias_in: float32 [384], replicated, may hold values from -3 to 3
- weight_mid: bfloat16 [384, 384], replicated, may hold values from -0.3125 to 0.3125
- bias_mid: float32 [384], replicated, may hold values from -3 to 3
- weight_out: bfloat16 [16, 384], replicated, may hold values from -0.3125 to 0.3125
- bias_out: float32 [16], replicated, may hold values from -2 to 2
Outputs:
- new_fields: float32 [16, 1024, 6144], P('field', 'space')
All inputs are finite; a program needn't handle non-finite values.
Results may differ from a plain program's by a relative error of at most 0.005.
Values may be sent and summed in bfloat16 or wider, within the bound.
No kernel may reach another device: no remote copies, remote signals or barrier semaphores. Data moves between devices by JAX's collectives and lax.ppermute only.
A program may use at most 64 MiB of HBM per device.

v0:
```python
import jax
import jax.numpy as jnp
from jax import lax
from jax.sharding import PartitionSpec as P

FIELDS = 16
SWEEPS = 3
ROWS_BLK = 1024


RELAX_WEIGHTS = (0.8, 1.25, 0.95)


def extended(cells, sides, width):
    for axis, dim in sides:
        count = lax.axis_size(axis)
        ends = count - 1
        head = lax.slice_in_dim(cells, 0, width, axis=dim)
        tail = lax.slice_in_dim(cells, cells.shape[dim] - width, cells.shape[dim], axis=dim)
        cells = jnp.concatenate(
            [
                lax.ppermute(tail, axis, [(i, (i + 1) % count) for i in range(ends)]),
                cells,
                lax.ppermute(head, axis, [((i + 1) % count, i) for i in range(ends)]),
            ],
            axis=dim,
        )
    return cells


def from_root(block, axis, holder):
    block = jnp.where(lax.axis_index(axis) == holder, block, jnp.zeros_like(block))
    return lax.psum(block, axis)


def relax_step(padded, source, coef_pad, weight):
    middle = padded[:, 1:-1]
    coef_mid = coef_pad[:, 1:-1]
    face_north = 0.5 * (coef_mid + coef_pad[:, 2:])
    face_south = 0.5 * (coef_mid + coef_pad[:, :-2])
    face_east = 0.5 * (coef_mid + jnp.roll(coef_mid, -1, 2))
    face_west = 0.5 * (coef_mid + jnp.roll(coef_mid, 1, 2))
    diagonal = 1.0 + face_north + face_south + face_east + face_west
    image = diagonal * middle - face_north * padded[:, 2:] - face_south * padded[:, :-2]
    image = image - face_east * jnp.roll(middle, -1, 2) - face_west * jnp.roll(middle, 1, 2)
    return middle + weight * (source - image) / diagonal


def lookup(zone_ids, diffusivity):
    coefs = jnp.zeros((diffusivity.shape[0],) + zone_ids.shape, jnp.float32)
    for number in range(diffusivity.shape[1]):
        coefs = coefs + jnp.where(
            (zone_ids == number)[None], diffusivity[:, number][:, None, None], jnp.float32(0.0)
        )
    return coefs


def on_device(
    fields,
    zone_ids,
    diffusivity,
    heat_rate,
    weight_in,
    bias_in,
    weight_mid,
    bias_mid,
    weight_out,
    bias_out,
):
    count_here, rows_here, columns = fields.shape
    coefs = lookup(zone_ids, diffusivity)
    stacked = extended(jnp.stack([fields, coefs]), (("space", 2),), 1)
    coef_pad = stacked[1]
    state = relax_step(stacked[0], fields, coef_pad, RELAX_WEIGHTS[0])
    for number in range(1, SWEEPS):
        padded = extended(state, (("space", 1),), 1)
        state = relax_step(padded, fields, coef_pad, RELAX_WEIGHTS[number])
    span = ROWS_BLK * lax.axis_size("field")
    blocks = rows_here * columns // span
    by_block = state.reshape(count_here, blocks, span)

    def one_block(row_block):
        hidden = jax.nn.silu(
            jnp.dot(weight_in, row_block, preferred_element_type=jnp.float32) + bias_in[:, None]
        ).astype(jnp.bfloat16)
        hidden = jax.nn.silu(
            jnp.dot(weight_mid, hidden, preferred_element_type=jnp.float32) + bias_mid[:, None]
        ).astype(jnp.bfloat16)
        return (
            jnp.dot(weight_out, hidden, preferred_element_type=jnp.float32) + bias_out[:, None]
        ).astype(jnp.bfloat16)

    moved = jnp.moveaxis(
        lax.all_to_all(
            by_block.astype(jnp.bfloat16), "field", split_axis=2, concat_axis=0, tiled=True
        ),
        1,
        0,
    )
    change = jnp.moveaxis(lax.map(one_block, moved), 0, 1)
    change = lax.all_to_all(change, "field", split_axis=0, concat_axis=2, tiled=True).astype(
        jnp.float32
    )
    heat_local = by_block[-1] + change[-1]
    heat_new = from_root(heat_local, "field", lax.axis_size("field") - 1)
    first_field = lax.axis_index("field") * count_here
    rate_pad = jnp.concatenate([heat_rate, jnp.zeros((1,), jnp.float32)], 0)
    rate_here = lax.dynamic_slice_in_dim(rate_pad, first_field, count_here)
    factor = jnp.exp(rate_here[:, None, None] * jnp.tanh(heat_new)[None])
    result = by_block + (change * factor).astype(jnp.bfloat16).astype(jnp.float32)
    field_ids = first_field + jnp.arange(count_here, dtype=jnp.int32)
    result = jnp.where((field_ids == FIELDS - 1)[:, None, None], heat_new[None], result)
    return result.reshape(count_here, rows_here, columns)


def solution(mesh):
    return jax.shard_map(
        on_device,
        mesh=mesh,
        in_specs=(
            P("field", "space", None),
            P("space", None),
            P("field", None),
            P(),
            P(),
            P(),
            P(),
            P(),
            P(),
            P(),
        ),
        out_specs=P("field", "space", None),
        check_vma=False,
    )
```

profile of v0, /device:TPU:1, one launch (start us, length us, event | category | flops | bytes accessed | tf_op | source)
XLA Modules:
  0.0 460.7 jit_solution(11899596553922637642)
XLA Ops:
  6.5 1.6 fusion.65
  8.2 6.7 %add_bitcast_fusion = f32[1,1,32,6144]{3,2,1,0:T(8,128)S(1)} fusion(s32[32,6144]{1,0:T(8,128)} %param.13, f32[]{:T(128)} %bitcast.13, f32[]{:T(128)} %bitcast.12, f32[]{:T(128)} %bitcast.11, f32[]{:T(128)} %bitcast.10, f32[]{:T(128)} %bitcast.9, f32[]{:T(128)} %bitcast.8, f32[]{:T(128)} %bitcast.7, f32[]{:T(128)} %bitcast.6), kind=kLoop, calls=%fused_computation.80 | loop fusion | flops 4521984 | bytes 1572896 | tf_op jit(solution)/shard_map/stack | solution.py:72
  14.9 4.8 %collective-permute-start = (f32[2,1,1,6144]{3,2,1,0:T(1,128)S(1)}, f32[2,1,1,6144]{3,2,1,0:T(1,128)S(1)}, u32[]{:S(2)}, u32[]{:S(2)}) collective-permute-start(f32[2,1,1,6144]{3,2,1,0:T(1,128)S(1)} %get-tuple-element.78), channel_id=1, source_target_pairs={{0,16},{16,32},{32,48},{48,64},{64,80},{80,96},{96,112},{112,128},... | collective-permute-start | bytes 147464 | tf_op jit(solution)/shard_map/ppermute | solution.py:22
  19.8 1.3 collective-permute-start.1
  21.1 4.2 collective-permute-done.1
  27.6 1.3 collective-permute-start.2
  28.9 4.6 %collective-permute-start.3 = (f32[1,1,6144]{2,1,0:T(1,128)S(1)}, f32[1,1,6144]{2,1,0:T(1,128)S(1)}, u32[]{:S(2)}, u32[]{:S(2)}) collective-permute-start(f32[1,1,6144]{2,1,0:T(1,128)S(1)} %get-tuple-element.99), channel_id=1, source_target_pairs={{0,16},{16,32},{32,48},{48,64},{64,80},{80,96},{96,112},{112,128},... | collective-permute-start | bytes 73736 | tf_op jit(solution)/shard_map/ppermute | solution.py:22
  35.6 1.3 collective-permute-start.4
  36.9 6.0 %collective-permute-start.5 = (f32[1,1,6144]{2,1,0:T(1,128)S(1)}, f32[1,1,6144]{2,1,0:T(1,128)S(1)}, u32[]{:S(2)}, u32[]{:S(2)}) collective-permute-start(f32[1,1,6144]{2,1,0:T(1,128)S(1)} %get-tuple-element.89), channel_id=1, source_target_pairs={{0,16},{16,32},{32,48},{48,64},{64,80},{80,96},{96,112},{112,128},... | collective-permute-start | bytes 73736 | tf_op jit(solution)/shard_map/ppermute | solution.py:22
  45.2 12.8 %copy.13 = bf16[1,12,16384]{1,0,2:T(2,128)(2,1)} copy(bf16[1,12,16384]{2,1,0:T(8,128)(2,1)S(1)} %convert_element_type.50) | data formatting | bytes 786432 | tf_op jit(solution)/shard_map/convert_element_type | solution.py:95
  58.5 90.8 %reduce = bf16[16384,12]{1,0:T(8,128)(2,1)} reduce(bf16[16384,1,12]{2,1,0:T(2,128)(2,1)} %bitcast.109, bf16[]{:T(256)} %broadcast.69), dimensions={1}, to_apply=%bitcast.85.reduce_sub_computation | reduce | bytes 786434
  149.3 9.5 %reshape.89 = bf16[16,2,6144]{2,1,0:T(2,128)(2,1)} reshape(bf16[16384,12]{1,0:T(8,128)(2,1)} %reduce) | data formatting | bytes 786432
  158.9 13.1 %all-to-all-start = ((bf16[16,2,6144]{2,1,0:T(2,128)(2,1)}), bf16[16,2,6144]{2,1,0:T(2,128)(2,1)S(1)}, u32[]{:S(2)}, u32[]{:S(2)}) async-start(bf16[16,2,6144]{2,1,0:T(2,128)(2,1)} %reshape.89), calls=%async_computation | async-start | bytes 786432 | tf_op jit(solution)/shard_map/all_to_all | solution.py:94
  172.0 12.3 %all-to-all-done = bf16[16,2,6144]{2,1,0:T(2,128)(2,1)S(1)} async-done(((bf16[16,2,6144]{2,1,0:T(2,128)(2,1)}), bf16[16,2,6144]{2,1,0:T(2,128)(2,1)S(1)}, u32[]{:S(2)}, u32[]{:S(2)}) %all-to-all-start) | async-done | bytes 393248 | tf_op jit(solution)/shard_map/all_to_all | solution.py:94
  184.3 12.2 %reshape.90 = bf16[16384,1,12]{2,1,0:T(2,128)(2,1)} reshape(bf16[16,2,6144]{2,1,0:T(2,128)(2,1)S(1)} %all-to-all-done) | data formatting | bytes 786432
  196.5 15.4 %copy.14 = bf16[1,12,16384]{2,1,0:T(8,128)(2,1)S(1)} copy(bf16[1,12,16384]{1,0,2:T(2,128)(2,1)} %bitcast.110) | data formatting | bytes 786432 | tf_op jit(solution)/shard_map/all_to_all | solution.py:94
  212.9 19.7 %while.10 = (s32[]{:T(128)}, bf16[12,16,1024]{2,1,0:T(8,128)(2,1)S(1)}, bf16[12,16,1024]{2,1,0:T(8,128)(2,1)S(1)}, bf16[384,16]{0,1:T(8,128)(2,1)S(1)}, f32[384]...) while((s32[]{:T(128)}, ...), condition=%wide.region_1.2_spmd, body=%wide.region_0.1_spmd.sunk | while | flops 331907072 | bytes 1962605 | solution.py:100
  232.6 1.1 copy.22
  233.6 4.5 all-to-all-start.1
  238.5 13.4 %all-to-all-done.1 = bf16[16,12,1024]{2,1,0:T(8,128)(2,1)S(1)} async-done(((bf16[16,12,1024]{2,1,0:T(8,128)(2,1)}), bf16[16,12,1024]{2,1,0:T(8,128)(2,1)S(1)}, u32[]{:S(2)}, u32[]{:S(2)}) %all-to-all-start.1) | async-done | bytes 393248 | tf_op jit(solution)/shard_map/all_to_all | solution.py:101
  253.3 1.1 add_select_fusion.1
  255.0 195.6 %all-reduce.2.cloned.1.call-done = f32[12,16384]{1,0:T(8,128)} async-done(((f32[12,16384]{1,0:T(8,128)}), f32[12,16384]{1,0:T(8,128)}) %all-reduce.2.cloned.1.call-update) | async-done | bytes 786448 | tf_op jit(solution)/shard_map/psum | solution.py:33
  450.6 2.2 add_select_fusion
  452.7 1.1 reshape.86
  (73 shorter events, 30.1 us)
Async XLA Ops:
  6.5 8.3 %copy-start = (f32[1,32,6144]{2,1,0:T(8,128)S(1)}, f32[1,32,6144]{2,1,0:T(8,128)}, u32[]{:S(2)}) copy-start(f32[1,32,6144]{2,1,0:T(8,128)} %param.12) | copy-start | bytes 2359300
  14.9 6.1 %collective-permute-start = (f32[2,1,1,6144]{3,2,1,0:T(1,128)S(1)}, f32[2,1,1,6144]{3,2,1,0:T(1,128)S(1)}, u32[]{:S(2)}, u32[]{:S(2)}) collective-permute-start(f32[2,1,1,6144]{3,2,1,0:T(1,128)S(1)} %get-tuple-element.78), channel_id=1, source_target_pairs={{0,16},{16,32},{32,48},{48,64},{64,80},{80,96},{96,112},{112,128},... | collective-permute-start | bytes 147464 | tf_op jit(solution)/shard_map/ppermute | solution.py:22
  19.8 5.5 %collective-permute-start.1 = (f32[2,1,1,6144]{3,2,1,0:T(1,128)S(1)}, f32[2,1,1,6144]{3,2,1,0:T(1,128)S(1)}, u32[]{:S(2)}, u32[]{:S(2)}) collective-permute-start(f32[2,1,1,6144]{3,2,1,0:T(1,128)S(1)} %get-tuple-element.79), channel_id=1, source_target_pairs={{16,0},{32,16},{48,32},{64,48},{80,64},{96,80},{112,96},{128,112},... | collective-permute-start | bytes 147464 | tf_op jit(solution)/shard_map/ppermute | solution.py:24
  27.6 6.0 %collective-permute-start.2 = (f32[1,1,6144]{2,1,0:T(1,128)S(1)}, f32[1,1,6144]{2,1,0:T(1,128)S(1)}, u32[]{:S(2)}, u32[]{:S(2)}) collective-permute-start(f32[1,1,6144]{2,1,0:T(1,128)S(1)} %get-tuple-element.98), channel_id=1, source_target_pairs={{16,0},{32,16},{48,32},{64,48},{80,64},{96,80},{112,96},{128,112},... | collective-permute-start | bytes 73736 | tf_op jit(solution)/shard_map/ppermute | solution.py:24
  28.9 5.6 %collective-permute-start.3 = (f32[1,1,6144]{2,1,0:T(1,128)S(1)}, f32[1,1,6144]{2,1,0:T(1,128)S(1)}, u32[]{:S(2)}, u32[]{:S(2)}) collective-permute-start(f32[1,1,6144]{2,1,0:T(1,128)S(1)} %get-tuple-element.99), channel_id=1, source_target_pairs={{0,16},{16,32},{32,48},{48,64},{64,80},{80,96},{96,112},{112,128},... | collective-permute-start | bytes 73736 | tf_op jit(solution)/shard_map/ppermute | solution.py:22
  35.6 7.4 %collective-permute-start.4 = (f32[1,1,6144]{2,1,0:T(1,128)S(1)}, f32[1,1,6144]{2,1,0:T(1,128)S(1)}, u32[]{:S(2)}, u32[]{:S(2)}) collective-permute-start(f32[1,1,6144]{2,1,0:T(1,128)S(1)} %get-tuple-element.88), channel_id=1, source_target_pairs={{16,0},{32,16},{48,32},{64,48},{80,64},{96,80},{112,96},{128,112},... | collective-permute-start | bytes 73736 | tf_op jit(solution)/shard_map/ppermute | solution.py:24
  36.9 6.8 %collective-permute-start.5 = (f32[1,1,6144]{2,1,0:T(1,128)S(1)}, f32[1,1,6144]{2,1,0:T(1,128)S(1)}, u32[]{:S(2)}, u32[]{:S(2)}) collective-permute-start(f32[1,1,6144]{2,1,0:T(1,128)S(1)} %get-tuple-element.89), channel_id=1, source_target_pairs={{0,16},{16,32},{32,48},{48,64},{64,80},{80,96},{96,112},{112,128},... | collective-permute-start | bytes 73736 | tf_op jit(solution)/shard_map/ppermute | solution.py:22
  158.9 25.4 %all-to-all-start = ((bf16[16,2,6144]{2,1,0:T(2,128)(2,1)}), bf16[16,2,6144]{2,1,0:T(2,128)(2,1)S(1)}, u32[]{:S(2)}, u32[]{:S(2)}) async-start(bf16[16,2,6144]{2,1,0:T(2,128)(2,1)} %reshape.89), calls=%async_computation | async-start | bytes 786432 | tf_op jit(solution)/shard_map/all_to_all | solution.py:94
  211.9 1.0 copy-start.1
  211.9 1.0 copy-start.2
  211.9 0.9 copy-start.3
  211.9 0.9 copy-start.4
  211.9 0.9 copy-start.5
  212.0 0.9 copy-start.6
  233.6 18.3 %all-to-all-start.1 = ((bf16[16,12,1024]{2,1,0:T(8,128)(2,1)}), bf16[16,12,1024]{2,1,0:T(8,128)(2,1)S(1)}, u32[]{:S(2)}, u32[]{:S(2)}) async-start(bf16[16,12,1024]{2,1,0:T(8,128)(2,1)} %bitcast.92), calls=%async_computation.1 | async-start | bytes 1048576 | tf_op jit(solution)/shard_map/all_to_all | solution.py:101
  238.2 212.4 %all-reduce.2.cloned.1.call-start = ((), (), s32[]{:S(2)}) async-start(), calls=%async_computation.2 | async-start | bytes 2097152 | tf_op jit(solution)/shard_map/psum | solution.py:33
  253.2 1.1 copy-start.7
Sparse Core Ops, SparseCore 0:
  254.5 196.0 all-reduce.1
where the time goes:
time: 462 us; the launch traced here: 461 us
  waiting for transfers between devices  227 us (49%)
  other arithmetic  104 us (23%)
  local copies, waits for them, and re-layouts  59.4 us (13%)
  starting transfers between devices  37 us (8%)
  matrix products  19.6 us (4%)
  between operations  13.7 us (3%)
    psum x1, waiting for transfers between devices, from_root(): return lax.psum(block, axis)  196 us
    unnamed x1, other arithmetic  90.8 us
    unnamed x22, local copies, waits for them, and re-layouts  23.9 us
    ppermute x3, starting transfers between devices, extended(): lax.ppermute(tail, axis, [(i, (i + 1) % count) for i in range(ends)])  15.5 us
    all_to_all x1, local copies, waits for them, and re-layouts, on_device(): lax.all_to_all(by_block.astype(jnp.bfloat16), 'field', split_axis=2, conc...  15.4 us
    all_to_all x1, waiting for transfers between devices, on_device(): lax.all_to_all(change, 'field', split_axis=0, concat_axis=2, tiled=True)  13.4 us
    convert_element_type x2, local copies, waits for them, and re-layouts, on_device(): by_block.astype(jnp.bfloat16)  13.4 us
    all_to_all x1, starting transfers between devices, on_device(): lax.all_to_all(by_block.astype(jnp.bfloat16), 'field', split_axis=2, conc...  13.1 us
  transfers between devices with their start and end apart: 9, of which 6 were waited for; matrix products, arithmetic and copies ran while one was open for 0% of the time, Pallas kernels for 0%

commit v1 on v0

v1 whole, which is shorter than its diff:
```python
import jax
import jax.numpy as jnp
from jax import lax
from jax.experimental import pallas as pl
from jax.experimental.pallas import tpu as pltpu
from jax.sharding import PartitionSpec as P

FIELDS = 16
SWEEPS = 3
HALO = SWEEPS
CHUNK = 384
ROW_BLOCK = 8

RELAX_WEIGHTS = (0.8, 1.25, 0.95)


def pad_rows(array):
    return jnp.pad(array, ((0, 0), (1, 1), (0, 0)))


def relax_step(padded, source, coef_pad, weight):
    middle = padded[:, 1:-1]
    coef_mid = coef_pad[:, 1:-1]
    face_north = 0.5 * (coef_mid + coef_pad[:, 2:])
    face_south = 0.5 * (coef_mid + coef_pad[:, :-2])
    face_east = 0.5 * (coef_mid + jnp.roll(coef_mid, -1, 2))
    face_west = 0.5 * (coef_mid + jnp.roll(coef_mid, 1, 2))
    diagonal = 1.0 + face_north + face_south + face_east + face_west
    image = diagonal * middle - face_north * padded[:, 2:] - face_south * padded[:, :-2]
    image = image - face_east * jnp.roll(middle, -1, 2) - face_west * jnp.roll(middle, 1, 2)
    return middle + weight * (source - image) / diagonal


def lookup(zone_ids, diffusivity):
    coefs = jnp.zeros((diffusivity.shape[0],) + zone_ids.shape, jnp.float32)
    for number in range(diffusivity.shape[1]):
        coefs = coefs + jnp.where(
            (zone_ids == number)[None], diffusivity[:, number][:, None, None], jnp.float32(0.0)
        )
    return coefs


def with_halo(block, axis, width):
    count = lax.axis_size(axis)
    head = block[:, :width]
    tail = block[:, -width:]
    from_above = lax.ppermute(tail, axis, [(i, i + 1) for i in range(count - 1)])
    from_below = lax.ppermute(head, axis, [(i + 1, i) for i in range(count - 1)])
    return jnp.concatenate([from_above, block, from_below], axis=1)


def surrogate_kernel(x_ref, w_in_ref, b_in_ref, w_mid_ref, b_mid_ref, w_out_ref, b_out_ref, rate_ref, o_ref):
    w_in = w_in_ref[...]
    w_mid = w_mid_ref[...]
    w_out = w_out_ref[...]
    b_in = b_in_ref[...]
    b_mid = b_mid_ref[...]
    b_out = b_out_ref[...]
    rate = rate_ref[...]
    is_heat = lax.broadcasted_iota(jnp.int32, (FIELDS, CHUNK), 0) == FIELDS - 1

    def row(r, carry):
        x = x_ref[r]
        inputs = x.astype(jnp.bfloat16)
        hidden = jax.nn.silu(jnp.dot(w_in, inputs, preferred_element_type=jnp.float32) + b_in)
        hidden = hidden.astype(jnp.bfloat16)
        hidden = jax.nn.silu(jnp.dot(w_mid, hidden, preferred_element_type=jnp.float32) + b_mid)
        hidden = hidden.astype(jnp.bfloat16)
        change = (jnp.dot(w_out, hidden, preferred_element_type=jnp.float32) + b_out).astype(jnp.bfloat16)
        change = change.astype(jnp.float32)
        heat = x[FIELDS - 1 :] + change[FIELDS - 1 :]
        factor = jnp.exp(rate * jnp.tanh(heat))
        scaled = (change * factor).astype(jnp.bfloat16)
        o_ref[r] = jnp.where(is_heat, change.astype(jnp.bfloat16), scaled)
        return carry

    lax.fori_loop(0, x_ref.shape[0], row, 0)


def surrogate(x, weight_in, bias_in, weight_mid, bias_mid, weight_out, bias_out, rate):
    rows = x.shape[0]
    full = lambda shape: pl.BlockSpec(shape, lambda i: (0,) * len(shape))
    return pl.pallas_call(
        surrogate_kernel,
        grid=(rows // ROW_BLOCK,),
        in_specs=[
            pl.BlockSpec((ROW_BLOCK, FIELDS, CHUNK), lambda i: (i, 0, 0)),
            full(weight_in.shape),
            full(bias_in.shape),
            full(weight_mid.shape),
            full(bias_mid.shape),
            full(weight_out.shape),
            full(bias_out.shape),
            full(rate.shape),
        ],
        out_specs=pl.BlockSpec((ROW_BLOCK, FIELDS, CHUNK), lambda i: (i, 0, 0)),
        out_shape=jax.ShapeDtypeStruct((rows, FIELDS, CHUNK), jnp.bfloat16),
    )(x, weight_in, bias_in, weight_mid, bias_mid, weight_out, bias_out, rate)


def on_device(
    fields,
    zone_ids,
    diffusivity,
    heat_rate,
    weight_in,
    bias_in,
    weight_mid,
    bias_mid,
    weight_out,
    bias_out,
):
    count_here, rows_here, columns = fields.shape
    coefs = lookup(zone_ids, diffusivity)
    stacked = with_halo(jnp.concatenate([fields, coefs], 0), "space", HALO)
    fields_ext = stacked[:count_here]
    coef_pad = pad_rows(stacked[count_here:])
    first_row = lax.axis_index("space") * rows_here - HALO
    global_row = first_row + lax.broadcasted_iota(jnp.int32, (1, rows_here + 2 * HALO, 1), 1)
    inside = (global_row >= 0) & (global_row < rows_here * lax.axis_size("space"))
    state = fields_ext
    for number in range(SWEEPS):
        state = relax_step(pad_rows(state), fields_ext, coef_pad, RELAX_WEIGHTS[number])
        state = jnp.where(inside, state, jnp.float32(0.0))
    state = state[:, HALO : HALO + rows_here]

    chunks = columns // CHUNK
    outgoing = state[0].reshape(rows_here, chunks, CHUNK).transpose(1, 0, 2)
    incoming = lax.all_to_all(outgoing, "field", 0, 0, tiled=True)
    cells = incoming.transpose(1, 0, 2)
    rate = jnp.concatenate([heat_rate, jnp.zeros((FIELDS - heat_rate.shape[0],), jnp.float32)])
    delta = surrogate(
        cells,
        weight_in,
        bias_in[:, None],
        weight_mid,
        bias_mid[:, None],
        weight_out,
        bias_out[:, None],
        rate[:, None],
    )
    returned = lax.all_to_all(delta.transpose(1, 0, 2), "field", 0, 0, tiled=True)
    returned = returned.transpose(1, 0, 2).reshape(1, rows_here, columns)
    return state + returned.astype(jnp.float32)


def solution(mesh):
    return jax.shard_map(
        on_device,
        mesh=mesh,
        in_specs=(
            P("field", "space", None),
            P("space", None),
            P("field", None),
            P(),
            P(),
            P(),
            P(),
            P(),
            P(),
            P(),
        ),
        out_specs=P("field", "space", None),
        check_vma=False,
    )
```

time: 462 us -> 113 us (0.24)
  the two profiles are of different devices: /device:TPU:1 before, /device:TPU:8 now
where the time goes in v1:
time: 113 us; the launch traced here: 112 us
  waiting for transfers between devices  26.3 us (23%)
  Pallas kernels  24.4 us (22%)
  starting transfers between devices  22.4 us (20%)
  blocking collectives  16 us (14%)
  other arithmetic  11.7 us (10%)
  local copies, waits for them, and re-layouts  11.2 us (10%)
    pallas_call x1, Pallas kernels, surrogate(): pl.pallas_call(surrogate_kernel, grid=(rows // ROW_BLOCK,), in_specs=[pl....  24.4 us
    all_to_all x1, waiting for transfers between devices, on_device(): incoming = lax.all_to_all(outgoing, 'field', 0, 0, tiled=True)  22.2 us
    all_to_all x1, blocking collectives, on_device(): lax.all_to_all(delta.transpose(1, 0, 2), 'field', 0, 0, tiled=True)  16 us
    all_to_all x1, starting transfers between devices, on_device(): incoming = lax.all_to_all(outgoing, 'field', 0, 0, tiled=True)  9.67 us
    ppermute x1, starting transfers between devices, with_halo(): lax.ppermute(head, axis, [(i + 1, i) for i in range(count - 1)])  8.47 us
    add x1, other arithmetic, lookup(): coefs + jnp.where((zone_ids == number)[None], diffusivity[:, number][:, N...  6.8 us
    ppermute x1, starting transfers between devices, with_halo(): lax.ppermute(tail, axis, [(i, i + 1) for i in range(count - 1)])  4.28 us
    ppermute x1, waiting for transfers between devices, with_halo(): lax.ppermute(tail, axis, [(i, i + 1) for i in range(count - 1)])  2.86 us
  transfers between devices with their start and end apart: 3, of which 3 were waited for; matrix products, arithmetic and copies ran while one was open for 3% of the time, Pallas kernels for 0%

profile of v1, /device:TPU:8, one launch (start us, length us, event | category | flops | bytes accessed | tf_op | source)
XLA Modules:
  0.0 112.1 jit_solution(3877796283796823525)
XLA Ops:
  0.0 1.6 %fusion.34 = (f32[1,1]{1,0:T(1,128)}, f32[1,1]{1,0:T(1,128)}, f32[1,1]{1,0:T(1,128)}, f32[1,1]{1,0:T(1,128)}, f32[1,1]{1,0:T(1,128)}, /*index=5*/f32[1,1]{1,0:T(1,128)}, f32[1,1]{1,0:T(1,128)}, f32[1,1]{1,0:T(1,128)}) fusion(f32[1,8]{1,0:T(1,128)} %param.12), kind=kLoop, calls=%fused_computation.63 | loop fusion | bytes 64 | tf_op jit(solution)/shard_map/slice | solution.py:38
  1.6 6.8 %add_bitcast_fusion = f32[1,32,6144]{2,1,0:T(8,128)S(1)} fusion(s32[32,6144]{1,0:T(8,128)} %param.11, f32[]{:T(128)} %bitcast.7, f32[]{:T(128)} %bitcast.6, f32[]{:T(128)} %bitcast.5, f32[]{:T(128)} %bitcast.4, f32[]{:T(128)} %bitcast.3, f32[]{:T(128)} %bitcast.2, f32[]{:T(128)} %bitcast.1, f32[]{:T(128)} %bitcast), kind=kLoop, calls=%fused_computation.53 | loop fusion | flops 4521984 | bytes 1572896 | tf_op jit(solution)/shard_map/add | solution.py:37
  8.5 4.3 %collective-permute-start = (f32[2,3,6144]{2,1,0:T(4,128)S(1)}, f32[2,3,6144]{2,1,0:T(4,128)S(1)}, u32[]{:S(2)}, u32[]{:S(2)}) collective-permute-start(f32[2,3,6144]{2,1,0:T(4,128)S(1)} %get-tuple-element.15), channel_id=1, source_target_pairs={{0,16},{16,32},{32,48},{48,64},{64,80},{80,96},{96,112},{112,128},... | collective-permute-start | bytes 442376 | tf_op jit(solution)/shard_map/ppermute | solution.py:47
  12.8 8.5 %collective-permute-start.1 = (f32[2,3,6144]{2,1,0:T(4,128)S(1)}, f32[2,3,6144]{2,1,0:T(4,128)S(1)}, u32[]{:S(2)}, u32[]{:S(2)}) collective-permute-start(f32[2,3,6144]{2,1,0:T(4,128)S(1)} %get-tuple-element.16), channel_id=1, source_target_pairs={{16,0},{32,16},{48,32},{64,48},{80,64},{96,80},{112,96},{128,112},... | collective-permute-start | bytes 442376 | tf_op jit(solution)/shard_map/ppermute | solution.py:48
  21.4 2.9 %collective-permute-done = f32[2,3,6144]{2,1,0:T(4,128)S(1)} collective-permute-done((f32[2,3,6144]{2,1,0:T(4,128)S(1)}, f32[2,3,6144]{2,1,0:T(4,128)S(1)}, u32[]{:S(2)}, u32[]{:S(2)}) %collective-permute-start) | collective-permute-done | bytes 147488 | tf_op jit(solution)/shard_map/ppermute | solution.py:47
  24.2 1.2 %collective-permute-done.1 = f32[2,3,6144]{2,1,0:T(4,128)S(1)} collective-permute-done((f32[2,3,6144]{2,1,0:T(4,128)S(1)}, f32[2,3,6144]{2,1,0:T(4,128)S(1)}, u32[]{:S(2)}, u32[]{:S(2)}) %collective-permute-start.1) | collective-permute-done | bytes 147488 | tf_op jit(solution)/shard_map/ppermute | solution.py:48
  25.6 0.7 fusion.29
  26.4 0.7 add_add_fusion
  27.1 0.8 fusion.24
  28.3 0.8 fusion.23
  29.6 0.7 fusion.22
  30.9 1.1 %copy.26 = f32[16,32,384]{2,1,0:T(8,128)} copy(f32[16,32,384]{2,0,1:T(8,128)S(1)} %bitcast.25) | data formatting | bytes 1572864 | tf_op jit(solution)/shard_map/transpose | solution.py:128
  32.0 9.7 %all-to-all-start = ((f32[16,32,384]{2,1,0:T(8,128)}), f32[16,32,384]{2,1,0:T(8,128)S(1)}, u32[]{:S(2)}, u32[]{:S(2)}) async-start(f32[16,32,384]{2,1,0:T(8,128)} %copy.26), calls=%async_computation | async-start | bytes 1572864 | tf_op jit(solution)/shard_map/all_to_all | solution.py:129
  41.7 0.8 broadcast_in_dim.133.b_in_ref
  42.5 0.8 broadcast_in_dim.134.b_mid_ref
  43.3 0.7 copy.28.w_in_ref
  44.1 0.7 copy.32.rate_ref
  44.8 0.7 copy.31.b_out_ref
  45.5 22.2 %all-to-all-done = f32[16,32,384]{2,1,0:T(8,128)S(1)} async-done(((f32[16,32,384]{2,1,0:T(8,128)}), f32[16,32,384]{2,1,0:T(8,128)S(1)}, u32[]{:S(2)}, u32[]{:S(2)}) %all-to-all-start) | async-done | bytes 786464 | tf_op jit(solution)/shard_map/all_to_all | solution.py:129
  67.7 1.3 %copy.37 = f32[16,32,384]{2,0,1:T(8,128)} copy(f32[16,32,384]{2,1,0:T(8,128)S(1)} %all-to-all-done) | data formatting | bytes 1572864 | tf_op jit(solution)/shard_map/all_to_all | solution.py:129
  69.1 24.4 %shard_map.100 = bf16[32,16,384]{2,1,0:T(8,128)(2,1)} custom-call(f32[32,16,384]{2,1,0:T(8,128)} %bitcast.26, bf16[384,16]{1,0:T(8,128)(2,1)} %copy.28.w_in_ref, f32[384,1]{1,0:T(8,128)} %broadcast_in_dim.133.b_in_ref, bf16[384,384]{1,0:T(8,128)(2,1)} %w_mid_ref.1, f32[384,1]{1,0:T(8,128)} %broadcast_in_dim.134.b_mid_ref, bf16[16,384]{1,0:T(8,128)(2,1)} %w_out_ref.1, ...), custom_call_target="tpu_custom_call" | custom-call | tf_op jit(solution)/shard_map/pallas_call | solution.py:83
  93.5 1.1 copy.33
  94.5 16.0 %all_to_all.10 = bf16[16,32,384]{2,1,0:T(8,128)(2,1)S(1)} all-to-all(bf16[16,32,384]{2,1,0:T(8,128)(2,1)S(1)} %copy.33), channel_id=1, replica_groups=mesh['space'=32,'field'=16] {'field'}, dimensions={0} | all-to-all | bytes 786432 | tf_op jit(solution)/shard_map/all_to_all | solution.py:142
  111.2 1.0 add.123
  (27 shorter events, 2.6 us)
Async XLA Ops:
  0.0 8.4 %copy-start = (f32[1,32,6144]{2,1,0:T(8,128)S(1)}, f32[1,32,6144]{2,1,0:T(8,128)}, u32[]{:S(2)}) copy-start(f32[1,32,6144]{2,1,0:T(8,128)} %param.10) | copy-start | bytes 2359300
  8.5 15.7 %collective-permute-start = (f32[2,3,6144]{2,1,0:T(4,128)S(1)}, f32[2,3,6144]{2,1,0:T(4,128)S(1)}, u32[]{:S(2)}, u32[]{:S(2)}) collective-permute-start(f32[2,3,6144]{2,1,0:T(4,128)S(1)} %get-tuple-element.15), channel_id=1, source_target_pairs={{0,16},{16,32},{32,48},{48,64},{64,80},{80,96},{96,112},{112,128},... | collective-permute-start | bytes 442376 | tf_op jit(solution)/shard_map/ppermute | solution.py:47
  12.8 12.6 %collective-permute-start.1 = (f32[2,3,6144]{2,1,0:T(4,128)S(1)}, f32[2,3,6144]{2,1,0:T(4,128)S(1)}, u32[]{:S(2)}, u32[]{:S(2)}) collective-permute-start(f32[2,3,6144]{2,1,0:T(4,128)S(1)} %get-tuple-element.16), channel_id=1, source_target_pairs={{16,0},{32,16},{48,32},{64,48},{80,64},{96,80},{112,96},{128,112},... | collective-permute-start | bytes 442376 | tf_op jit(solution)/shard_map/ppermute | solution.py:48
  30.9 10.9 %copy-start.2 = (f32[384]{0:T(512)S(1)}, f32[384]{0:T(512)}, u32[]{:S(2)}) copy-start(f32[384]{0:T(512)} %param.15) | copy-start | bytes 4612
  30.9 11.7 %copy-start.3 = (f32[384]{0:T(512)S(1)}, f32[384]{0:T(512)}, u32[]{:S(2)}) copy-start(f32[384]{0:T(512)} %param.17) | copy-start | bytes 4612
  30.9 12.4 %copy-start.1 = (bf16[384,16]{0,1:T(8,128)(2,1)S(1)}, bf16[384,16]{0,1:T(8,128)(2,1)}, u32[]{:S(2)}) copy-start(bf16[384,16]{0,1:T(8,128)(2,1)} %param.14) | copy-start | bytes 36868
  30.9 13.2 %copy-start.5 = (f32[15]{0:T(128)S(1)}, f32[15]{0:T(128)}, u32[]{:S(2)}) copy-start(f32[15]{0:T(128)} %param.13) | copy-start | bytes 184
  30.9 13.9 %copy-start.4 = (f32[16]{0:T(128)S(1)}, f32[16]{0:T(128)}, u32[]{:S(2)}) copy-start(f32[16]{0:T(128)} %param.19) | copy-start | bytes 196
  32.0 35.7 %all-to-all-start = ((f32[16,32,384]{2,1,0:T(8,128)}), f32[16,32,384]{2,1,0:T(8,128)S(1)}, u32[]{:S(2)}, u32[]{:S(2)}) async-start(f32[16,32,384]{2,1,0:T(8,128)} %copy.26), calls=%async_computation | async-start | bytes 1572864 | tf_op jit(solution)/shard_map/all_to_all | solution.py:129

commit v2 on v1

--- a/solution.py
+++ b/solution.py
@@ -31,13 +31,27 @@
     return middle + weight * (source - image) / diagonal
 
 
+def lookup_kernel(table_ref, zone_ref, o_ref):
+    zone = zone_ref[...]
+    level = [table_ref[0, number] for number in range(table_ref.shape[1])]
+    bit = 1
+    while len(level) > 1:
+        pick = (zone & bit) != 0
+        level = [jnp.where(pick, level[k + 1], level[k]) for k in range(0, len(level), 2)]
+        bit *= 2
+    o_ref[0] = level[0]
+
+
 def lookup(zone_ids, diffusivity):
-    coefs = jnp.zeros((diffusivity.shape[0],) + zone_ids.shape, jnp.float32)
-    for number in range(diffusivity.shape[1]):
-        coefs = coefs + jnp.where(
-            (zone_ids == number)[None], diffusivity[:, number][:, None, None], jnp.float32(0.0)
-        )
-    return coefs
+    return pl.pallas_call(
+        lookup_kernel,
+        in_specs=[
+            pl.BlockSpec(memory_space=pltpu.SMEM),
+            pl.BlockSpec(memory_space=pltpu.VMEM),
+        ],
+        out_specs=pl.BlockSpec(memory_space=pltpu.VMEM),
+        out_shape=jax.ShapeDtypeStruct((1,) + zone_ids.shape, jnp.float32),
+    )(diffusivity, zone_ids)
 
 
 def with_halo(block, axis, width):
@@ -47,6 +61,11 @@
     from_above = lax.ppermute(tail, axis, [(i, i + 1) for i in range(count - 1)])
     from_below = lax.ppermute(head, axis, [(i + 1, i) for i in range(count - 1)])
     return jnp.concatenate([from_above, block, from_below], axis=1)
+
+
+def silu(x):
+    half = 0.5 * x
+    return half + half * jnp.tanh(half)
 
 
 def surrogate_kernel(x_ref, w_in_ref, b_in_ref, w_mid_ref, b_mid_ref, w_out_ref, b_out_ref, rate_ref, o_ref):
@@ -62,9 +81,9 @@
     def row(r, carry):
         x = x_ref[r]
         inputs = x.astype(jnp.bfloat16)
-        hidden = jax.nn.silu(jnp.dot(w_in, inputs, preferred_element_type=jnp.float32) + b_in)
+        hidden = silu(jnp.dot(w_in, inputs, preferred_element_type=jnp.float32) + b_in)
         hidden = hidden.astype(jnp.bfloat16)
-        hidden = jax.nn.silu(jnp.dot(w_mid, hidden, preferred_element_type=jnp.float32) + b_mid)
+        hidden = silu(jnp.dot(w_mid, hidden, preferred_element_type=jnp.float32) + b_mid)
         hidden = hidden.astype(jnp.bfloat16)
         change = (jnp.dot(w_out, hidden, preferred_element_type=jnp.float32) + b_out).astype(jnp.bfloat16)
         change = change.astype(jnp.float32)

time: 113 us -> 108 us (0.956)
  other arithmetic: 11.7 us -> 5.99 us
  Pallas kernels: 24.4 us -> 27.6 us
  local copies, waits for them, and re-layouts: 11.2 us -> 9.58 us
    add x1 -> x0, other arithmetic: 6.8 us -> none  [lookup(): coefs + jnp.where((zone_ids == number)[None], diffusivity[:, number][:, N...]
    pallas_call x0 -> x1, Pallas kernels: none -> 2.43 us  [lookup(): pl.pallas_call(lookup_kernel, in_specs=[pl.BlockSpec(memory_space=pltpu.S...]
    slice x1 -> x0, local copies, waits for them, and re-layouts: 1.62 us -> none  [lookup(): diffusivity[:, number][:, None, None]]
  transfers between devices with their start and end apart: 3 -> 3, of which waited for: 3 -> 3; matrix products, arithmetic and copies ran while one was open for 3% -> 4% of each run, Pallas kernels for 0% -> 0%
where the time goes in v2:
time: 108 us
  Pallas kernels  27.6 us (26%)
  waiting for transfers between devices  26.3 us (24%)
  starting transfers between devices  22.4 us (21%)
  blocking collectives  16 us (15%)
  local copies, waits for them, and re-layouts  9.58 us (9%)
  other arithmetic  5.99 us (6%)
    pallas_call x1, Pallas kernels, surrogate(): pl.pallas_call(surrogate_kernel, grid=(rows // ROW_BLOCK,), in_specs=[pl....  25.2 us
    all_to_all x1, waiting for transfers between devices, on_device(): incoming = lax.all_to_all(outgoing, 'field', 0, 0, tiled=True)  22.2 us
    all_to_all x1, blocking collectives, on_device(): lax.all_to_all(delta.transpose(1, 0, 2), 'field', 0, 0, tiled=True)  16 us
    all_to_all x1, starting transfers between devices, on_device(): incoming = lax.all_to_all(outgoing, 'field', 0, 0, tiled=True)  9.67 us
    ppermute x1, starting transfers between devices, with_halo(): lax.ppermute(head, axis, [(i + 1, i) for i in range(count - 1)])  8.47 us
    ppermute x1, starting transfers between devices, with_halo(): lax.ppermute(tail, axis, [(i, i + 1) for i in range(count - 1)])  4.28 us
    ppermute x1, waiting for transfers between devices, with_halo(): lax.ppermute(tail, axis, [(i, i + 1) for i in range(count - 1)])  2.86 us
    pallas_call x1, Pallas kernels, lookup(): pl.pallas_call(lookup_kernel, in_specs=[pl.BlockSpec(memory_space=pltpu.S...  2.43 us
  transfers between devices with their start and end apart: 3, of which 3 were waited for; matrix products, arithmetic and copies ran while one was open for 4% of the time, Pallas kernels for 0%

profile of v2, /device:TPU:8, one launch (start us, length us, event | category | flops | bytes accessed | tf_op | source)
XLA Modules:
  0.0 108.0 jit_solution(8794562119486020372)
XLA Ops:
  0.0 2.4 %shard_map.100 = f32[1,32,6144]{2,1,0:T(8,128)} custom-call(f32[1,8]{1,0:T(1,128)} %table_ref.1, s32[32,6144]{1,0:T(8,128)} %zone_ref.1), custom_call_target="tpu_custom_call" | custom-call | tf_op jit(solution)/shard_map/pallas_call | solution.py:46
  2.4 1.2 %pad_maximum_fusion.14 = (f32[2,3,6144]{2,1,0:T(4,128)S(1)}, f32[2,3,6144]{2,1,0:T(4,128)S(1)}) fusion(f32[1,32,6144]{2,1,0:T(8,128)} %shard_map.100, f32[1,32,6144]{2,1,0:T(8,128)S(1)} %copy-done.1), kind=kLoop, calls=%fused_computation.55 | loop fusion | flops 73728 | bytes 1867776 | tf_op jit(solution)/shard_map/slice | solution.py:60
  3.6 4.3 %collective-permute-start = (f32[2,3,6144]{2,1,0:T(4,128)S(1)}, f32[2,3,6144]{2,1,0:T(4,128)S(1)}, u32[]{:S(2)}, u32[]{:S(2)}) collective-permute-start(f32[2,3,6144]{2,1,0:T(4,128)S(1)} %get-tuple-element.15), channel_id=1, source_target_pairs={{0,16},{16,32},{32,48},{48,64},{64,80},{80,96},{96,112},{112,128},... | collective-permute-start | bytes 442376 | tf_op jit(solution)/shard_map/ppermute | solution.py:61
  7.9 8.5 %collective-permute-start.1 = (f32[2,3,6144]{2,1,0:T(4,128)S(1)}, f32[2,3,6144]{2,1,0:T(4,128)S(1)}, u32[]{:S(2)}, u32[]{:S(2)}) collective-permute-start(f32[2,3,6144]{2,1,0:T(4,128)S(1)} %get-tuple-element.16), channel_id=1, source_target_pairs={{16,0},{32,16},{48,32},{64,48},{80,64},{96,80},{112,96},{128,112},... | collective-permute-start | bytes 442376 | tf_op jit(solution)/shard_map/ppermute | solution.py:62
  16.5 2.9 %collective-permute-done = f32[2,3,6144]{2,1,0:T(4,128)S(1)} collective-permute-done((f32[2,3,6144]{2,1,0:T(4,128)S(1)}, f32[2,3,6144]{2,1,0:T(4,128)S(1)}, u32[]{:S(2)}, u32[]{:S(2)}) %collective-permute-start) | collective-permute-done | bytes 147488 | tf_op jit(solution)/shard_map/ppermute | solution.py:61
  19.3 1.2 %collective-permute-done.1 = f32[2,3,6144]{2,1,0:T(4,128)S(1)} collective-permute-done((f32[2,3,6144]{2,1,0:T(4,128)S(1)}, f32[2,3,6144]{2,1,0:T(4,128)S(1)}, u32[]{:S(2)}, u32[]{:S(2)}) %collective-permute-start.1) | collective-permute-done | bytes 147488 | tf_op jit(solution)/shard_map/ppermute | solution.py:62
  20.7 0.7 fusion.29
  21.5 0.7 add_add_fusion
  22.2 0.8 fusion.24
  23.4 0.8 fusion.23
  24.7 0.7 fusion.22
  26.0 1.1 %copy.32 = f32[32,16,384]{2,0,1:T(8,128)} copy(f32[32,16,384]{2,1,0:T(8,128)S(1)} %bitcast.16) | data formatting | bytes 1572864 | tf_op jit(solution)/shard_map/reshape;squeeze | solution.py:147
  27.1 9.7 %all-to-all-start = ((f32[16,32,384]{2,1,0:T(8,128)}), f32[16,32,384]{2,1,0:T(8,128)S(1)}, u32[]{:S(2)}, u32[]{:S(2)}) async-start(f32[16,32,384]{2,1,0:T(8,128)} %bitcast.14), calls=%async_computation | async-start | bytes 1572864 | tf_op jit(solution)/shard_map/all_to_all | solution.py:148
  36.8 0.8 broadcast_in_dim.38.b_in_ref
  37.6 0.8 broadcast_in_dim.39.b_mid_ref
  38.4 0.7 copy.21.w_in_ref
  39.2 0.7 copy.25.rate_ref
  39.9 0.7 copy.24.b_out_ref
  40.6 22.2 %all-to-all-done = f32[16,32,384]{2,1,0:T(8,128)S(1)} async-done(((f32[16,32,384]{2,1,0:T(8,128)}), f32[16,32,384]{2,1,0:T(8,128)S(1)}, u32[]{:S(2)}, u32[]{:S(2)}) %all-to-all-start) | async-done | bytes 786464 | tf_op jit(solution)/shard_map/all_to_all | solution.py:148
  62.8 1.3 %copy.31 = f32[16,32,384]{2,0,1:T(8,128)} copy(f32[16,32,384]{2,1,0:T(8,128)S(1)} %all-to-all-done) | data formatting | bytes 1572864 | tf_op jit(solution)/shard_map/all_to_all | solution.py:148
  64.2 25.2 %shard_map.101 = bf16[32,16,384]{2,1,0:T(8,128)(2,1)} custom-call(f32[32,16,384]{2,1,0:T(8,128)} %bitcast.17, bf16[384,16]{1,0:T(8,128)(2,1)} %copy.21.w_in_ref, f32[384,1]{1,0:T(8,128)} %broadcast_in_dim.38.b_in_ref, bf16[384,384]{1,0:T(8,128)(2,1)} %w_mid_ref.1, f32[384,1]{1,0:T(8,128)} %broadcast_in_dim.39.b_mid_ref, bf16[16,384]{1,0:T(8,128)(2,1)} %w_out_ref.1, ...), custom_call_target="tpu_custom_call" | custom-call | tf_op jit(solution)/shard_map/pallas_call | solution.py:102
  89.3 1.1 copy.26
  90.4 16.0 %all_to_all.10 = bf16[16,32,384]{2,1,0:T(8,128)(2,1)S(1)} all-to-all(bf16[16,32,384]{2,1,0:T(8,128)(2,1)S(1)} %copy.26), channel_id=1, replica_groups=mesh['space'=32,'field'=16] {'field'}, dimensions={0} | all-to-all | bytes 786432 | tf_op jit(solution)/shard_map/all_to_all | solution.py:161
  107.1 1.0 add.85
  (28 shorter events, 2.5 us)
Async XLA Ops:
  0.0 2.4 %copy-start.1 = (f32[1,32,6144]{2,1,0:T(8,128)S(1)}, f32[1,32,6144]{2,1,0:T(8,128)}, u32[]{:S(2)}) copy-start(f32[1,32,6144]{2,1,0:T(8,128)} %param.10) | copy-start | bytes 2359300
  2.4 18.1 %copy-start = (f32[1,32,6144]{2,1,0:T(8,128)S(1)}, f32[1,32,6144]{2,1,0:T(8,128)}, u32[]{:S(2)}) copy-start(f32[1,32,6144]{2,1,0:T(8,128)} %shard_map.100) | copy-start | bytes 2359300
  3.6 15.7 %collective-permute-start = (f32[2,3,6144]{2,1,0:T(4,128)S(1)}, f32[2,3,6144]{2,1,0:T(4,128)S(1)}, u32[]{:S(2)}, u32[]{:S(2)}) collective-permute-start(f32[2,3,6144]{2,1,0:T(4,128)S(1)} %get-tuple-element.15), channel_id=1, source_target_pairs={{0,16},{16,32},{32,48},{48,64},{64,80},{80,96},{96,112},{112,128},... | collective-permute-start | bytes 442376 | tf_op jit(solution)/shard_map/ppermute | solution.py:61
  7.9 12.6 %collective-permute-start.1 = (f32[2,3,6144]{2,1,0:T(4,128)S(1)}, f32[2,3,6144]{2,1,0:T(4,128)S(1)}, u32[]{:S(2)}, u32[]{:S(2)}) collective-permute-start(f32[2,3,6144]{2,1,0:T(4,128)S(1)} %get-tuple-element.16), channel_id=1, source_target_pairs={{16,0},{32,16},{48,32},{64,48},{80,64},{96,80},{112,96},{128,112},... | collective-permute-start | bytes 442376 | tf_op jit(solution)/shard_map/ppermute | solution.py:62
  26.0 10.9 %copy-start.3 = (f32[384]{0:T(512)S(1)}, f32[384]{0:T(512)}, u32[]{:S(2)}) copy-start(f32[384]{0:T(512)} %param.15) | copy-start | bytes 4612
  26.0 11.7 %copy-start.4 = (f32[384]{0:T(512)S(1)}, f32[384]{0:T(512)}, u32[]{:S(2)}) copy-start(f32[384]{0:T(512)} %param.17) | copy-start | bytes 4612
  26.0 12.4 %copy-start.2 = (bf16[384,16]{0,1:T(8,128)(2,1)S(1)}, bf16[384,16]{0,1:T(8,128)(2,1)}, u32[]{:S(2)}) copy-start(bf16[384,16]{0,1:T(8,128)(2,1)} %param.14) | copy-start | bytes 36868
  26.0 13.2 %copy-start.6 = (f32[15]{0:T(128)S(1)}, f32[15]{0:T(128)}, u32[]{:S(2)}) copy-start(f32[15]{0:T(128)} %param.13) | copy-start | bytes 184
  26.0 13.9 %copy-start.5 = (f32[16]{0:T(128)S(1)}, f32[16]{0:T(128)}, u32[]{:S(2)}) copy-start(f32[16]{0:T(128)} %param.19) | copy-start | bytes 196
  27.1 35.7 %all-to-all-start = ((f32[16,32,384]{2,1,0:T(8,128)}), f32[16,32,384]{2,1,0:T(8,128)S(1)}, u32[]{:S(2)}, u32[]{:S(2)}) async-start(f32[16,32,384]{2,1,0:T(8,128)} %bitcast.14), calls=%async_computation | async-start | bytes 1572864 | tf_op jit(solution)/shard_map/all_to_all | solution.py:148

commit v3 on v2

--- a/solution.py
+++ b/solution.py
@@ -9,7 +9,6 @@
 SWEEPS = 3
 HALO = SWEEPS
 CHUNK = 384
-ROW_BLOCK = 8
 
 RELAX_WEIGHTS = (0.8, 1.25, 0.95)
 
@@ -63,58 +62,21 @@
     return jnp.concatenate([from_above, block, from_below], axis=1)
 
 
-def silu(x):
-    half = 0.5 * x
-    return half + half * jnp.tanh(half)
-
-
-def surrogate_kernel(x_ref, w_in_ref, b_in_ref, w_mid_ref, b_mid_ref, w_out_ref, b_out_ref, rate_ref, o_ref):
-    w_in = w_in_ref[...]
-    w_mid = w_mid_ref[...]
-    w_out = w_out_ref[...]
-    b_in = b_in_ref[...]
-    b_mid = b_mid_ref[...]
-    b_out = b_out_ref[...]
-    rate = rate_ref[...]
-    is_heat = lax.broadcasted_iota(jnp.int32, (FIELDS, CHUNK), 0) == FIELDS - 1
-
-    def row(r, carry):
-        x = x_ref[r]
-        inputs = x.astype(jnp.bfloat16)
-        hidden = silu(jnp.dot(w_in, inputs, preferred_element_type=jnp.float32) + b_in)
-        hidden = hidden.astype(jnp.bfloat16)
-        hidden = silu(jnp.dot(w_mid, hidden, preferred_element_type=jnp.float32) + b_mid)
-        hidden = hidden.astype(jnp.bfloat16)
-        change = (jnp.dot(w_out, hidden, preferred_element_type=jnp.float32) + b_out).astype(jnp.bfloat16)
-        change = change.astype(jnp.float32)
-        heat = x[FIELDS - 1 :] + change[FIELDS - 1 :]
-        factor = jnp.exp(rate * jnp.tanh(heat))
-        scaled = (change * factor).astype(jnp.bfloat16)
-        o_ref[r] = jnp.where(is_heat, change.astype(jnp.bfloat16), scaled)
-        return carry
-
-    lax.fori_loop(0, x_ref.shape[0], row, 0)
-
-
-def surrogate(x, weight_in, bias_in, weight_mid, bias_mid, weight_out, bias_out, rate):
-    rows = x.shape[0]
-    full = lambda shape: pl.BlockSpec(shape, lambda i: (0,) * len(shape))
-    return pl.pallas_call(
-        surrogate_kernel,
-        grid=(rows // ROW_BLOCK,),
-        in_specs=[
-            pl.BlockSpec((ROW_BLOCK, FIELDS, CHUNK), lambda i: (i, 0, 0)),
-            full(weight_in.shape),
-            full(bias_in.shape),
-            full(weight_mid.shape),
-            full(bias_mid.shape),
-            full(weight_out.shape),
-            full(bias_out.shape),
-            full(rate.shape),
-        ],
-        out_specs=pl.BlockSpec((ROW_BLOCK, FIELDS, CHUNK), lambda i: (i, 0, 0)),
-        out_shape=jax.ShapeDtypeStruct((rows, FIELDS, CHUNK), jnp.bfloat16),
-    )(x, weight_in, bias_in, weight_mid, bias_mid, weight_out, bias_out, rate)
+def surrogate(cells, weight_in, bias_in, weight_mid, bias_mid, weight_out, bias_out, rate):
+    inputs = cells.astype(jnp.bfloat16)
+    hidden = jax.nn.silu(
+        jnp.dot(weight_in, inputs, preferred_element_type=jnp.float32) + bias_in[:, None]
+    ).astype(jnp.bfloat16)
+    hidden = jax.nn.silu(
+        jnp.dot(weight_mid, hidden, preferred_element_type=jnp.float32) + bias_mid[:, None]
+    ).astype(jnp.bfloat16)
+    change = (jnp.dot(weight_out, hidden, preferred_element_type=jnp.float32) + bias_out[:, None]).astype(
+        jnp.bfloat16
+    )
+    heat = cells[-1] + change[-1].astype(jnp.float32)
+    factor = jnp.exp(rate[:, None] * jnp.tanh(heat)[None])
+    scaled = (change[:-1].astype(jnp.float32) * factor).astype(jnp.bfloat16)
+    return jnp.concatenate([scaled, change[-1:]], 0)
 
 
 def on_device(
@@ -146,19 +108,17 @@
     chunks = columns // CHUNK
     outgoing = state[0].reshape(rows_here, chunks, CHUNK).transpose(1, 0, 2)
     incoming = lax.all_to_all(outgoing, "field", 0, 0, tiled=True)
-    cells = incoming.transpose(1, 0, 2)
-    rate = jnp.concatenate([heat_rate, jnp.zeros((FIELDS - heat_rate.shape[0],), jnp.float32)])
     delta = surrogate(
-        cells,
+        incoming.reshape(FIELDS, rows_here * CHUNK),
         weight_in,
-        bias_in[:, None],
+        bias_in,
         weight_mid,
-        bias_mid[:, None],
+        bias_mid,
         weight_out,
-        bias_out[:, None],
-        rate[:, None],
+        bias_out,
+        heat_rate,
     )
-    returned = lax.all_to_all(delta.transpose(1, 0, 2), "field", 0, 0, tiled=True)
+    returned = lax.all_to_all(delta.reshape(FIELDS, rows_here, CHUNK), "field", 0, 0, tiled=True)
     returned = returned.transpose(1, 0, 2).reshape(1, rows_here, columns)
     return state + returned.astype(jnp.float32)
 

time: 108 us -> 102 us (0.944)
  blocking collectives: 16 us -> 51.4 us
  Pallas kernels: 27.6 us -> 2.44 us
  waiting for transfers between devices: 26.3 us -> 4.04 us
  matrix products: 0 us -> 20 us
  starting transfers between devices: 22.4 us -> 12.8 us
  local copies, waits for them, and re-layouts: 9.58 us -> 2.94 us
  other arithmetic: 5.99 us -> 8.03 us
    all_to_all x1 -> x2, blocking collectives: 16 us -> 51.4 us  [the longest x1 35.5 us: on_device(): incoming = lax.all_to_all(outgoing, 'field', 0, 0, tiled=True)]
    pallas_call x1 -> x0, Pallas kernels: 25.2 us -> none  [surrogate(): pl.pallas_call(surrogate_kernel, grid=(rows // ROW_BLOCK,), in_specs=[pl....]
    all_to_all x1 -> x0, waiting for transfers between devices: 22.2 us -> none  [on_device(): incoming = lax.all_to_all(outgoing, 'field', 0, 0, tiled=True)]
    dot_general x0 -> x2, matrix products: none -> 20 us  [the longest x1 12.5 us: surrogate(): jnp.dot(weight_out, hidden, preferred_element_type=jnp.float32)]
    all_to_all x1 -> x0, starting transfers between devices: 9.67 us -> none  [on_device(): incoming = lax.all_to_all(outgoing, 'field', 0, 0, tiled=True)]
    broadcast_in_dim x4 -> x0, local copies, waits for them, and re-layouts: 2.95 us -> none  [the longest x1 0.8 us: on_device(): bias_mid[:, None]]
    concatenate x1, other arithmetic: 0.21 us -> 1.6 us  [with_halo(): return jnp.concatenate([from_above, block, from_below], axis=1)]
    all_to_all x1 -> x0, local copies, waits for them, and re-layouts: 1.34 us -> none  [on_device(): incoming = lax.all_to_all(outgoing, 'field', 0, 0, tiled=True)]
  transfers between devices with their start and end apart: 3 -> 2, of which waited for: 3 -> 2; matrix products, arithmetic and copies ran while one was open for 4% -> 0% of each run, Pallas kernels for 0% -> 0%
where the time goes in v3:
time: 102 us
  blocking collectives  51.4 us (50%)
  matrix products  20 us (20%)
  starting transfers between devices  12.8 us (13%)
  other arithmetic  8.03 us (8%)
  waiting for transfers between devices  4.04 us (4%)
  local copies, waits for them, and re-layouts  2.94 us (3%)
  Pallas kernels  2.44 us (2%)
    all_to_all x1, blocking collectives, on_device(): incoming = lax.all_to_all(outgoing, 'field', 0, 0, tiled=True)  35.5 us
    all_to_all x1, blocking collectives, on_device(): lax.all_to_all(delta.reshape(FIELDS, rows_here, CHUNK), 'field', 0, 0, ti...  16 us
    dot_general x1, matrix products, surrogate(): jnp.dot(weight_out, hidden, preferred_element_type=jnp.float32)  12.5 us
    ppermute x1, starting transfers between devices, with_halo(): lax.ppermute(head, axis, [(i + 1, i) for i in range(count - 1)])  8.47 us
    dot_general x1, matrix products, surrogate(): jnp.dot(weight_in, inputs, preferred_element_type=jnp.float32)  7.52 us
    ppermute x1, starting transfers between devices, with_halo(): lax.ppermute(tail, axis, [(i, i + 1) for i in range(count - 1)])  4.28 us
    ppermute x1, waiting for transfers between devices, with_halo(): lax.ppermute(tail, axis, [(i, i + 1) for i in range(count - 1)])  2.86 us
    pallas_call x1, Pallas kernels, lookup(): pl.pallas_call(lookup_kernel, in_specs=[pl.BlockSpec(memory_space=pltpu.S...  2.44 us
  transfers between devices with their start and end apart: 2, of which 2 were waited for; matrix products, arithmetic and copies ran while one was open for 0% of the time, Pallas kernels for 0%

profile of v3, /device:TPU:8, one launch (start us, length us, event | category | flops | bytes accessed | tf_op | source)
XLA Modules:
  0.0 102.0 jit_solution(10847556525568298394)
XLA Ops:
  0.0 2.4 %shard_map.100 = f32[1,32,6144]{2,1,0:T(8,128)} custom-call(f32[1,8]{1,0:T(1,128)} %table_ref.1, s32[32,6144]{1,0:T(8,128)} %zone_ref.1), custom_call_target="tpu_custom_call" | custom-call | tf_op jit(solution)/shard_map/pallas_call | solution.py:45
  2.4 1.4 %pad_maximum_fusion.15 = (f32[2,3,6144]{2,1,0:T(4,128)S(1)}, f32[2,3,6144]{2,1,0:T(4,128)S(1)}) fusion(f32[1,32,6144]{2,1,0:T(8,128)} %shard_map.100, f32[1,32,6144]{2,1,0:T(8,128)} %param.10), kind=kLoop, calls=%fused_computation.71 | loop fusion | flops 73728 | bytes 1867776 | tf_op jit(solution)/shard_map/slice | solution.py:59
  3.8 4.3 %collective-permute-start = (f32[2,3,6144]{2,1,0:T(4,128)S(1)}, f32[2,3,6144]{2,1,0:T(4,128)S(1)}, u32[]{:S(2)}, u32[]{:S(2)}) collective-permute-start(f32[2,3,6144]{2,1,0:T(4,128)S(1)} %get-tuple-element.15), channel_id=1, source_target_pairs={{0,16},{16,32},{32,48},{48,64},{64,80},{80,96},{96,112},{112,128},... | collective-permute-start | bytes 442376 | tf_op jit(solution)/shard_map/ppermute | solution.py:60
  8.1 8.5 %collective-permute-start.1 = (f32[2,3,6144]{2,1,0:T(4,128)S(1)}, f32[2,3,6144]{2,1,0:T(4,128)S(1)}, u32[]{:S(2)}, u32[]{:S(2)}) collective-permute-start(f32[2,3,6144]{2,1,0:T(4,128)S(1)} %get-tuple-element.16), channel_id=1, source_target_pairs={{16,0},{32,16},{48,32},{64,48},{80,64},{96,80},{112,96},{128,112},... | collective-permute-start | bytes 442376 | tf_op jit(solution)/shard_map/ppermute | solution.py:61
  16.7 2.9 %collective-permute-done = f32[2,3,6144]{2,1,0:T(4,128)S(1)} collective-permute-done((f32[2,3,6144]{2,1,0:T(4,128)S(1)}, f32[2,3,6144]{2,1,0:T(4,128)S(1)}, u32[]{:S(2)}, u32[]{:S(2)}) %collective-permute-start) | collective-permute-done | bytes 147488 | tf_op jit(solution)/shard_map/ppermute | solution.py:60
  19.5 1.2 %collective-permute-done.1 = f32[2,3,6144]{2,1,0:T(4,128)S(1)} collective-permute-done((f32[2,3,6144]{2,1,0:T(4,128)S(1)}, f32[2,3,6144]{2,1,0:T(4,128)S(1)}, u32[]{:S(2)}, u32[]{:S(2)}) %collective-permute-start.1) | collective-permute-done | bytes 147488 | tf_op jit(solution)/shard_map/ppermute | solution.py:61
  20.7 1.6 %pad_maximum_fusion = f32[2,38,6144]{2,1,0:T(8,128)S(1)} fusion(f32[2,3,6144]{2,1,0:T(4,128)S(1)} %collective-permute-done.1, f32[1,32,6144]{2,1,0:T(8,128)} %shard_map.100, f32[1,32,6144]{2,1,0:T(8,128)} %param.10, f32[2,3,6144]{2,1,0:T(4,128)S(1)} %collective-permute-done), kind=kLoop, calls=%fused_computation.15 | loop fusion | flops 1400832 | bytes 3735552 | tf_op jit(solution)/shard_map/concatenate | solution.py:62
  22.3 0.7 fusion.40
  23.1 0.7 add_add_fusion
  23.8 0.9 fusion.34
  24.6 0.3 fusion.43
  25.0 0.9 fusion.33
  25.9 0.3 fusion.41
  26.3 0.8 fusion.32
  27.1 0.4 fusion.35
  27.5 0.1 copy.16
  27.7 0.3 copy.21
  27.9 35.5 %all_to_all.10 = f32[16,32,384]{2,1,0:T(8,128)S(1)} all-to-all(f32[16,32,384]{2,1,0:T(8,128)S(1)} %bitcast.52), channel_id=1, replica_groups=mesh['space'=32,'field'=16] {'field'}, dimensions={0} | all-to-all | bytes 1572864 | tf_op jit(solution)/shard_map/all_to_all | solution.py:110
  63.7 7.5 %fusion.6 = bf16[384,12288]{0,1:T(8,128)(2,1)} fusion(bf16[16,12288]{1,0:T(8,128)(2,1)S(1)} %bitcast.57, bf16[384,16]{0,1:T(8,128)(2,1)S(1)} %copy-done.4, f32[384]{0:T(512)S(1)} %copy-done.6), kind=kOutput, calls=%fused_computation.10 | convolution fusion | flops 179306496 | bytes 9844224 | tf_op jit(solution)/shard_map/dot_general | solution.py:68
  71.3 12.5 %fusion.9 = bf16[16,12288]{1,0:T(8,128)(2,1)S(1)} fusion(bf16[16,384]{1,0:T(8,128)(2,1)S(1)} %copy-done.5, bf16[384,12288]{0,1:T(8,128)(2,1)} %fusion.6, bf16[384,384]{1,0:T(8,128)(2,1)S(1)} %copy-done, f32[384]{0:T(512)S(1)} %copy-done.7, f32[16]{0:T(128)S(1)} %copy-done.8), kind=kOutput, calls=%fused_computation.14 | convolution fusion | flops 3803578368 | bytes 10139200 | tf_op jit(solution)/shard_map/dot_general | solution.py:73
  84.0 0.2 multiply_convert_fusion
  84.3 16.0 %all_to_all.11 = bf16[16,32,384]{2,1,0:T(8,128)(2,1)S(1)} all-to-all(bf16[16,32,384]{2,1,0:T(8,128)(2,1)S(1)} %bitcast.55), channel_id=1, replica_groups=mesh['space'=32,'field'=16] {'field'}, dimensions={0} | all-to-all | bytes 786432 | tf_op jit(solution)/shard_map/all_to_all | solution.py:121
  100.4 0.5 copy.15
  101.0 1.0 add.138
  (33 shorter events, 1.1 us)
Async XLA Ops:
  0.0 71.2 %copy-start = (bf16[384,384]{1,0:T(8,128)(2,1)S(1)}, bf16[384,384]{1,0:T(8,128)(2,1)}, u32[]{:S(2)}) copy-start(bf16[384,384]{1,0:T(8,128)(2,1)} %param.16) | copy-start | bytes 884740
  0.0 23.1 %copy-start.2 = (f32[1,32,6144]{2,1,0:T(8,128)S(1)}, f32[1,32,6144]{2,1,0:T(8,128)}, u32[]{:S(2)}) copy-start(f32[1,32,6144]{2,1,0:T(8,128)} %param.10) | copy-start | bytes 2359300
  2.4 20.6 %copy-start.1 = (f32[1,32,6144]{2,1,0:T(8,128)S(1)}, f32[1,32,6144]{2,1,0:T(8,128)}, u32[]{:S(2)}) copy-start(f32[1,32,6144]{2,1,0:T(8,128)} %shard_map.100) | copy-start | bytes 2359300
  3.8 15.7 %collective-permute-start = (f32[2,3,6144]{2,1,0:T(4,128)S(1)}, f32[2,3,6144]{2,1,0:T(4,128)S(1)}, u32[]{:S(2)}, u32[]{:S(2)}) collective-permute-start(f32[2,3,6144]{2,1,0:T(4,128)S(1)} %get-tuple-element.15), channel_id=1, source_target_pairs={{0,16},{16,32},{32,48},{48,64},{64,80},{80,96},{96,112},{112,128},... | collective-permute-start | bytes 442376 | tf_op jit(solution)/shard_map/ppermute | solution.py:60
  8.1 12.6 %collective-permute-start.1 = (f32[2,3,6144]{2,1,0:T(4,128)S(1)}, f32[2,3,6144]{2,1,0:T(4,128)S(1)}, u32[]{:S(2)}, u32[]{:S(2)}) collective-permute-start(f32[2,3,6144]{2,1,0:T(4,128)S(1)} %get-tuple-element.16), channel_id=1, source_target_pairs={{16,0},{32,16},{48,32},{64,48},{80,64},{96,80},{112,96},{128,112},... | collective-permute-start | bytes 442376 | tf_op jit(solution)/shard_map/ppermute | solution.py:61
  26.3 37.4 %copy-start.4 = (bf16[384,16]{0,1:T(8,128)(2,1)S(1)}, bf16[384,16]{0,1:T(8,128)(2,1)}, u32[]{:S(2)}) copy-start(bf16[384,16]{0,1:T(8,128)(2,1)} %param.14) | copy-start | bytes 36868
  26.3 37.4 %copy-start.6 = (f32[384]{0:T(512)S(1)}, f32[384]{0:T(512)}, u32[]{:S(2)}) copy-start(f32[384]{0:T(512)} %param.15) | copy-start | bytes 4612
  63.7 7.6 %copy-start.5 = (bf16[16,384]{1,0:T(8,128)(2,1)S(1)}, bf16[16,384]{1,0:T(8,128)(2,1)}, u32[]{:S(2)}) copy-start(bf16[16,384]{1,0:T(8,128)(2,1)} %param.18) | copy-start | bytes 36868
  63.7 7.5 %copy-start.7 = (f32[384]{0:T(512)S(1)}, f32[384]{0:T(512)}, u32[]{:S(2)}) copy-start(f32[384]{0:T(512)} %param.17) | copy-start | bytes 4612
  63.7 7.5 %copy-start.8 = (f32[16]{0:T(128)S(1)}, f32[16]{0:T(128)}, u32[]{:S(2)}) copy-start(f32[16]{0:T(128)} %param.19) | copy-start | bytes 196
  71.3 12.7 %copy-start.3 = (f32[15]{0:T(128)S(1)}, f32[15]{0:T(128)}, u32[]{:S(2)}) copy-start(f32[15]{0:T(128)} %param.13) | copy-start | bytes 184

commit v4 on v3

--- a/solution.py
+++ b/solution.py
@@ -53,13 +53,24 @@
     )(diffusivity, zone_ids)
 
 
-def with_halo(block, axis, width):
-    count = lax.axis_size(axis)
-    head = block[:, :width]
-    tail = block[:, -width:]
-    from_above = lax.ppermute(tail, axis, [(i, i + 1) for i in range(count - 1)])
-    from_below = lax.ppermute(head, axis, [(i + 1, i) for i in range(count - 1)])
-    return jnp.concatenate([from_above, block, from_below], axis=1)
+def select_tree(zone, table):
+    level = [table[number] for number in range(table.shape[0])]
+    bit = 1
+    while len(level) > 1:
+        pick = (zone & bit) != 0
+        level = [jnp.where(pick, level[k + 1], level[k]) for k in range(0, len(level), 2)]
+        bit *= 2
+    return level[0]
+
+
+def sweeps(source, coef, inside):
+    coef_pad = pad_rows(coef)
+    state = source
+    for number in range(SWEEPS):
+        state = relax_step(pad_rows(state), source, coef_pad, RELAX_WEIGHTS[number])
+        if inside is not None:
+            state = jnp.where(inside, state, jnp.float32(0.0))
+    return state
 
 
 def surrogate(cells, weight_in, bias_in, weight_mid, bias_mid, weight_out, bias_out, rate):
@@ -92,18 +103,37 @@
     bias_out,
 ):
     count_here, rows_here, columns = fields.shape
+    count = lax.axis_size("space")
+    raw = jnp.concatenate([fields, zone_ids.astype(jnp.float32)[None]], 0)
+    from_above = lax.ppermute(raw[:, -HALO:], "space", [(i, i + 1) for i in range(count - 1)])
+    from_below = lax.ppermute(raw[:, :HALO], "space", [(i + 1, i) for i in range(count - 1)])
     coefs = lookup(zone_ids, diffusivity)
-    stacked = with_halo(jnp.concatenate([fields, coefs], 0), "space", HALO)
-    fields_ext = stacked[:count_here]
-    coef_pad = pad_rows(stacked[count_here:])
-    first_row = lax.axis_index("space") * rows_here - HALO
-    global_row = first_row + lax.broadcasted_iota(jnp.int32, (1, rows_here + 2 * HALO, 1), 1)
-    inside = (global_row >= 0) & (global_row < rows_here * lax.axis_size("space"))
-    state = fields_ext
-    for number in range(SWEEPS):
-        state = relax_step(pad_rows(state), fields_ext, coef_pad, RELAX_WEIGHTS[number])
-        state = jnp.where(inside, state, jnp.float32(0.0))
-    state = state[:, HALO : HALO + rows_here]
+    interior = sweeps(fields, coefs, None)
+    strip = 3 * HALO
+    first_row = lax.axis_index("space") * rows_here
+    offsets = jnp.array([-HALO, rows_here - 2 * HALO], jnp.int32)[:, None, None]
+    global_row = first_row + offsets + lax.broadcasted_iota(jnp.int32, (2, strip, 1), 1)
+    inside = (global_row >= 0) & (global_row < rows_here * count)
+    halo = jnp.stack([from_above, from_below])
+    halo_fields = halo[:, 0]
+    halo_coef = select_tree(halo[:, 1].astype(jnp.int32), diffusivity[0])
+    strip_fields = jnp.stack(
+        [
+            jnp.concatenate([halo_fields[0], fields[0, : 2 * HALO]], 0),
+            jnp.concatenate([fields[0, -2 * HALO :], halo_fields[1]], 0),
+        ]
+    )
+    strip_coef = jnp.stack(
+        [
+            jnp.concatenate([halo_coef[0], coefs[0, : 2 * HALO]], 0),
+            jnp.concatenate([coefs[0, -2 * HALO :], halo_coef[1]], 0),
+        ]
+    )
+    strip_coef = jnp.where(inside, strip_coef, jnp.float32(0.0))
+    edges = sweeps(strip_fields, strip_coef, inside)
+    state = jnp.concatenate(
+        [edges[0, HALO : 2 * HALO], interior[0, HALO : rows_here - HALO], edges[1, HALO : 2 * HALO]], 0
+    )[None]
 
     chunks = columns // CHUNK
     outgoing = state[0].reshape(rows_here, chunks, CHUNK).transpose(1, 0, 2)

time: 102 us -> 125 us (1.23)
  other arithmetic: 8.03 us -> 23.2 us
  local copies, waits for them, and re-layouts: 2.94 us -> 14 us
  waiting for transfers between devices: 4.04 us -> 0.01 us
    select_n x3 -> x5, other arithmetic: 2.17 us -> 9.17 us  [the longest x1 6.08 us: select_tree(): jnp.where(pick, level[k + 1], level[k])]
    slice x2 -> x12, local copies, waits for them, and re-layouts: 0.14 us -> 6.4 us  [the longest x6 2.88 us: relax_step(): jnp.roll(middle, 1, 2)]
    squeeze x0 -> x5, local copies, waits for them, and re-layouts: none -> 5.46 us  [the longest x1 1.8 us: on_device(): coefs[0, :2 * HALO]]
    ppermute x2, waiting for transfers between devices: 4.04 us -> 0.01 us  [the longest x1 0.01 us: on_device(): lax.ppermute(raw[:, :HALO], 'space', [(i + 1, i) for i in range(count - 1)])]
    add x0 -> x4, other arithmetic: none -> 3.31 us  [the longest x3 3.3 us: relax_step(): return middle + weight * (source - image) / diagonal]
    add x1, other arithmetic: 0.67 us -> 3.26 us  [relax_step(): diagonal = 1.0 + face_north + face_south + face_east + face_west]
    concatenate x1 -> x0, other arithmetic: 1.6 us -> none  [with_halo(): return jnp.concatenate([from_above, block, from_below], axis=1)]
    broadcast_in_dim x0 -> x1, other arithmetic: none -> 1.28 us  [on_device(): raw = jnp.concatenate([fields, zone_ids.astype(jnp.float32)[None]], 0)]
  transfers between devices with their start and end apart: 2 -> 2, of which waited for: 2 -> 0; matrix products, arithmetic and copies ran while one was open for 0% -> 16% of each run, Pallas kernels for 0% -> 2%
where the time goes in v4:
time: 125 us; the launch traced here: 124 us
  blocking collectives  51.4 us (41%)
  other arithmetic  23.2 us (19%)
  matrix products  20 us (16%)
  local copies, waits for them, and re-layouts  14 us (11%)
  starting transfers between devices  12.7 us (10%)
  Pallas kernels  2.35 us (2%)
    all_to_all x1, blocking collectives, on_device(): incoming = lax.all_to_all(outgoing, 'field', 0, 0, tiled=True)  35.5 us
    all_to_all x1, blocking collectives, on_device(): lax.all_to_all(delta.reshape(FIELDS, rows_here, CHUNK), 'field', 0, 0, ti...  16 us
    dot_general x1, matrix products, surrogate(): jnp.dot(weight_out, hidden, preferred_element_type=jnp.float32)  12.5 us
    ppermute x1, starting transfers between devices, on_device(): lax.ppermute(raw[:, :HALO], 'space', [(i + 1, i) for i in range(count - 1)])  8.48 us
    dot_general x1, matrix products, surrogate(): jnp.dot(weight_in, inputs, preferred_element_type=jnp.float32)  7.51 us
    select_n x1, other arithmetic, select_tree(): jnp.where(pick, level[k + 1], level[k])  6.08 us
    ppermute x1, starting transfers between devices, on_device(): lax.ppermute(raw[:, -HALO:], 'space', [(i, i + 1) for i in range(count -...  4.27 us
    add x3, other arithmetic, relax_step(): return middle + weight * (source - image) / diagonal  3.3 us
  transfers between devices with their start and end apart: 2, of which 0 were waited for; matrix products, arithmetic and copies ran while one was open for 16% of the time, Pallas kernels for 2%

profile of v4, /device:TPU:8, one launch (start us, length us, event | category | flops | bytes accessed | tf_op | source)
XLA Modules:
  0.0 124.1 jit_solution(12365389717477712189)
XLA Ops:
  0.0 1.3 %convert_bitcast_fusion.1 = f32[1,32,6144]{2,1,0:T(8,128)S(1)} fusion(s32[32,6144]{1,0:T(8,128)} %zone_ref.1), kind=kLoop, calls=%fused_computation.117 | loop fusion | flops 196608 | bytes 1572864 | tf_op jit(solution)/shard_map/broadcast_in_dim | solution.py:107
  1.3 1.9 %pad_maximum_fusion.4 = (f32[2,3,6144]{2,1,0:T(4,128)}, f32[2,3,6144]{2,1,0:T(4,128)}) fusion(f32[1,32,6144]{2,1,0:T(8,128)S(1)} %convert_bitcast_fusion.1, f32[1,32,6144]{2,1,0:T(8,128)} %param.11), kind=kLoop, calls=%fused_computation.131 | loop fusion | flops 73728 | bytes 1867776 | tf_op jit(solution)/shard_map/slice | solution.py:108
  3.1 4.3 %collective-permute-start = (f32[2,3,6144]{2,1,0:T(4,128)}, f32[2,3,6144]{2,1,0:T(4,128)}, u32[]{:S(2)}, u32[]{:S(2)}) collective-permute-start(f32[2,3,6144]{2,1,0:T(4,128)} %get-tuple-element.16), channel_id=1, source_target_pairs={{0,16},{16,32},{32,48},{48,64},{64,80},{80,96},{96,112},{112,128},... | collective-permute-start | bytes 442376 | tf_op jit(solution)/shard_map/ppermute | solution.py:108
  7.4 8.5 %collective-permute-start.1 = (f32[2,3,6144]{2,1,0:T(4,128)}, f32[2,3,6144]{2,1,0:T(4,128)}, u32[]{:S(2)}, u32[]{:S(2)}) collective-permute-start(f32[2,3,6144]{2,1,0:T(4,128)} %get-tuple-element.17), channel_id=1, source_target_pairs={{16,0},{32,16},{48,32},{64,48},{80,64},{96,80},{112,96},{128,112},... | collective-permute-start | bytes 442376 | tf_op jit(solution)/shard_map/ppermute | solution.py:109
  15.9 0.8 fusion.82
  16.7 1.8 %slice_bitcast_fusion.3 = (f32[6,6144]{1,0:T(8,128)}, f32[6,6144]{1,0:T(8,128)}) fusion(f32[1,32,6144]{2,1,0:T(8,128)} %param.11), kind=kLoop, calls=%fused_computation.137 | loop fusion | bytes 589824 | tf_op jit(solution)/shard_map/squeeze | solution.py:122
  18.5 2.4 %shard_map.109 = f32[1,32,6144]{2,1,0:T(8,128)} custom-call(f32[1,8]{1,0:T(1,128)} %table_ref.1, s32[32,6144]{1,0:T(8,128)} %zone_ref.1), custom_call_target="tpu_custom_call" | custom-call | tf_op jit(solution)/shard_map/pallas_call | solution.py:45
  21.7 1.8 %slice_bitcast_fusion.1 = (f32[6,6144]{1,0:T(8,128)}, f32[6,6144]{1,0:T(8,128)}) fusion(f32[1,32,6144]{2,1,0:T(8,128)} %shard_map.109), kind=kLoop, calls=%fused_computation.127 | loop fusion | bytes 589824 | tf_op jit(solution)/shard_map/squeeze | solution.py:128
  23.5 1.7 %fusion.84 = (f32[1,32,6143]{2,1,0:T(8,128)S(1)}, f32[1,32,6143]{2,1,0:T(8,128)S(1)}) fusion(f32[1,32,6144]{2,1,0:T(8,128)} %shard_map.109), kind=kLoop, calls=%fused_computation.158 | loop fusion | bytes 3145216 | tf_op jit(solution)/shard_map/jit(_roll_static)/slice | solution.py:25
  25.4 3.3 %add_add_fusion = (f32[1,32,6144]{2,1,0:T(8,128)}, f32[1,32,6144]{2,1,0:T(8,128)S(1)}, f32[1,32,6144]{2,1,0:T(8,128)S(1)}, f32[1,32,6144]{2,1,0:T(8,128)S(1)}, f32[1,32,6144]{2,1,0:T(8,128)S(1)}) fusion(f32[1,32,6144]{2,1,0:T(8,128)} %shard_map.109, f32[1,32,6143]{2,1,0:T(8,128)S(1)} %get-tuple-element.35, f32[1,32,1]{2,1,0:T(8,128)S(1)} %get-tuple-element.37, ...), kind=kLoop, calls=%fused_computation.111 | loop fusion | flops 2752512 | bytes 6291456 | tf_op jit(solution)/shard_map/add | solution.py:27
  30.4 1.4 %fusion.79 = (f32[1,32,6143]{2,1,0:T(8,128)}, f32[1,32,6143]{2,1,0:T(8,128)}) fusion(f32[1,32,6144]{2,1,0:T(8,128)S(1)} %fusion.32), kind=kLoop, calls=%fused_computation.153 | loop fusion | bytes 3145216 | tf_op jit(solution)/shard_map/jit(_roll_static)/slice | solution.py:29
  31.8 2.0 %fusion.36 = (f32[1,32,6144]{2,1,0:T(8,128)S(1)}, f32[1,32,6144]{2,1,0:T(8,128)S(1)}) fusion(f32[1,32,6144]{2,1,0:T(8,128)} %copy-done.3, f32[1,32,6144]{2,1,0:T(8,128)S(1)} %fusion.32, f32[1,32,6144]{2,1,0:T(8,128)} %copy-done.2, f32[1,32,6144]{2,1,0:T(8,128)S(1)} %get-tuple-element.6, f32[1,32,6144]{2,1,0:T(8,128)S(1)} %get-tuple-element.7, ...), kind=kLoop, calls=%fused_computation.58 | loop fusion | flops 2162688 | bytes 6291456 | tf_op jit(solution)/shard_map/sub | solution.py:28
  33.8 2.1 %slice_add_fusion = f32[1,26,6144]{2,1,0:T(8,128)S(1)} fusion(f32[1,32,6144]{2,1,0:T(8,128)S(1)} %fusion.32, f32[1,32,6144]{2,1,0:T(8,128)} %get-tuple-element.5, f32[1,32,6144]{2,1,0:T(8,128)S(1)} %copy-done.1, f32[1,32,6144]{2,1,0:T(8,128)S(1)} %get-tuple-element.6, f32[1,32,6144]{2,1,0:T(8,128)S(1)} %get-tuple-element.25, ...), kind=kLoop, calls=%fused_computation.62 | loop fusion | flops 1277952 | bytes 5259264 | tf_op jit(solution)/shard_map/add | solution.py:30
  36.8 0.9 slice_bitcast_fusion.7
  37.8 0.9 slice_bitcast_fusion.6
  39.2 6.1 %select_select_fusion = f32[2,1,3,6144]{3,2,1,0:T(4,128)S(1)} fusion(f32[1,2,3,6144]{3,2,1,0:T(4,128)} %bitcast.6, f32[1,2,3,6144]{3,2,1,0:T(4,128)} %bitcast.1, f32[]{:T(128)} %bitcast.16, f32[]{:T(128)} %bitcast.15, f32[]{:T(128)} %bitcast.14, f32[]{:T(128)} %bitcast.13, f32[]{:T(128)} %bitcast.12, f32[]{:T(128)} %bitcast.11, f32[]{:T(128)} %bitcast.10, ...), kind=kLoop, calls=%fused_computation.132 | loop fusion | flops 552960 | bytes 442400 | tf_op jit(solution)/shard_map/jit(_where)/select_n | solution.py:61
  46.0 1.1 broadcast_select_fusion.1
  47.4 0.9 broadcast_select_fusion
  48.7 0.9 fusion.64
  50.0 35.5 %all_to_all.10 = f32[16,32,384]{2,1,0:T(8,128)S(1)} all-to-all(f32[16,32,384]{2,1,0:T(8,128)S(1)} %copy.15), channel_id=1, replica_groups=mesh['space'=32,'field'=16] {'field'}, dimensions={0} | all-to-all | bytes 1572864 | tf_op jit(solution)/shard_map/all_to_all | solution.py:140
  85.8 7.5 %fusion.6 = bf16[384,12288]{0,1:T(8,128)(2,1)} fusion(bf16[16,12288]{1,0:T(8,128)(2,1)S(1)} %bitcast.104, bf16[384,16]{0,1:T(8,128)(2,1)S(1)} %copy-done.10, f32[384]{0:T(512)S(1)} %copy-done.12), kind=kOutput, calls=%fused_computation.10 | convolution fusion | flops 179306496 | bytes 9844224 | tf_op jit(solution)/shard_map/dot_general | solution.py:79
  93.4 12.5 %fusion.9 = bf16[16,12288]{1,0:T(8,128)(2,1)S(1)} fusion(bf16[16,384]{1,0:T(8,128)(2,1)S(1)} %copy-done.11, bf16[384,12288]{0,1:T(8,128)(2,1)} %fusion.6, bf16[384,384]{1,0:T(8,128)(2,1)S(1)} %copy-done, f32[384]{0:T(512)S(1)} %copy-done.13, f32[16]{0:T(128)S(1)} %copy-done.14), kind=kOutput, calls=%fused_computation.14 | convolution fusion | flops 3803578368 | bytes 10139200 | tf_op jit(solution)/shard_map/dot_general | solution.py:84
  106.5 16.0 %all_to_all.11 = bf16[16,32,384]{2,1,0:T(8,128)(2,1)S(1)} all-to-all(bf16[16,32,384]{2,1,0:T(8,128)(2,1)S(1)} %bitcast.100), channel_id=1, replica_groups=mesh['space'=32,'field'=16] {'field'}, dimensions={0} | all-to-all | bytes 786432 | tf_op jit(solution)/shard_map/all_to_all | solution.py:151
  123.1 1.0 maximum_add_fusion.4
  (76 shorter events, 7.4 us)
Async XLA Ops:
  0.0 93.3 %copy-start = (bf16[384,384]{1,0:T(8,128)(2,1)S(1)}, bf16[384,384]{1,0:T(8,128)(2,1)}, u32[]{:S(2)}) copy-start(bf16[384,384]{1,0:T(8,128)(2,1)} %param.17) | copy-start | bytes 884740
  0.0 25.1 %copy-start.1 = (f32[1,32,6144]{2,1,0:T(8,128)S(1)}, f32[1,32,6144]{2,1,0:T(8,128)}, u32[]{:S(2)}) copy-start(f32[1,32,6144]{2,1,0:T(8,128)} %param.11) | copy-start | bytes 2359300
  3.1 33.7 %collective-permute-start = (f32[2,3,6144]{2,1,0:T(4,128)}, f32[2,3,6144]{2,1,0:T(4,128)}, u32[]{:S(2)}, u32[]{:S(2)}) collective-permute-start(f32[2,3,6144]{2,1,0:T(4,128)} %get-tuple-element.16), channel_id=1, source_target_pairs={{0,16},{16,32},{32,48},{48,64},{64,80},{80,96},{96,112},{112,128},... | collective-permute-start | bytes 442376 | tf_op jit(solution)/shard_map/ppermute | solution.py:108
  7.4 30.3 %collective-permute-start.1 = (f32[2,3,6144]{2,1,0:T(4,128)}, f32[2,3,6144]{2,1,0:T(4,128)}, u32[]{:S(2)}, u32[]{:S(2)}) collective-permute-start(f32[2,3,6144]{2,1,0:T(4,128)} %get-tuple-element.17), channel_id=1, source_target_pairs={{16,0},{32,16},{48,32},{64,48},{80,64},{96,80},{112,96},{128,112},... | collective-permute-start | bytes 442376 | tf_op jit(solution)/shard_map/ppermute | solution.py:109
  28.7 1.6 %copy-start.2 = (f32[1,32,6144]{2,1,0:T(8,128)}, f32[1,32,6144]{2,1,0:T(8,128)S(1)}, u32[]{:S(2)}) copy-start(f32[1,32,6144]{2,1,0:T(8,128)S(1)} %get-tuple-element.8) | copy-start | bytes 2359300
  28.7 1.7 %copy-start.3 = (f32[1,32,6144]{2,1,0:T(8,128)}, f32[1,32,6144]{2,1,0:T(8,128)S(1)}, u32[]{:S(2)}) copy-start(f32[1,32,6144]{2,1,0:T(8,128)S(1)} %get-tuple-element.9) | copy-start | bytes 2359300
  28.7 3.1 %copy-start.15 = (s32[2]{0:T(128)S(1)}, s32[2]{0:T(128)}, u32[]{:S(2)}) copy-start(s32[2]{0:T(128)} %constant.12.clone) | copy-start | bytes 28
  30.3 5.9 %copy-start.8 = (f32[1,8]{1,0:T(1,128)S(1)}, f32[1,8]{1,0:T(1,128)}, u32[]{:S(2)}) copy-start(f32[1,8]{1,0:T(1,128)} %table_ref.1) | copy-start | bytes 100
  31.8 6.9 %copy-start.6 = (f32[6,6144]{1,0:T(8,128)S(1)}, f32[6,6144]{1,0:T(8,128)}, u32[]{:S(2)}) copy-start(f32[6,6144]{1,0:T(8,128)} %get-tuple-element.56) | copy-start | bytes 442372
  31.8 6.9 %copy-start.7 = (f32[6,6144]{1,0:T(8,128)S(1)}, f32[6,6144]{1,0:T(8,128)}, u32[]{:S(2)}) copy-start(f32[6,6144]{1,0:T(8,128)} %get-tuple-element.57) | copy-start | bytes 442372
  33.8 11.5 %copy-start.4 = (f32[6,6144]{1,0:T(8,128)S(1)}, f32[6,6144]{1,0:T(8,128)}, u32[]{:S(2)}) copy-start(f32[6,6144]{1,0:T(8,128)} %get-tuple-element.50) | copy-start | bytes 442372
  33.8 11.5 %copy-start.5 = (f32[6,6144]{1,0:T(8,128)S(1)}, f32[6,6144]{1,0:T(8,128)}, u32[]{:S(2)}) copy-start(f32[6,6144]{1,0:T(8,128)} %get-tuple-element.51) | copy-start | bytes 442372
  48.3 37.4 %copy-start.10 = (bf16[384,16]{0,1:T(8,128)(2,1)S(1)}, bf16[384,16]{0,1:T(8,128)(2,1)}, u32[]{:S(2)}) copy-start(bf16[384,16]{0,1:T(8,128)(2,1)} %param.15) | copy-start | bytes 36868
  48.3 37.4 %copy-start.12 = (f32[384]{0:T(512)S(1)}, f32[384]{0:T(512)}, u32[]{:S(2)}) copy-start(f32[384]{0:T(512)} %param.16) | copy-start | bytes 4612
  85.8 7.6 %copy-start.11 = (bf16[16,384]{1,0:T(8,128)(2,1)S(1)}, bf16[16,384]{1,0:T(8,128)(2,1)}, u32[]{:S(2)}) copy-start(bf16[16,384]{1,0:T(8,128)(2,1)} %param.19) | copy-start | bytes 36868
  85.8 7.5 %copy-start.13 = (f32[384]{0:T(512)S(1)}, f32[384]{0:T(512)}, u32[]{:S(2)}) copy-start(f32[384]{0:T(512)} %param.18) | copy-start | bytes 4612
  85.8 7.5 %copy-start.14 = (f32[16]{0:T(128)S(1)}, f32[16]{0:T(128)}, u32[]{:S(2)}) copy-start(f32[16]{0:T(128)} %param.20) | copy-start | bytes 196
  93.4 12.7 %copy-start.9 = (f32[15]{0:T(128)S(1)}, f32[15]{0:T(128)}, u32[]{:S(2)}) copy-start(f32[15]{0:T(128)} %param.14) | copy-start | bytes 184

commit v5 on v3

--- a/solution.py
+++ b/solution.py
@@ -8,6 +8,7 @@
 FIELDS = 16
 SWEEPS = 3
 HALO = SWEEPS
+ROOM = 8
 CHUNK = 384
 
 RELAX_WEIGHTS = (0.8, 1.25, 0.95)
@@ -53,13 +54,61 @@
     )(diffusivity, zone_ids)
 
 
-def with_halo(block, axis, width):
+def with_halo(block, axis, width, room):
     count = lax.axis_size(axis)
     head = block[:, :width]
     tail = block[:, -width:]
     from_above = lax.ppermute(tail, axis, [(i, i + 1) for i in range(count - 1)])
     from_below = lax.ppermute(head, axis, [(i + 1, i) for i in range(count - 1)])
-    return jnp.concatenate([from_above, block, from_below], axis=1)
+    zeros = jnp.zeros(block.shape[:1] + (room - width,) + block.shape[2:], block.dtype)
+    return jnp.concatenate([zeros, from_above, block, from_below, zeros], axis=1)
+
+
+def diffusion_kernel(bounds_ref, ext_ref, state_ref, chunks_ref):
+    _, rows, cols = ext_ref.shape
+    here = state_ref.shape[1]
+    q = lax.broadcasted_iota(jnp.int32, (rows, cols), 0)
+    inside = (q >= bounds_ref[0]) & (q < bounds_ref[1])
+    coef = ext_ref[1]
+    face_north = 0.5 * (coef + pltpu.roll(coef, rows - 1, 0))
+    face_south = 0.5 * (coef + pltpu.roll(coef, 1, 0))
+    face_east = 0.5 * (coef + pltpu.roll(coef, cols - 1, 1))
+    face_west = 0.5 * (coef + pltpu.roll(coef, 1, 1))
+    diagonal = 1.0 + face_north + face_south + face_east + face_west
+    source = ext_ref[0]
+    state = source
+    for weight in RELAX_WEIGHTS:
+        image = (
+            diagonal * state
+            - face_north * pltpu.roll(state, rows - 1, 0)
+            - face_south * pltpu.roll(state, 1, 0)
+        )
+        image = image - face_east * pltpu.roll(state, cols - 1, 1) - face_west * pltpu.roll(state, 1, 1)
+        state = state + weight * (source - image) / diagonal
+        state = jnp.where(inside, state, jnp.float32(0.0))
+    state = state[ROOM : ROOM + here]
+    state_ref[0] = state
+    for number in range(chunks_ref.shape[0]):
+        chunks_ref[number] = state[:, number * CHUNK : (number + 1) * CHUNK]
+
+
+def diffusion(ext, bounds, here):
+    _, rows, cols = ext.shape
+    return pl.pallas_call(
+        diffusion_kernel,
+        in_specs=[
+            pl.BlockSpec(memory_space=pltpu.SMEM),
+            pl.BlockSpec(memory_space=pltpu.VMEM),
+        ],
+        out_specs=[
+            pl.BlockSpec(memory_space=pltpu.VMEM),
+            pl.BlockSpec(memory_space=pltpu.VMEM),
+        ],
+        out_shape=[
+            jax.ShapeDtypeStruct((1, here, cols), jnp.float32),
+            jax.ShapeDtypeStruct((cols // CHUNK, here, CHUNK), jnp.float32),
+        ],
+    )(bounds, ext)
 
 
 def surrogate(cells, weight_in, bias_in, weight_mid, bias_mid, weight_out, bias_out, rate):
@@ -93,20 +142,15 @@
 ):
     count_here, rows_here, columns = fields.shape
     coefs = lookup(zone_ids, diffusivity)
-    stacked = with_halo(jnp.concatenate([fields, coefs], 0), "space", HALO)
-    fields_ext = stacked[:count_here]
-    coef_pad = pad_rows(stacked[count_here:])
-    first_row = lax.axis_index("space") * rows_here - HALO
-    global_row = first_row + lax.broadcasted_iota(jnp.int32, (1, rows_here + 2 * HALO, 1), 1)
-    inside = (global_row >= 0) & (global_row < rows_here * lax.axis_size("space"))
-    state = fields_ext
-    for number in range(SWEEPS):
-        state = relax_step(pad_rows(state), fields_ext, coef_pad, RELAX_WEIGHTS[number])
-        state = jnp.where(inside, state, jnp.float32(0.0))
-    state = state[:, HALO : HALO + rows_here]
-
-    chunks = columns // CHUNK
-    outgoing = state[0].reshape(rows_here, chunks, CHUNK).transpose(1, 0, 2)
+    ext = with_halo(jnp.concatenate([fields, coefs], 0), "space", HALO, ROOM)
+    first = ROOM - lax.axis_index("space") * rows_here
+    bounds = jnp.stack(
+        [
+            jnp.maximum(ROOM - HALO, first),
+            jnp.minimum(ROOM + rows_here + HALO, first + rows_here * lax.axis_size("space")),
+        ]
+    ).astype(jnp.int32)
+    state, outgoing = diffusion(ext, bounds, rows_here)
     incoming = lax.all_to_all(outgoing, "field", 0, 0, tiled=True)
     delta = surrogate(
         incoming.reshape(FIELDS, rows_here * CHUNK),

time: 102 us -> 111 us (1.088)
  Pallas kernels: 2.44 us -> 8.8 us
  other arithmetic: 8.03 us -> 4.89 us
  local copies, waits for them, and re-layouts: 2.94 us -> 5.62 us
  waiting for transfers between devices: 4.04 us -> 6.29 us
    pallas_call x0 -> x1, Pallas kernels: none -> 6.4 us  [diffusion(): pl.pallas_call(diffusion_kernel, in_specs=[pl.BlockSpec(memory_space=pltp...]
    concatenate x0 -> x1, local copies, waits for them, and re-layouts: none -> 4.65 us  [with_halo(): jnp.concatenate([zeros, from_above, block, from_below, zeros], axis=1)]
    ppermute x1, waiting for transfers between devices: 2.86 us -> 6.23 us  [with_halo(): lax.ppermute(tail, axis, [(i, i + 1) for i in range(count - 1)])]
    ppermute x1, starting transfers between devices: 8.47 us -> 10.8 us  [with_halo(): lax.ppermute(head, axis, [(i + 1, i) for i in range(count - 1)])]
    ppermute x1, starting transfers between devices: 4.28 us -> 1.92 us  [with_halo(): lax.ppermute(tail, axis, [(i, i + 1) for i in range(count - 1)])]
    select_n x3 -> x0, other arithmetic: 2.17 us -> none  [on_device(): state = jnp.where(inside, state, jnp.float32(0.0))]
    slice x7 -> x0, local copies, waits for them, and re-layouts: 1.6 us -> none  [the longest x5 1.46 us: relax_step(): jnp.roll(middle, -1, 2)]
    slice x1 -> x0, other arithmetic: 1.35 us -> none  [with_halo(): tail = block[:, -width:]]
  transfers between devices with their start and end apart: 2 -> 2, of which waited for: 2 -> 2; matrix products, arithmetic and copies ran while one was open for 0% -> 2% of each run, Pallas kernels for 0% -> 0%
where the time goes in v5:
time: 111 us; the launch traced here: 110 us
  blocking collectives  51.6 us (46%)
  matrix products  20.1 us (18%)
  starting transfers between devices  12.8 us (12%)
  Pallas kernels  8.8 us (8%)
  waiting for transfers between devices  6.29 us (6%)
  local copies, waits for them, and re-layouts  5.62 us (5%)
  other arithmetic  4.89 us (4%)
    all_to_all x1, blocking collectives, on_device(): incoming = lax.all_to_all(outgoing, 'field', 0, 0, tiled=True)  35.7 us
    all_to_all x1, blocking collectives, on_device(): lax.all_to_all(delta.reshape(FIELDS, rows_here, CHUNK), 'field', 0, 0, ti...  16 us
    dot_general x1, matrix products, surrogate(): jnp.dot(weight_out, hidden, preferred_element_type=jnp.float32)  12.6 us
    ppermute x1, starting transfers between devices, with_halo(): lax.ppermute(head, axis, [(i + 1, i) for i in range(count - 1)])  10.8 us
    dot_general x1, matrix products, surrogate(): jnp.dot(weight_in, inputs, preferred_element_type=jnp.float32)  7.52 us
    pallas_call x1, Pallas kernels, diffusion(): pl.pallas_call(diffusion_kernel, in_specs=[pl.BlockSpec(memory_space=pltp...  6.4 us
    ppermute x1, waiting for transfers between devices, with_halo(): lax.ppermute(tail, axis, [(i, i + 1) for i in range(count - 1)])  6.23 us
    concatenate x1, local copies, waits for them, and re-layouts, with_halo(): jnp.concatenate([zeros, from_above, block, from_below, zeros], axis=1)  4.65 us
  transfers between devices with their start and end apart: 2, of which 2 were waited for; matrix products, arithmetic and copies ran while one was open for 2% of the time, Pallas kernels for 0%

profile of v5, /device:TPU:8, one launch (start us, length us, event | category | flops | bytes accessed | tf_op | source)
XLA Modules:
  0.0 110.3 jit_solution(395916126501231173)
XLA Ops:
  0.0 2.4 %shard_map.100 = f32[1,32,6144]{2,1,0:T(8,128)} custom-call(f32[1,8]{1,0:T(1,128)} %table_ref.1, s32[32,6144]{1,0:T(8,128)} %zone_ref.1), custom_call_target="tpu_custom_call" | custom-call | tf_op jit(solution)/shard_map/pallas_call | solution.py:46
  2.4 1.3 %fusion.11 = (f32[2,3,6144]{2,1,0:T(4,128)S(1)}, f32[2,3,6144]{2,1,0:T(4,128)S(1)}) fusion(f32[1,32,6144]{2,1,0:T(8,128)} %param.10, f32[1,32,6144]{2,1,0:T(8,128)} %shard_map.100), kind=kLoop, calls=%fused_computation.24 | loop fusion | flops 73728 | bytes 1867776 | tf_op jit(solution)/shard_map/concatenate | solution.py:145
  3.7 10.8 %collective-permute-start.1 = (f32[2,3,6144]{2,1,0:T(4,128)S(1)}, f32[2,3,6144]{2,1,0:T(4,128)S(1)}, u32[]{:S(2)}, u32[]{:S(2)}) collective-permute-start(f32[2,3,6144]{2,1,0:T(4,128)S(1)} %get-tuple-element.9), channel_id=1, source_target_pairs={{16,0},{32,16},{48,32},{64,48},{80,64},{96,80},{112,96},{128,112},... | collective-permute-start | bytes 442376 | tf_op jit(solution)/shard_map/ppermute | solution.py:62
  14.5 1.9 %collective-permute-start = (f32[2,3,6144]{2,1,0:T(4,128)S(1)}, f32[2,3,6144]{2,1,0:T(4,128)S(1)}, u32[]{:S(2)}, u32[]{:S(2)}) collective-permute-start(f32[2,3,6144]{2,1,0:T(4,128)S(1)} %get-tuple-element.10), channel_id=1, source_target_pairs={{0,16},{16,32},{32,48},{48,64},{64,80},{80,96},{96,112},{112,128},... | collective-permute-start | bytes 442376 | tf_op jit(solution)/shard_map/ppermute | solution.py:61
  16.5 1.5 %pad_maximum_fusion = f32[2,32,6144]{2,1,0:T(8,128)S(1)} fusion(f32[1,32,6144]{2,1,0:T(8,128)} %shard_map.100, f32[1,32,6144]{2,1,0:T(8,128)} %param.10), kind=kLoop, calls=%fused_computation.17 | loop fusion | flops 393216 | bytes 3145728 | tf_op jit(solution)/shard_map/concatenate | solution.py:145
  18.0 0.7 pad_add_fusion.bounds_ref
  18.6 0.1 collective-permute-done.1
  18.7 6.2 %collective-permute-done = f32[2,3,6144]{2,1,0:T(4,128)S(1)} collective-permute-done((f32[2,3,6144]{2,1,0:T(4,128)S(1)}, f32[2,3,6144]{2,1,0:T(4,128)S(1)}, u32[]{:S(2)}, u32[]{:S(2)}) %collective-permute-start) | collective-permute-done | bytes 147488 | tf_op jit(solution)/shard_map/ppermute | solution.py:61
  24.9 4.6 %concatenate.10.ext_ref = f32[2,48,6144]{2,1,0:T(8,128)} concatenate(f32[2,5,6144]{2,1,0:T(8,128)S(1)} %broadcast_in_dim.2, f32[2,3,6144]{2,1,0:T(4,128)S(1)} %collective-permute-done, f32[2,32,6144]{2,1,0:T(8,128)S(1)} %pad_maximum_fusion, f32[2,3,6144]{2,1,0:T(4,128)S(1)} %collective-permute-done.1, f32[2,5,6144]{2,1,0:T(8,128)S(1)} %broadcast_in_dim.2), dimensions={1} | concatenate | bytes 4718592 | tf_op jit(solution)/shard_map/concatenate | solution.py:64
  29.6 6.4 %shard_map.101 = (f32[1,32,6144]{2,1,0:T(8,128)}, f32[16,32,384]{2,1,0:T(8,128)}) custom-call(s32[2]{0:T(128)} %pad_add_fusion.bounds_ref, f32[2,48,6144]{2,1,0:T(8,128)} %concatenate.10.ext_ref), custom_call_target="tpu_custom_call" | custom-call | tf_op jit(solution)/shard_map/pallas_call | solution.py:97
  36.0 35.7 %all_to_all.10 = f32[16,32,384]{2,1,0:T(8,128)S(1)} all-to-all(f32[16,32,384]{2,1,0:T(8,128)} %get-tuple-element.8), channel_id=1, replica_groups=mesh['space'=32,'field'=16] {'field'}, dimensions={0} | all-to-all | bytes 1572864 | tf_op jit(solution)/shard_map/all_to_all | solution.py:154
  71.7 0.1 copy.13
  71.9 0.1 copy.14
  72.0 7.5 %fusion.6 = bf16[384,12288]{0,1:T(8,128)(2,1)} fusion(bf16[16,12288]{1,0:T(8,128)(2,1)S(1)} %bitcast.50, bf16[384,16]{0,1:T(8,128)(2,1)S(1)} %copy-done.3, f32[384]{0:T(512)S(1)} %copy-done.5), kind=kOutput, calls=%fused_computation.10 | convolution fusion | flops 179306496 | bytes 9844224 | tf_op jit(solution)/shard_map/dot_general | solution.py:117
  79.5 12.6 %fusion.9 = bf16[16,12288]{1,0:T(8,128)(2,1)S(1)} fusion(bf16[16,384]{1,0:T(8,128)(2,1)S(1)} %copy-done.4, bf16[384,12288]{0,1:T(8,128)(2,1)} %fusion.6, bf16[384,384]{1,0:T(8,128)(2,1)S(1)} %copy-done, f32[384]{0:T(512)S(1)} %copy-done.6, f32[16]{0:T(128)S(1)} %copy-done.7), kind=kOutput, calls=%fused_computation.14 | convolution fusion | flops 3803578368 | bytes 10139200 | tf_op jit(solution)/shard_map/dot_general | solution.py:122
  92.1 0.1 slice.28
  92.2 0.1 add_tanh_fusion
  92.3 0.2 multiply_convert_fusion
  92.5 0.1 pad_maximum_fusion.1
  92.7 16.0 %all_to_all.11 = bf16[16,32,384]{2,1,0:T(8,128)(2,1)S(1)} all-to-all(bf16[16,32,384]{2,1,0:T(8,128)(2,1)S(1)} %bitcast.48), channel_id=1, replica_groups=mesh['space'=32,'field'=16] {'field'}, dimensions={0} | all-to-all | bytes 786432 | tf_op jit(solution)/shard_map/all_to_all | solution.py:165
  108.7 0.1 convert_bitcast_fusion
  108.7 0.5 copy.12
  109.2 0.1 reshape.28
  109.4 1.0 add.61
  (20 shorter events, 0.2 us)
Async XLA Ops:
  0.0 79.5 %copy-start = (bf16[384,384]{1,0:T(8,128)(2,1)S(1)}, bf16[384,384]{1,0:T(8,128)(2,1)}, u32[]{:S(2)}) copy-start(bf16[384,384]{1,0:T(8,128)(2,1)} %param.16) | copy-start | bytes 884740
  0.0 71.9 %copy-start.5 = (f32[384]{0:T(512)S(1)}, f32[384]{0:T(512)}, u32[]{:S(2)}) copy-start(f32[384]{0:T(512)} %param.15) | copy-start | bytes 4612
  0.0 71.9 %copy-start.3 = (bf16[384,16]{0,1:T(8,128)(2,1)S(1)}, bf16[384,16]{0,1:T(8,128)(2,1)}, u32[]{:S(2)}) copy-start(bf16[384,16]{0,1:T(8,128)(2,1)} %param.14) | copy-start | bytes 36868
  3.7 15.0 %collective-permute-start.1 = (f32[2,3,6144]{2,1,0:T(4,128)S(1)}, f32[2,3,6144]{2,1,0:T(4,128)S(1)}, u32[]{:S(2)}, u32[]{:S(2)}) collective-permute-start(f32[2,3,6144]{2,1,0:T(4,128)S(1)} %get-tuple-element.9), channel_id=1, source_target_pairs={{16,0},{32,16},{48,32},{64,48},{80,64},{96,80},{112,96},{128,112},... | collective-permute-start | bytes 442376 | tf_op jit(solution)/shard_map/ppermute | solution.py:62
  14.5 10.4 %collective-permute-start = (f32[2,3,6144]{2,1,0:T(4,128)S(1)}, f32[2,3,6144]{2,1,0:T(4,128)S(1)}, u32[]{:S(2)}, u32[]{:S(2)}) collective-permute-start(f32[2,3,6144]{2,1,0:T(4,128)S(1)} %get-tuple-element.10), channel_id=1, source_target_pairs={{0,16},{16,32},{32,48},{48,64},{64,80},{80,96},{96,112},{112,128},... | collective-permute-start | bytes 442376 | tf_op jit(solution)/shard_map/ppermute | solution.py:61
  71.9 7.6 %copy-start.4 = (bf16[16,384]{1,0:T(8,128)(2,1)S(1)}, bf16[16,384]{1,0:T(8,128)(2,1)}, u32[]{:S(2)}) copy-start(bf16[16,384]{1,0:T(8,128)(2,1)} %param.18) | copy-start | bytes 36868
  72.0 7.5 %copy-start.6 = (f32[384]{0:T(512)S(1)}, f32[384]{0:T(512)}, u32[]{:S(2)}) copy-start(f32[384]{0:T(512)} %param.17) | copy-start | bytes 4612
  72.0 7.5 %copy-start.7 = (f32[16]{0:T(128)S(1)}, f32[16]{0:T(128)}, u32[]{:S(2)}) copy-start(f32[16]{0:T(128)} %param.19) | copy-start | bytes 196
  79.5 12.8 %copy-start.2 = (f32[15]{0:T(128)S(1)}, f32[15]{0:T(128)}, u32[]{:S(2)}) copy-start(f32[15]{0:T(128)} %param.13) | copy-start | bytes 184
  79.5 29.8 %copy-start.1 = (f32[1,32,6144]{2,1,0:T(8,128)S(1)}, f32[1,32,6144]{2,1,0:T(8,128)}, u32[]{:S(2)}) copy-start(f32[1,32,6144]{2,1,0:T(8,128)} %get-tuple-element.7) | copy-start | bytes 2359300

commit v6 on v3

--- a/solution.py
+++ b/solution.py
@@ -9,6 +9,8 @@
 SWEEPS = 3
 HALO = SWEEPS
 CHUNK = 384
+ROW_BLOCK = 8
+NT = (((1,), (1,)), ((), ()))
 
 RELAX_WEIGHTS = (0.8, 1.25, 0.95)
 
@@ -62,21 +64,37 @@
     return jnp.concatenate([from_above, block, from_below], axis=1)
 
 
-def surrogate(cells, weight_in, bias_in, weight_mid, bias_mid, weight_out, bias_out, rate):
+def mlp_kernel(x_ref, w_in_ref, b_in_ref, w_mid_ref, b_mid_ref, w_out_ref, b_out_ref, rate_ref, o_ref):
+    rows = x_ref.shape[0]
+    cells = jnp.concatenate([x_ref[r].T for r in range(rows)], axis=0)
     inputs = cells.astype(jnp.bfloat16)
-    hidden = jax.nn.silu(
-        jnp.dot(weight_in, inputs, preferred_element_type=jnp.float32) + bias_in[:, None]
-    ).astype(jnp.bfloat16)
-    hidden = jax.nn.silu(
-        jnp.dot(weight_mid, hidden, preferred_element_type=jnp.float32) + bias_mid[:, None]
-    ).astype(jnp.bfloat16)
-    change = (jnp.dot(weight_out, hidden, preferred_element_type=jnp.float32) + bias_out[:, None]).astype(
-        jnp.bfloat16
-    )
-    heat = cells[-1] + change[-1].astype(jnp.float32)
-    factor = jnp.exp(rate[:, None] * jnp.tanh(heat)[None])
-    scaled = (change[:-1].astype(jnp.float32) * factor).astype(jnp.bfloat16)
-    return jnp.concatenate([scaled, change[-1:]], 0)
+    hidden = jax.nn.silu(lax.dot_general(inputs, w_in_ref[...], NT, preferred_element_type=jnp.float32) + b_in_ref[...])
+    hidden = hidden.astype(jnp.bfloat16)
+    hidden = jax.nn.silu(lax.dot_general(hidden, w_mid_ref[...], NT, preferred_element_type=jnp.float32) + b_mid_ref[...])
+    hidden = hidden.astype(jnp.bfloat16)
+    change = lax.dot_general(hidden, w_out_ref[...], NT, preferred_element_type=jnp.float32) + b_out_ref[...]
+    change = change.astype(jnp.bfloat16).astype(jnp.float32).T
+    x = cells.T
+    heat = x[FIELDS - 1 :] + change[FIELDS - 1 :]
+    factor = jnp.exp(rate_ref[...] * jnp.tanh(heat))
+    scaled = (change * factor).astype(jnp.bfloat16)
+    is_heat = lax.broadcasted_iota(jnp.int32, change.shape, 0) == FIELDS - 1
+    out = jnp.where(is_heat, change.astype(jnp.bfloat16), scaled)
+    for r in range(rows):
+        o_ref[r] = out[:, r * CHUNK : (r + 1) * CHUNK]
+
+def surrogate_rows(x, weight_in, bias_in, weight_mid, bias_mid, weight_out, bias_out, rate):
+    rows = x.shape[0]
+    full = lambda shape: pl.BlockSpec(shape, lambda i: (0,) * len(shape))
+    return pl.pallas_call(
+        mlp_kernel,
+        grid=(rows // ROW_BLOCK,),
+        in_specs=[pl.BlockSpec((ROW_BLOCK, FIELDS, CHUNK), lambda i: (i, 0, 0)),
+                  full(weight_in.shape), full(bias_in.shape), full(weight_mid.shape), full(bias_mid.shape),
+                  full(weight_out.shape), full(bias_out.shape), full(rate.shape)],
+        out_specs=pl.BlockSpec((ROW_BLOCK, FIELDS, CHUNK), lambda i: (i, 0, 0)),
+        out_shape=jax.ShapeDtypeStruct((rows, FIELDS, CHUNK), jnp.bfloat16),
+    )(x, weight_in, bias_in, weight_mid, bias_mid, weight_out, bias_out, rate)
 
 
 def on_device(
@@ -108,17 +126,18 @@
     chunks = columns // CHUNK
     outgoing = state[0].reshape(rows_here, chunks, CHUNK).transpose(1, 0, 2)
     incoming = lax.all_to_all(outgoing, "field", 0, 0, tiled=True)
-    delta = surrogate(
-        incoming.reshape(FIELDS, rows_here * CHUNK),
+    rate = jnp.concatenate([heat_rate, jnp.zeros((FIELDS - heat_rate.shape[0],), jnp.float32)])
+    delta = surrogate_rows(
+        incoming.transpose(1, 0, 2),
         weight_in,
-        bias_in,
+        bias_in[None],
         weight_mid,
-        bias_mid,
+        bias_mid[None],
         weight_out,
-        bias_out,
-        heat_rate,
+        bias_out[None],
+        rate[:, None],
     )
-    returned = lax.all_to_all(delta.reshape(FIELDS, rows_here, CHUNK), "field", 0, 0, tiled=True)
+    returned = lax.all_to_all(delta.transpose(1, 0, 2), "field", 0, 0, tiled=True)
     returned = returned.transpose(1, 0, 2).reshape(1, rows_here, columns)
     return state + returned.astype(jnp.float32)
 

time: 102 us -> 98.8 us (0.969)
  blocking collectives: 51.4 us -> 16 us
  waiting for transfers between devices: 4.04 us -> 27.4 us
  matrix products: 20 us -> 0 us
  Pallas kernels: 2.44 us -> 18.1 us
  starting transfers between devices: 12.8 us -> 22.4 us
  local copies, waits for them, and re-layouts: 2.94 us -> 8.45 us
  other arithmetic: 8.03 us -> 5.99 us
    all_to_all x2 -> x1, blocking collectives: 51.4 us -> 16 us  [on_device(): lax.all_to_all(delta.transpose(1, 0, 2), 'field', 0, 0, tiled=True)]
    all_to_all x0 -> x1, waiting for transfers between devices: none -> 23.3 us  [on_device(): incoming = lax.all_to_all(outgoing, 'field', 0, 0, tiled=True)]
    dot_general x2 -> x0, matrix products: 20 us -> none  [the longest x1 12.5 us: surrogate(): jnp.dot(weight_out, hidden, preferred_element_type=jnp.float32)]
    pallas_call x0 -> x1, Pallas kernels: none -> 15.6 us  [surrogate_rows(): pl.pallas_call(mlp_kernel, grid=(rows // ROW_BLOCK,), in_specs=[pl.BlockS...]
    all_to_all x0 -> x1, starting transfers between devices: none -> 9.67 us  [on_device(): incoming = lax.all_to_all(outgoing, 'field', 0, 0, tiled=True)]
    broadcast_in_dim x0 -> x3, local copies, waits for them, and re-layouts: none -> 1.83 us  [the longest x1 0.67 us: on_device(): rate[:, None]]
    concatenate x1, other arithmetic: 1.6 us -> 0.21 us  [with_halo(): return jnp.concatenate([from_above, block, from_below], axis=1)]
    all_to_all x0 -> x1, local copies, waits for them, and re-layouts: none -> 1.34 us  [on_device(): incoming = lax.all_to_all(outgoing, 'field', 0, 0, tiled=True)]
  transfers between devices with their start and end apart: 2 -> 3, of which waited for: 2 -> 3; matrix products, arithmetic and copies ran while one was open for 0% -> 3% of each run, Pallas kernels for 0% -> 0%
where the time goes in v6:
time: 98.8 us; the launch traced here: 98.5 us
  waiting for transfers between devices  27.4 us (28%)
  starting transfers between devices  22.4 us (23%)
  Pallas kernels  18.1 us (18%)
  blocking collectives  16 us (16%)
  local copies, waits for them, and re-layouts  8.45 us (9%)
  other arithmetic  5.99 us (6%)
    all_to_all x1, waiting for transfers between devices, on_device(): incoming = lax.all_to_all(outgoing, 'field', 0, 0, tiled=True)  23.3 us
    all_to_all x1, blocking collectives, on_device(): lax.all_to_all(delta.transpose(1, 0, 2), 'field', 0, 0, tiled=True)  16 us
    pallas_call x1, Pallas kernels, surrogate_rows(): pl.pallas_call(mlp_kernel, grid=(rows // ROW_BLOCK,), in_specs=[pl.BlockS...  15.6 us
    all_to_all x1, starting transfers between devices, on_device(): incoming = lax.all_to_all(outgoing, 'field', 0, 0, tiled=True)  9.67 us
    ppermute x1, starting transfers between devices, with_halo(): lax.ppermute(head, axis, [(i + 1, i) for i in range(count - 1)])  8.47 us
    ppermute x1, starting transfers between devices, with_halo(): lax.ppermute(tail, axis, [(i, i + 1) for i in range(count - 1)])  4.28 us
    ppermute x1, waiting for transfers between devices, with_halo(): lax.ppermute(tail, axis, [(i, i + 1) for i in range(count - 1)])  2.86 us
    pallas_call x1, Pallas kernels, lookup(): pl.pallas_call(lookup_kernel, in_specs=[pl.BlockSpec(memory_space=pltpu.S...  2.43 us
  transfers between devices with their start and end apart: 3, of which 3 were waited for; matrix products, arithmetic and copies ran while one was open for 3% of the time, Pallas kernels for 0%

profile of v6, /device:TPU:8, one launch (start us, length us, event | category | flops | bytes accessed | tf_op | source)
XLA Modules:
  0.0 98.5 jit_solution(4459527400089815035)
XLA Ops:
  0.0 2.4 %shard_map.100 = f32[1,32,6144]{2,1,0:T(8,128)} custom-call(f32[1,8]{1,0:T(1,128)} %table_ref.1, s32[32,6144]{1,0:T(8,128)} %zone_ref.1), custom_call_target="tpu_custom_call" | custom-call | tf_op jit(solution)/shard_map/pallas_call | solution.py:47
  2.4 1.2 %pad_maximum_fusion.14 = (f32[2,3,6144]{2,1,0:T(4,128)S(1)}, f32[2,3,6144]{2,1,0:T(4,128)S(1)}) fusion(f32[1,32,6144]{2,1,0:T(8,128)} %shard_map.100, f32[1,32,6144]{2,1,0:T(8,128)S(1)} %copy-done.1), kind=kLoop, calls=%fused_computation.55 | loop fusion | flops 73728 | bytes 1867776 | tf_op jit(solution)/shard_map/slice | solution.py:61
  3.6 4.3 %collective-permute-start = (f32[2,3,6144]{2,1,0:T(4,128)S(1)}, f32[2,3,6144]{2,1,0:T(4,128)S(1)}, u32[]{:S(2)}, u32[]{:S(2)}) collective-permute-start(f32[2,3,6144]{2,1,0:T(4,128)S(1)} %get-tuple-element.15), channel_id=1, source_target_pairs={{0,16},{16,32},{32,48},{48,64},{64,80},{80,96},{96,112},{112,128},... | collective-permute-start | bytes 442376 | tf_op jit(solution)/shard_map/ppermute | solution.py:62
  7.9 8.5 %collective-permute-start.1 = (f32[2,3,6144]{2,1,0:T(4,128)S(1)}, f32[2,3,6144]{2,1,0:T(4,128)S(1)}, u32[]{:S(2)}, u32[]{:S(2)}) collective-permute-start(f32[2,3,6144]{2,1,0:T(4,128)S(1)} %get-tuple-element.16), channel_id=1, source_target_pairs={{16,0},{32,16},{48,32},{64,48},{80,64},{96,80},{112,96},{128,112},... | collective-permute-start | bytes 442376 | tf_op jit(solution)/shard_map/ppermute | solution.py:63
  16.5 2.9 %collective-permute-done = f32[2,3,6144]{2,1,0:T(4,128)S(1)} collective-permute-done((f32[2,3,6144]{2,1,0:T(4,128)S(1)}, f32[2,3,6144]{2,1,0:T(4,128)S(1)}, u32[]{:S(2)}, u32[]{:S(2)}) %collective-permute-start) | collective-permute-done | bytes 147488 | tf_op jit(solution)/shard_map/ppermute | solution.py:62
  19.3 1.2 %collective-permute-done.1 = f32[2,3,6144]{2,1,0:T(4,128)S(1)} collective-permute-done((f32[2,3,6144]{2,1,0:T(4,128)S(1)}, f32[2,3,6144]{2,1,0:T(4,128)S(1)}, u32[]{:S(2)}, u32[]{:S(2)}) %collective-permute-start.1) | collective-permute-done | bytes 147488 | tf_op jit(solution)/shard_map/ppermute | solution.py:63
  20.7 0.7 fusion.29
  21.5 0.7 add_add_fusion
  22.2 0.8 fusion.24
  23.4 0.8 fusion.23
  24.7 0.7 fusion.22
  26.0 1.1 %copy.23 = f32[32,16,384]{2,0,1:T(8,128)} copy(f32[32,16,384]{2,1,0:T(8,128)S(1)} %bitcast.17) | data formatting | bytes 1572864 | tf_op jit(solution)/shard_map/reshape;squeeze | solution.py:127
  27.1 9.7 %all-to-all-start = ((f32[16,32,384]{2,1,0:T(8,128)}), f32[16,32,384]{2,1,0:T(8,128)S(1)}, u32[]{:S(2)}, u32[]{:S(2)}) async-start(f32[16,32,384]{2,1,0:T(8,128)} %bitcast.14), calls=%async_computation | async-start | bytes 1572864 | tf_op jit(solution)/shard_map/all_to_all | solution.py:128
  36.8 0.7 copy.15.w_in_ref
  37.6 0.7 copy.16.rate_ref
  38.3 0.6 broadcast_in_dim.34.b_in_ref
  38.9 0.6 broadcast_in_dim.35.b_mid_ref
  39.5 23.3 %all-to-all-done = f32[16,32,384]{2,1,0:T(8,128)S(1)} async-done(((f32[16,32,384]{2,1,0:T(8,128)}), f32[16,32,384]{2,1,0:T(8,128)S(1)}, u32[]{:S(2)}, u32[]{:S(2)}) %all-to-all-start) | async-done | bytes 786464 | tf_op jit(solution)/shard_map/all_to_all | solution.py:128
  62.8 1.3 %copy.22 = f32[16,32,384]{2,0,1:T(8,128)} copy(f32[16,32,384]{2,1,0:T(8,128)S(1)} %all-to-all-done) | data formatting | bytes 1572864 | tf_op jit(solution)/shard_map/all_to_all | solution.py:128
  64.1 15.6 %shard_map.101 = bf16[32,16,384]{2,1,0:T(8,128)(2,1)} custom-call(f32[32,16,384]{2,1,0:T(8,128)} %bitcast.16, bf16[384,16]{1,0:T(8,128)(2,1)} %copy.15.w_in_ref, f32[1,384]{1,0:T(1,128)} %broadcast_in_dim.34.b_in_ref, bf16[384,384]{1,0:T(8,128)(2,1)} %w_mid_ref.1, f32[1,384]{1,0:T(1,128)} %broadcast_in_dim.35.b_mid_ref, bf16[16,384]{1,0:T(8,128)(2,1)} %w_out_ref.1, ...), custom_call_target="tpu_custom_call" | custom-call | tf_op jit(solution)/shard_map/pallas_call | solution.py:89
  79.8 1.1 %copy.17 = bf16[16,32,384]{2,1,0:T(8,128)(2,1)S(1)} copy(bf16[16,32,384]{2,0,1:T(8,128)(2,1)} %bitcast.18) | data formatting | bytes 786432 | tf_op jit(solution)/shard_map/transpose | solution.py:140
  80.8 16.0 %all_to_all.10 = bf16[16,32,384]{2,1,0:T(8,128)(2,1)S(1)} all-to-all(bf16[16,32,384]{2,1,0:T(8,128)(2,1)S(1)} %copy.17), channel_id=1, replica_groups=mesh['space'=32,'field'=16] {'field'}, dimensions={0} | all-to-all | bytes 786432 | tf_op jit(solution)/shard_map/all_to_all | solution.py:140
  96.9 0.5 copy.18
  97.5 1.0 add.85
  (25 shorter events, 2.1 us)
Async XLA Ops:
  0.0 2.4 %copy-start.1 = (f32[1,32,6144]{2,1,0:T(8,128)S(1)}, f32[1,32,6144]{2,1,0:T(8,128)}, u32[]{:S(2)}) copy-start(f32[1,32,6144]{2,1,0:T(8,128)} %param.10) | copy-start | bytes 2359300
  2.4 18.1 %copy-start = (f32[1,32,6144]{2,1,0:T(8,128)S(1)}, f32[1,32,6144]{2,1,0:T(8,128)}, u32[]{:S(2)}) copy-start(f32[1,32,6144]{2,1,0:T(8,128)} %shard_map.100) | copy-start | bytes 2359300
  3.6 15.7 %collective-permute-start = (f32[2,3,6144]{2,1,0:T(4,128)S(1)}, f32[2,3,6144]{2,1,0:T(4,128)S(1)}, u32[]{:S(2)}, u32[]{:S(2)}) collective-permute-start(f32[2,3,6144]{2,1,0:T(4,128)S(1)} %get-tuple-element.15), channel_id=1, source_target_pairs={{0,16},{16,32},{32,48},{48,64},{64,80},{80,96},{96,112},{112,128},... | collective-permute-start | bytes 442376 | tf_op jit(solution)/shard_map/ppermute | solution.py:62
  7.9 12.6 %collective-permute-start.1 = (f32[2,3,6144]{2,1,0:T(4,128)S(1)}, f32[2,3,6144]{2,1,0:T(4,128)S(1)}, u32[]{:S(2)}, u32[]{:S(2)}) collective-permute-start(f32[2,3,6144]{2,1,0:T(4,128)S(1)} %get-tuple-element.16), channel_id=1, source_target_pairs={{16,0},{32,16},{48,32},{64,48},{80,64},{96,80},{112,96},{128,112},... | collective-permute-start | bytes 442376 | tf_op jit(solution)/shard_map/ppermute | solution.py:63
  26.0 10.8 %copy-start.2 = (bf16[384,16]{0,1:T(8,128)(2,1)S(1)}, bf16[384,16]{0,1:T(8,128)(2,1)}, u32[]{:S(2)}) copy-start(bf16[384,16]{0,1:T(8,128)(2,1)} %param.14) | copy-start | bytes 36868
  26.0 11.6 %copy-start.5 = (f32[15]{0:T(128)S(1)}, f32[15]{0:T(128)}, u32[]{:S(2)}) copy-start(f32[15]{0:T(128)} %param.13) | copy-start | bytes 184
  26.0 12.3 %copy-start.3 = (f32[384]{0:T(512)S(1)}, f32[384]{0:T(512)}, u32[]{:S(2)}) copy-start(f32[384]{0:T(512)} %param.15) | copy-start | bytes 4612
  26.0 12.9 %copy-start.4 = (f32[384]{0:T(512)S(1)}, f32[384]{0:T(512)}, u32[]{:S(2)}) copy-start(f32[384]{0:T(512)} %param.17) | copy-start | bytes 4612
  27.1 35.7 %all-to-all-start = ((f32[16,32,384]{2,1,0:T(8,128)}), f32[16,32,384]{2,1,0:T(8,128)S(1)}, u32[]{:S(2)}, u32[]{:S(2)}) async-start(f32[16,32,384]{2,1,0:T(8,128)} %bitcast.14), calls=%async_computation | async-start | bytes 1572864 | tf_op jit(solution)/shard_map/all_to_all | solution.py:128

commit v7 on v6

--- a/solution.py
+++ b/solution.py
@@ -10,6 +10,7 @@
 HALO = SWEEPS
 CHUNK = 384
 ROW_BLOCK = 8
+GROUPS = 2
 NT = (((1,), (1,)), ((), ()))
 
 RELAX_WEIGHTS = (0.8, 1.25, 0.95)
@@ -124,22 +125,27 @@
     state = state[:, HALO : HALO + rows_here]
 
     chunks = columns // CHUNK
-    outgoing = state[0].reshape(rows_here, chunks, CHUNK).transpose(1, 0, 2)
-    incoming = lax.all_to_all(outgoing, "field", 0, 0, tiled=True)
     rate = jnp.concatenate([heat_rate, jnp.zeros((FIELDS - heat_rate.shape[0],), jnp.float32)])
-    delta = surrogate_rows(
-        incoming.transpose(1, 0, 2),
-        weight_in,
-        bias_in[None],
-        weight_mid,
-        bias_mid[None],
-        weight_out,
-        bias_out[None],
-        rate[:, None],
-    )
-    returned = lax.all_to_all(delta.transpose(1, 0, 2), "field", 0, 0, tiled=True)
-    returned = returned.transpose(1, 0, 2).reshape(1, rows_here, columns)
-    return state + returned.astype(jnp.float32)
+    group = rows_here // GROUPS
+    pieces = []
+    for number in range(GROUPS):
+        part = state[0, number * group : (number + 1) * group]
+        outgoing = part.reshape(group, chunks, CHUNK).transpose(1, 0, 2)
+        incoming = lax.all_to_all(outgoing, "field", 0, 0, tiled=True)
+        delta = surrogate_rows(
+            incoming.transpose(1, 0, 2),
+            weight_in,
+            bias_in[None],
+            weight_mid,
+            bias_mid[None],
+            weight_out,
+            bias_out[None],
+            rate[:, None],
+        )
+        returned = lax.all_to_all(delta.transpose(1, 0, 2), "field", 0, 0, tiled=True)
+        returned = returned.transpose(1, 0, 2).reshape(group, columns)
+        pieces.append(part + returned.astype(jnp.float32))
+    return jnp.concatenate(pieces, 0)[None]
 
 
 def solution(mesh):

time: 98.8 us -> 117 us (1.18)
  starting transfers between devices: 22.4 us -> 45.1 us
  blocking collectives: 16 us -> 0 us
  waiting for transfers between devices: 27.4 us -> 32 us
  local copies, waits for them, and re-layouts: 8.45 us -> 11.3 us
  Pallas kernels: 18.1 us -> 19.8 us
  other arithmetic: 5.99 us -> 7.51 us
    all_to_all x0 -> x2, starting transfers between devices: none -> 19.1 us  [on_device(): lax.all_to_all(delta.transpose(1, 0, 2), 'field', 0, 0, tiled=True)]
    all_to_all x1 -> x0, blocking collectives: 16 us -> none  [on_device(): lax.all_to_all(delta.transpose(1, 0, 2), 'field', 0, 0, tiled=True)]
    all_to_all x0 -> x2, waiting for transfers between devices: none -> 11.3 us  [on_device(): lax.all_to_all(delta.transpose(1, 0, 2), 'field', 0, 0, tiled=True)]
    all_to_all x1 -> x2, waiting for transfers between devices: 23.3 us -> 16.6 us  [on_device(): incoming = lax.all_to_all(outgoing, 'field', 0, 0, tiled=True)]
    all_to_all x1 -> x2, starting transfers between devices: 9.67 us -> 13.2 us  [on_device(): incoming = lax.all_to_all(outgoing, 'field', 0, 0, tiled=True)]
    select_n x3, other arithmetic: 2.14 us -> 4.96 us  [on_device(): state = jnp.where(inside, state, jnp.float32(0.0))]
    transpose x1 -> x2, local copies, waits for them, and re-layouts: 1.07 us -> 3.3 us  [on_device(): delta.transpose(1, 0, 2)]
    pallas_call x1 -> x2, Pallas kernels: 15.6 us -> 17.4 us  [surrogate_rows(): pl.pallas_call(mlp_kernel, grid=(rows // ROW_BLOCK,), in_specs=[pl.BlockS...]
  transfers between devices with their start and end apart: 3 -> 6, of which waited for: 3 -> 5; matrix products, arithmetic and copies ran while one was open for 3% -> 8% of each run, Pallas kernels for 0% -> 15%
where the time goes in v7:
time: 117 us; the launch traced here: 116 us
  starting transfers between devices  45.1 us (39%)
  waiting for transfers between devices  32 us (27%)
  Pallas kernels  19.8 us (17%)
  local copies, waits for them, and re-layouts  11.3 us (10%)
  other arithmetic  7.51 us (6%)
    all_to_all x2, starting transfers between devices, on_device(): lax.all_to_all(delta.transpose(1, 0, 2), 'field', 0, 0, tiled=True)  19.1 us
    pallas_call x2, Pallas kernels, surrogate_rows(): pl.pallas_call(mlp_kernel, grid=(rows // ROW_BLOCK,), in_specs=[pl.BlockS...  17.4 us
    all_to_all x2, waiting for transfers between devices, on_device(): incoming = lax.all_to_all(outgoing, 'field', 0, 0, tiled=True)  16.6 us
    all_to_all x2, starting transfers between devices, on_device(): incoming = lax.all_to_all(outgoing, 'field', 0, 0, tiled=True)  13.2 us
    all_to_all x2, waiting for transfers between devices, on_device(): lax.all_to_all(delta.transpose(1, 0, 2), 'field', 0, 0, tiled=True)  11.3 us
    ppermute x1, starting transfers between devices, with_halo(): lax.ppermute(head, axis, [(i + 1, i) for i in range(count - 1)])  8.47 us
    select_n x3, other arithmetic, on_device(): state = jnp.where(inside, state, jnp.float32(0.0))  4.96 us
    ppermute x1, starting transfers between devices, with_halo(): lax.ppermute(tail, axis, [(i, i + 1) for i in range(count - 1)])  4.28 us
  transfers between devices with their start and end apart: 6, of which 5 were waited for; matrix products, arithmetic and copies ran while one was open for 8% of the time, Pallas kernels for 15%

profile of v7, /device:TPU:8, one launch (start us, length us, event | category | flops | bytes accessed | tf_op | source)
XLA Modules:
  0.0 115.9 jit_solution(3584464165450098247)
XLA Ops:
  0.0 2.4 %shard_map.100 = f32[1,32,6144]{2,1,0:T(8,128)} custom-call(f32[1,8]{1,0:T(1,128)} %table_ref.1, s32[32,6144]{1,0:T(8,128)} %zone_ref.1), custom_call_target="tpu_custom_call" | custom-call | tf_op jit(solution)/shard_map/pallas_call | solution.py:48
  2.4 1.2 %pad_maximum_fusion.14 = (f32[2,3,6144]{2,1,0:T(4,128)S(1)}, f32[2,3,6144]{2,1,0:T(4,128)S(1)}) fusion(f32[1,32,6144]{2,1,0:T(8,128)} %shard_map.100, f32[1,32,6144]{2,1,0:T(8,128)S(1)} %copy-done.1), kind=kLoop, calls=%fused_computation.62 | loop fusion | flops 73728 | bytes 1867776 | tf_op jit(solution)/shard_map/slice | solution.py:62
  3.6 4.3 %collective-permute-start = (f32[2,3,6144]{2,1,0:T(4,128)S(1)}, f32[2,3,6144]{2,1,0:T(4,128)S(1)}, u32[]{:S(2)}, u32[]{:S(2)}) collective-permute-start(f32[2,3,6144]{2,1,0:T(4,128)S(1)} %get-tuple-element.16), channel_id=1, source_target_pairs={{0,16},{16,32},{32,48},{48,64},{64,80},{80,96},{96,112},{112,128},... | collective-permute-start | bytes 442376 | tf_op jit(solution)/shard_map/ppermute | solution.py:63
  7.9 8.5 %collective-permute-start.1 = (f32[2,3,6144]{2,1,0:T(4,128)S(1)}, f32[2,3,6144]{2,1,0:T(4,128)S(1)}, u32[]{:S(2)}, u32[]{:S(2)}) collective-permute-start(f32[2,3,6144]{2,1,0:T(4,128)S(1)} %get-tuple-element.17), channel_id=1, source_target_pairs={{16,0},{32,16},{48,32},{64,48},{80,64},{96,80},{112,96},{128,112},... | collective-permute-start | bytes 442376 | tf_op jit(solution)/shard_map/ppermute | solution.py:64
  16.4 2.9 %collective-permute-done = f32[2,3,6144]{2,1,0:T(4,128)S(1)} collective-permute-done((f32[2,3,6144]{2,1,0:T(4,128)S(1)}, f32[2,3,6144]{2,1,0:T(4,128)S(1)}, u32[]{:S(2)}, u32[]{:S(2)}) %collective-permute-start) | collective-permute-done | bytes 147488 | tf_op jit(solution)/shard_map/ppermute | solution.py:63
  19.3 1.2 %collective-permute-done.1 = f32[2,3,6144]{2,1,0:T(4,128)S(1)} collective-permute-done((f32[2,3,6144]{2,1,0:T(4,128)S(1)}, f32[2,3,6144]{2,1,0:T(4,128)S(1)}, u32[]{:S(2)}, u32[]{:S(2)}) %collective-permute-start.1) | collective-permute-done | bytes 147488 | tf_op jit(solution)/shard_map/ppermute | solution.py:64
  21.5 2.8 %fusion.29 = (f32[1,38,6144]{2,1,0:T(8,128)S(1)}, f32[1,38,6144]{2,1,0:T(8,128)S(1)}, f32[1,38,6144]{2,1,0:T(8,128)S(1)}) fusion(f32[1,38,6144]{2,1,0:T(8,128)S(1)} %get-tuple-element.15, f32[1,38,6143]{2,1,0:T(8,128)S(1)} %get-tuple-element.12, f32[2,3,6144]{2,1,0:T(4,128)S(1)} %collective-permute-done.1, f32[1,32,6144]{2,1,0:T(8,128)S(1)} %copy-done, ...), kind=kLoop, calls=%fused_computation.50 | loop fusion | flops 9805824 | bytes 11206086 | tf_op jit(solution)/shard_map/jit(_where)/select_n | solution.py:124
  24.7 1.1 broadcast_select_fusion
  26.2 1.1 fusion.28
  27.5 0.9 copy.38
  28.4 9.7 %all-to-all-start = ((f32[16,16,384]{2,1,0:T(8,128)}), f32[16,16,384]{2,1,0:T(8,128)S(1)}, u32[]{:S(2)}, u32[]{:S(2)}) async-start(f32[16,16,384]{2,1,0:T(8,128)} %bitcast.36), calls=%async_computation | async-start | bytes 786432 | tf_op jit(solution)/shard_map/all_to_all | solution.py:134
  38.1 0.9 copy.36
  39.0 16.6 %all-to-all-done = f32[16,16,384]{2,1,0:T(8,128)S(1)} async-done(((f32[16,16,384]{2,1,0:T(8,128)}), f32[16,16,384]{2,1,0:T(8,128)S(1)}, u32[]{:S(2)}, u32[]{:S(2)}) %all-to-all-start) | async-done | bytes 393248 | tf_op jit(solution)/shard_map/all_to_all | solution.py:134
  55.6 3.6 %all-to-all-start.2 = ((f32[16,16,384]{2,1,0:T(8,128)}), f32[16,16,384]{2,1,0:T(8,128)S(1)}, u32[]{:S(2)}, u32[]{:S(2)}) async-start(f32[16,16,384]{2,1,0:T(8,128)} %bitcast.34), calls=%async_computation.2 | async-start | bytes 786432 | tf_op jit(solution)/shard_map/all_to_all | solution.py:134
  61.9 0.9 copy.37
  62.8 8.7 %shard_map.101 = bf16[16,16,384]{2,1,0:T(8,128)(2,1)} custom-call(f32[16,16,384]{2,1,0:T(8,128)} %bitcast.42, bf16[384,16]{1,0:T(8,128)(2,1)} %copy.17.w_in_ref, f32[1,384]{1,0:T(1,128)} %broadcast_in_dim.41.b_in_ref, bf16[384,384]{1,0:T(8,128)(2,1)} %w_mid_ref.3, f32[1,384]{1,0:T(1,128)} %broadcast_in_dim.42.b_mid_ref, bf16[16,384]{1,0:T(8,128)(2,1)} %w_out_ref.3, ...), custom_call_target="tpu_custom_call" | custom-call | tf_op jit(solution)/shard_map/pallas_call | solution.py:90
  71.5 1.7 %copy.19 = bf16[16,16,384]{2,1,0:T(8,128)(2,1)} copy(bf16[16,16,384]{2,0,1:T(8,128)(2,1)} %bitcast.46) | data formatting | bytes 393216 | tf_op jit(solution)/shard_map/transpose | solution.py:145
  73.1 9.6 %all-to-all-start.1 = ((bf16[16,16,384]{2,1,0:T(8,128)(2,1)}), bf16[16,16,384]{2,1,0:T(8,128)(2,1)S(1)}, u32[]{:S(2)}, u32[]{:S(2)}) async-start(bf16[16,16,384]{2,1,0:T(8,128)(2,1)} %copy.19), calls=%async_computation.1 | async-start | bytes 393216 | tf_op jit(solution)/shard_map/all_to_all | solution.py:145
  82.7 0.9 copy.35
  83.6 8.7 %shard_map.102 = bf16[16,16,384]{2,1,0:T(8,128)(2,1)} custom-call(f32[16,16,384]{2,1,0:T(8,128)} %bitcast.38, bf16[384,16]{1,0:T(8,128)(2,1)} %copy.17.w_in_ref, f32[1,384]{1,0:T(1,128)} %broadcast_in_dim.41.b_in_ref, bf16[384,384]{1,0:T(8,128)(2,1)} %w_mid_ref.3, f32[1,384]{1,0:T(1,128)} %broadcast_in_dim.42.b_mid_ref, bf16[16,384]{1,0:T(8,128)(2,1)} %w_out_ref.3, ...), custom_call_target="tpu_custom_call" | custom-call | tf_op jit(solution)/shard_map/pallas_call | solution.py:90
  92.3 1.6 %copy.25 = bf16[16,16,384]{2,1,0:T(8,128)(2,1)} copy(bf16[16,16,384]{2,0,1:T(8,128)(2,1)} %bitcast.45) | data formatting | bytes 393216 | tf_op jit(solution)/shard_map/transpose | solution.py:145
  94.0 9.6 %all-to-all-start.3 = ((bf16[16,16,384]{2,1,0:T(8,128)(2,1)}), bf16[16,16,384]{2,1,0:T(8,128)(2,1)S(1)}, u32[]{:S(2)}, u32[]{:S(2)}) async-start(bf16[16,16,384]{2,1,0:T(8,128)(2,1)} %copy.25), calls=%async_computation.3 | async-start | bytes 393216 | tf_op jit(solution)/shard_map/all_to_all | solution.py:145
  103.6 11.2 %all-to-all-done.3 = bf16[16,16,384]{2,1,0:T(8,128)(2,1)S(1)} async-done(((bf16[16,16,384]{2,1,0:T(8,128)(2,1)}), bf16[16,16,384]{2,1,0:T(8,128)(2,1)S(1)}, u32[]{:S(2)}, u32[]{:S(2)}) %all-to-all-start.3) | async-done | bytes 196640 | tf_op jit(solution)/shard_map/all_to_all | solution.py:145
  115.0 0.9 maximum_bitcast_fusion
  (35 shorter events, 5.0 us)
Async XLA Ops:
  0.0 2.4 %copy-start.1 = (f32[1,32,6144]{2,1,0:T(8,128)S(1)}, f32[1,32,6144]{2,1,0:T(8,128)}, u32[]{:S(2)}) copy-start(f32[1,32,6144]{2,1,0:T(8,128)} %param.10) | copy-start | bytes 2359300
  2.4 18.1 %copy-start = (f32[1,32,6144]{2,1,0:T(8,128)S(1)}, f32[1,32,6144]{2,1,0:T(8,128)}, u32[]{:S(2)}) copy-start(f32[1,32,6144]{2,1,0:T(8,128)} %shard_map.100) | copy-start | bytes 2359300
  3.6 15.7 %collective-permute-start = (f32[2,3,6144]{2,1,0:T(4,128)S(1)}, f32[2,3,6144]{2,1,0:T(4,128)S(1)}, u32[]{:S(2)}, u32[]{:S(2)}) collective-permute-start(f32[2,3,6144]{2,1,0:T(4,128)S(1)} %get-tuple-element.16), channel_id=1, source_target_pairs={{0,16},{16,32},{32,48},{48,64},{64,80},{80,96},{96,112},{112,128},... | collective-permute-start | bytes 442376 | tf_op jit(solution)/shard_map/ppermute | solution.py:63
  7.9 12.6 %collective-permute-start.1 = (f32[2,3,6144]{2,1,0:T(4,128)S(1)}, f32[2,3,6144]{2,1,0:T(4,128)S(1)}, u32[]{:S(2)}, u32[]{:S(2)}) collective-permute-start(f32[2,3,6144]{2,1,0:T(4,128)S(1)} %get-tuple-element.17), channel_id=1, source_target_pairs={{16,0},{32,16},{48,32},{64,48},{80,64},{96,80},{112,96},{128,112},... | collective-permute-start | bytes 442376 | tf_op jit(solution)/shard_map/ppermute | solution.py:64
  27.5 31.7 %copy-start.2 = (bf16[384,16]{0,1:T(8,128)(2,1)S(1)}, bf16[384,16]{0,1:T(8,128)(2,1)}, u32[]{:S(2)}) copy-start(bf16[384,16]{0,1:T(8,128)(2,1)} %param.14) | copy-start | bytes 36868
  27.5 32.5 %copy-start.5 = (f32[15]{0:T(128)S(1)}, f32[15]{0:T(128)}, u32[]{:S(2)}) copy-start(f32[15]{0:T(128)} %param.13) | copy-start | bytes 184
  27.5 33.2 %copy-start.3 = (f32[384]{0:T(512)S(1)}, f32[384]{0:T(512)}, u32[]{:S(2)}) copy-start(f32[384]{0:T(512)} %param.15) | copy-start | bytes 4612
  27.5 33.8 %copy-start.4 = (f32[384]{0:T(512)S(1)}, f32[384]{0:T(512)}, u32[]{:S(2)}) copy-start(f32[384]{0:T(512)} %param.17) | copy-start | bytes 4612
  28.4 27.2 %all-to-all-start = ((f32[16,16,384]{2,1,0:T(8,128)}), f32[16,16,384]{2,1,0:T(8,128)S(1)}, u32[]{:S(2)}, u32[]{:S(2)}) async-start(f32[16,16,384]{2,1,0:T(8,128)} %bitcast.36), calls=%async_computation | async-start | bytes 786432 | tf_op jit(solution)/shard_map/all_to_all | solution.py:134
  55.6 17.5 %all-to-all-start.2 = ((f32[16,16,384]{2,1,0:T(8,128)}), f32[16,16,384]{2,1,0:T(8,128)S(1)}, u32[]{:S(2)}, u32[]{:S(2)}) async-start(f32[16,16,384]{2,1,0:T(8,128)} %bitcast.34), calls=%async_computation.2 | async-start | bytes 786432 | tf_op jit(solution)/shard_map/all_to_all | solution.py:134
  73.1 20.8 %all-to-all-start.1 = ((bf16[16,16,384]{2,1,0:T(8,128)(2,1)}), bf16[16,16,384]{2,1,0:T(8,128)(2,1)S(1)}, u32[]{:S(2)}, u32[]{:S(2)}) async-start(bf16[16,16,384]{2,1,0:T(8,128)(2,1)} %copy.19), calls=%async_computation.1 | async-start | bytes 393216 | tf_op jit(solution)/shard_map/all_to_all | solution.py:145
  94.0 20.9 %all-to-all-start.3 = ((bf16[16,16,384]{2,1,0:T(8,128)(2,1)}), bf16[16,16,384]{2,1,0:T(8,128)(2,1)S(1)}, u32[]{:S(2)}, u32[]{:S(2)}) async-start(bf16[16,16,384]{2,1,0:T(8,128)(2,1)} %copy.25), calls=%async_computation.3 | async-start | bytes 393216 | tf_op jit(solution)/shard_map/all_to_all | solution.py:145

commit v8 on v6

--- a/solution.py
+++ b/solution.py
@@ -66,7 +66,7 @@
 
 def mlp_kernel(x_ref, w_in_ref, b_in_ref, w_mid_ref, b_mid_ref, w_out_ref, b_out_ref, rate_ref, o_ref):
     rows = x_ref.shape[0]
-    cells = jnp.concatenate([x_ref[r].T for r in range(rows)], axis=0)
+    cells = jnp.concatenate([x_ref[r].astype(jnp.float32).T for r in range(rows)], axis=0)
     inputs = cells.astype(jnp.bfloat16)
     hidden = jax.nn.silu(lax.dot_general(inputs, w_in_ref[...], NT, preferred_element_type=jnp.float32) + b_in_ref[...])
     hidden = hidden.astype(jnp.bfloat16)
@@ -124,7 +124,7 @@
     state = state[:, HALO : HALO + rows_here]
 
     chunks = columns // CHUNK
-    outgoing = state[0].reshape(rows_here, chunks, CHUNK).transpose(1, 0, 2)
+    outgoing = state[0].reshape(rows_here, chunks, CHUNK).transpose(1, 0, 2).astype(jnp.bfloat16)
     incoming = lax.all_to_all(outgoing, "field", 0, 0, tiled=True)
     rate = jnp.concatenate([heat_rate, jnp.zeros((FIELDS - heat_rate.shape[0],), jnp.float32)])
     delta = surrogate_rows(

time: 98.8 us -> 88.8 us (0.90)
  waiting for transfers between devices: 27.4 us -> 19 us
  Pallas kernels: 18.1 us -> 16.9 us
    all_to_all x1, waiting for transfers between devices: 23.3 us -> 14.9 us  [on_device(): incoming = lax.all_to_all(outgoing, 'field', 0, 0, tiled=True)]
    pallas_call x1, Pallas kernels: 15.6 us -> 14.5 us  [surrogate_rows(): pl.pallas_call(mlp_kernel, grid=(rows // ROW_BLOCK,), in_specs=[pl.BlockS...]
    another operation x1 -> x0, local copies, waits for them, and re-layouts: 1.12 us -> none  [on_device(): outgoing = state[0].reshape(rows_here, chunks, CHUNK).transpose(1, 0, 2)]
    select_n x3 -> x2, other arithmetic: 2.14 us -> 1.69 us  [on_device(): state = jnp.where(inside, state, jnp.float32(0.0))]
where the time goes in v8:
time: 88.8 us; the launch traced here: 88.3 us
  starting transfers between devices  22.4 us (25%)
  waiting for transfers between devices  19 us (21%)
  Pallas kernels  16.9 us (19%)
  blocking collectives  16.3 us (18%)
  local copies, waits for them, and re-layouts  7.6 us (9%)
  other arithmetic  6 us (7%)
    all_to_all x1, blocking collectives, on_device(): lax.all_to_all(delta.transpose(1, 0, 2), 'field', 0, 0, tiled=True)  16.3 us
    all_to_all x1, waiting for transfers between devices, on_device(): incoming = lax.all_to_all(outgoing, 'field', 0, 0, tiled=True)  14.9 us
    pallas_call x1, Pallas kernels, surrogate_rows(): pl.pallas_call(mlp_kernel, grid=(rows // ROW_BLOCK,), in_specs=[pl.BlockS...  14.5 us
    all_to_all x1, starting transfers between devices, on_device(): incoming = lax.all_to_all(outgoing, 'field', 0, 0, tiled=True)  9.67 us
    ppermute x1, starting transfers between devices, with_halo(): lax.ppermute(head, axis, [(i + 1, i) for i in range(count - 1)])  8.47 us
    ppermute x1, starting transfers between devices, with_halo(): lax.ppermute(tail, axis, [(i, i + 1) for i in range(count - 1)])  4.28 us
    ppermute x1, waiting for transfers between devices, with_halo(): lax.ppermute(tail, axis, [(i, i + 1) for i in range(count - 1)])  2.86 us
    pallas_call x1, Pallas kernels, lookup(): pl.pallas_call(lookup_kernel, in_specs=[pl.BlockSpec(memory_space=pltpu.S...  2.43 us
  transfers between devices with their start and end apart: 3, of which 3 were waited for; matrix products, arithmetic and copies ran while one was open for 3% of the time, Pallas kernels for 0%

profile of v8, /device:TPU:8, one launch (start us, length us, event | category | flops | bytes accessed | tf_op | source)
XLA Modules:
  0.0 88.3 jit_solution(1169418478990339554)
XLA Ops:
  0.0 2.4 %shard_map.100 = f32[1,32,6144]{2,1,0:T(8,128)} custom-call(f32[1,8]{1,0:T(1,128)} %table_ref.1, s32[32,6144]{1,0:T(8,128)} %zone_ref.1), custom_call_target="tpu_custom_call" | custom-call | tf_op jit(solution)/shard_map/pallas_call | solution.py:47
  2.4 1.2 %pad_maximum_fusion.14 = (f32[2,3,6144]{2,1,0:T(4,128)S(1)}, f32[2,3,6144]{2,1,0:T(4,128)S(1)}) fusion(f32[1,32,6144]{2,1,0:T(8,128)} %shard_map.100, f32[1,32,6144]{2,1,0:T(8,128)S(1)} %copy-done.1), kind=kLoop, calls=%fused_computation.55 | loop fusion | flops 73728 | bytes 1867776 | tf_op jit(solution)/shard_map/slice | solution.py:61
  3.6 4.3 %collective-permute-start = (f32[2,3,6144]{2,1,0:T(4,128)S(1)}, f32[2,3,6144]{2,1,0:T(4,128)S(1)}, u32[]{:S(2)}, u32[]{:S(2)}) collective-permute-start(f32[2,3,6144]{2,1,0:T(4,128)S(1)} %get-tuple-element.17), channel_id=1, source_target_pairs={{0,16},{16,32},{32,48},{48,64},{64,80},{80,96},{96,112},{112,128},... | collective-permute-start | bytes 442376 | tf_op jit(solution)/shard_map/ppermute | solution.py:62
  7.9 8.5 %collective-permute-start.1 = (f32[2,3,6144]{2,1,0:T(4,128)S(1)}, f32[2,3,6144]{2,1,0:T(4,128)S(1)}, u32[]{:S(2)}, u32[]{:S(2)}) collective-permute-start(f32[2,3,6144]{2,1,0:T(4,128)S(1)} %get-tuple-element.18), channel_id=1, source_target_pairs={{16,0},{32,16},{48,32},{64,48},{80,64},{96,80},{112,96},{128,112},... | collective-permute-start | bytes 442376 | tf_op jit(solution)/shard_map/ppermute | solution.py:63
  16.5 2.9 %collective-permute-done = f32[2,3,6144]{2,1,0:T(4,128)S(1)} collective-permute-done((f32[2,3,6144]{2,1,0:T(4,128)S(1)}, f32[2,3,6144]{2,1,0:T(4,128)S(1)}, u32[]{:S(2)}, u32[]{:S(2)}) %collective-permute-start) | collective-permute-done | bytes 147488 | tf_op jit(solution)/shard_map/ppermute | solution.py:62
  19.3 1.2 %collective-permute-done.1 = f32[2,3,6144]{2,1,0:T(4,128)S(1)} collective-permute-done((f32[2,3,6144]{2,1,0:T(4,128)S(1)}, f32[2,3,6144]{2,1,0:T(4,128)S(1)}, u32[]{:S(2)}, u32[]{:S(2)}) %collective-permute-start.1) | collective-permute-done | bytes 147488 | tf_op jit(solution)/shard_map/ppermute | solution.py:63
  20.7 0.7 fusion.31
  21.5 0.7 add_add_fusion
  22.2 0.8 fusion.24
  23.4 0.8 fusion.23
  24.7 0.7 fusion.22
  25.9 0.8 copy.23
  26.8 9.7 %all-to-all-start = ((bf16[16,32,384]{2,1,0:T(8,128)(2,1)}), bf16[16,32,384]{2,1,0:T(8,128)(2,1)S(1)}, u32[]{:S(2)}, u32[]{:S(2)}) async-start(bf16[16,32,384]{2,1,0:T(8,128)(2,1)} %bitcast.14), calls=%async_computation | async-start | bytes 786432 | tf_op jit(solution)/shard_map/all_to_all | solution.py:128
  36.4 0.8 copy.15.w_in_ref
  37.3 0.7 copy.16.rate_ref
  37.9 0.6 broadcast_in_dim.34.b_in_ref
  38.5 0.6 broadcast_in_dim.35.b_mid_ref
  39.1 14.9 %all-to-all-done = bf16[16,32,384]{2,1,0:T(8,128)(2,1)S(1)} async-done(((bf16[16,32,384]{2,1,0:T(8,128)(2,1)}), bf16[16,32,384]{2,1,0:T(8,128)(2,1)S(1)}, u32[]{:S(2)}, u32[]{:S(2)}) %all-to-all-start) | async-done | bytes 393248 | tf_op jit(solution)/shard_map/all_to_all | solution.py:128
  54.0 0.9 copy.22
  54.9 14.5 %shard_map.101 = bf16[32,16,384]{2,1,0:T(8,128)(2,1)} custom-call(bf16[32,16,384]{2,1,0:T(8,128)(2,1)} %bitcast.15, bf16[384,16]{1,0:T(8,128)(2,1)} %copy.15.w_in_ref, f32[1,384]{1,0:T(1,128)} %broadcast_in_dim.34.b_in_ref, bf16[384,384]{1,0:T(8,128)(2,1)} %w_mid_ref.1, f32[1,384]{1,0:T(1,128)} %broadcast_in_dim.35.b_mid_ref, bf16[16,384]{1,0:T(8,128)(2,1)} %w_out_ref.1, ...), custom_call_target="tpu_custom_call" | custom-call | tf_op jit(solution)/shard_map/pallas_call | solution.py:89
  69.3 1.1 %copy.17 = bf16[16,32,384]{2,1,0:T(8,128)(2,1)S(1)} copy(bf16[16,32,384]{2,0,1:T(8,128)(2,1)} %bitcast.16) | data formatting | bytes 786432 | tf_op jit(solution)/shard_map/transpose | solution.py:140
  70.4 16.3 %all_to_all.10 = bf16[16,32,384]{2,1,0:T(8,128)(2,1)S(1)} all-to-all(bf16[16,32,384]{2,1,0:T(8,128)(2,1)S(1)} %copy.17), channel_id=1, replica_groups=mesh['space'=32,'field'=16] {'field'}, dimensions={0} | all-to-all | bytes 786432 | tf_op jit(solution)/shard_map/all_to_all | solution.py:140
  86.8 0.5 copy.18
  87.4 1.0 %add.85 = f32[1,32,6144]{2,1,0:T(8,128)} add(f32[1,32,6144]{2,1,0:T(8,128)S(1)} %get-tuple-element.6, f32[1,32,6144]{2,1,0:T(8,128)S(1)} %reshape.29) | non-fusion elementwise | flops 196608 | bytes 2359296 | tf_op jit(solution)/shard_map/add | solution.py:142
  (25 shorter events, 2.0 us)
Async XLA Ops:
  0.0 2.4 %copy-start.1 = (f32[1,32,6144]{2,1,0:T(8,128)S(1)}, f32[1,32,6144]{2,1,0:T(8,128)}, u32[]{:S(2)}) copy-start(f32[1,32,6144]{2,1,0:T(8,128)} %param.10) | copy-start | bytes 2359300
  2.4 18.1 %copy-start = (f32[1,32,6144]{2,1,0:T(8,128)S(1)}, f32[1,32,6144]{2,1,0:T(8,128)}, u32[]{:S(2)}) copy-start(f32[1,32,6144]{2,1,0:T(8,128)} %shard_map.100) | copy-start | bytes 2359300
  3.6 15.7 %collective-permute-start = (f32[2,3,6144]{2,1,0:T(4,128)S(1)}, f32[2,3,6144]{2,1,0:T(4,128)S(1)}, u32[]{:S(2)}, u32[]{:S(2)}) collective-permute-start(f32[2,3,6144]{2,1,0:T(4,128)S(1)} %get-tuple-element.17), channel_id=1, source_target_pairs={{0,16},{16,32},{32,48},{48,64},{64,80},{80,96},{96,112},{112,128},... | collective-permute-start | bytes 442376 | tf_op jit(solution)/shard_map/ppermute | solution.py:62
  7.9 12.6 %collective-permute-start.1 = (f32[2,3,6144]{2,1,0:T(4,128)S(1)}, f32[2,3,6144]{2,1,0:T(4,128)S(1)}, u32[]{:S(2)}, u32[]{:S(2)}) collective-permute-start(f32[2,3,6144]{2,1,0:T(4,128)S(1)} %get-tuple-element.18), channel_id=1, source_target_pairs={{16,0},{32,16},{48,32},{64,48},{80,64},{96,80},{112,96},{128,112},... | collective-permute-start | bytes 442376 | tf_op jit(solution)/shard_map/ppermute | solution.py:63
  25.8 10.6 %copy-start.2 = (bf16[384,16]{0,1:T(8,128)(2,1)S(1)}, bf16[384,16]{0,1:T(8,128)(2,1)}, u32[]{:S(2)}) copy-start(bf16[384,16]{0,1:T(8,128)(2,1)} %param.14) | copy-start | bytes 36868
  25.8 11.4 %copy-start.5 = (f32[15]{0:T(128)S(1)}, f32[15]{0:T(128)}, u32[]{:S(2)}) copy-start(f32[15]{0:T(128)} %param.13) | copy-start | bytes 184
  25.8 12.1 %copy-start.3 = (f32[384]{0:T(512)S(1)}, f32[384]{0:T(512)}, u32[]{:S(2)}) copy-start(f32[384]{0:T(512)} %param.15) | copy-start | bytes 4612
  25.9 12.7 %copy-start.4 = (f32[384]{0:T(512)S(1)}, f32[384]{0:T(512)}, u32[]{:S(2)}) copy-start(f32[384]{0:T(512)} %param.17) | copy-start | bytes 4612
  26.8 27.2 %all-to-all-start = ((bf16[16,32,384]{2,1,0:T(8,128)(2,1)}), bf16[16,32,384]{2,1,0:T(8,128)(2,1)S(1)}, u32[]{:S(2)}, u32[]{:S(2)}) async-start(bf16[16,32,384]{2,1,0:T(8,128)(2,1)} %bitcast.14), calls=%async_computation | async-start | bytes 786432 | tf_op jit(solution)/shard_map/all_to_all | solution.py:128

commit v9 on v8

--- a/solution.py
+++ b/solution.py
@@ -110,8 +110,23 @@
     bias_out,
 ):
     count_here, rows_here, columns = fields.shape
+    count = lax.axis_size("space")
+    where = lax.axis_index("space")
+    raw = jnp.concatenate([fields, zone_ids.astype(jnp.float32)[None]], 0)
+    from_above = lax.ppermute(raw[:, -HALO:], "space", [(i, i + 1) for i in range(count - 1)])
+    from_below = lax.ppermute(raw[:, :HALO], "space", [(i + 1, i) for i in range(count - 1)])
     coefs = lookup(zone_ids, diffusivity)
-    stacked = with_halo(jnp.concatenate([fields, coefs], 0), "space", HALO)
+    halo_coefs = lookup(jnp.concatenate([from_above[1], from_below[1]], 0).astype(jnp.int32), diffusivity)[0]
+    coef_above = jnp.where(where > 0, halo_coefs[:HALO], jnp.float32(0.0))
+    coef_below = jnp.where(where < count - 1, halo_coefs[HALO:], jnp.float32(0.0))
+    stacked = jnp.concatenate(
+        [
+            jnp.stack([from_above[0], coef_above]),
+            jnp.concatenate([fields, coefs], 0),
+            jnp.stack([from_below[0], coef_below]),
+        ],
+        axis=1,
+    )
     fields_ext = stacked[:count_here]
     coef_pad = pad_rows(stacked[count_here:])
     first_row = lax.axis_index("space") * rows_here - HALO

time: 88.8 us -> 91.8 us (1.034)
  other arithmetic: 6 us -> 9.63 us
  waiting for transfers between devices: 19 us -> 16.5 us
  Pallas kernels: 16.9 us -> 18.5 us
    ppermute x2, waiting for transfers between devices: 4.04 us -> 1.64 us  [the longest x1 1.14 us: on_device(): lax.ppermute(raw[:, :HALO], 'space', [(i + 1, i) for i in range(count - 1)])]
    pallas_call x1 -> x2, Pallas kernels: 2.43 us -> 4.05 us  [lookup(): pl.pallas_call(lookup_kernel, in_specs=[pl.BlockSpec(memory_space=pltpu.S...]
    broadcast_in_dim x0 -> x1, other arithmetic: none -> 1.26 us  [on_device(): raw = jnp.concatenate([fields, zone_ids.astype(jnp.float32)[None]], 0)]
    slice x1, other arithmetic: 1.16 us -> 0.08 us  [on_device(): raw[:, -HALO:]]
    select_n x0 -> x1, other arithmetic: none -> 1.07 us  [on_device(): coef_above = jnp.where(where > 0, halo_coefs[:HALO], jnp.float32(0.0))]
  transfers between devices with their start and end apart: 3 -> 3, of which waited for: 3 -> 3; matrix products, arithmetic and copies ran while one was open for 3% -> 3% of each run, Pallas kernels for 0% -> 3%
where the time goes in v9:
time: 91.8 us; the launch traced here: 91.4 us
  starting transfers between devices  22.4 us (24%)
  Pallas kernels  18.5 us (20%)
  waiting for transfers between devices  16.5 us (18%)
  blocking collectives  16.3 us (18%)
  other arithmetic  9.63 us (10%)
  local copies, waits for them, and re-layouts  7.79 us (8%)
    all_to_all x1, blocking collectives, on_device(): lax.all_to_all(delta.transpose(1, 0, 2), 'field', 0, 0, tiled=True)  16.3 us
    all_to_all x1, waiting for transfers between devices, on_device(): incoming = lax.all_to_all(outgoing, 'field', 0, 0, tiled=True)  14.9 us
    pallas_call x1, Pallas kernels, surrogate_rows(): pl.pallas_call(mlp_kernel, grid=(rows // ROW_BLOCK,), in_specs=[pl.BlockS...  14.4 us
    all_to_all x1, starting transfers between devices, on_device(): incoming = lax.all_to_all(outgoing, 'field', 0, 0, tiled=True)  9.67 us
    ppermute x1, starting transfers between devices, on_device(): lax.ppermute(raw[:, :HALO], 'space', [(i + 1, i) for i in range(count - 1)])  8.47 us
    ppermute x1, starting transfers between devices, on_device(): lax.ppermute(raw[:, -HALO:], 'space', [(i, i + 1) for i in range(count -...  4.28 us
    pallas_call x2, Pallas kernels, lookup(): pl.pallas_call(lookup_kernel, in_specs=[pl.BlockSpec(memory_space=pltpu.S...  4.05 us
    select_n x2, other arithmetic, on_device(): state = jnp.where(inside, state, jnp.float32(0.0))  2.55 us
  transfers between devices with their start and end apart: 3, of which 3 were waited for; matrix products, arithmetic and copies ran while one was open for 3% of the time, Pallas kernels for 3%

profile of v9, /device:TPU:8, one launch (start us, length us, event | category | flops | bytes accessed | tf_op | source)
XLA Modules:
  0.0 91.4 jit_solution(15077014336380103660)
XLA Ops:
  0.0 1.3 %convert_bitcast_fusion.1 = f32[1,32,6144]{2,1,0:T(8,128)S(1)} fusion(s32[32,6144]{1,0:T(8,128)} %zone_ref.1), kind=kLoop, calls=%fused_computation.60 | loop fusion | flops 196608 | bytes 1572864 | tf_op jit(solution)/shard_map/broadcast_in_dim | solution.py:115
  1.5 4.3 %collective-permute-start = (f32[2,3,6144]{2,1,0:T(4,128)S(1)}, f32[2,3,6144]{2,1,0:T(4,128)S(1)}, u32[]{:S(2)}, u32[]{:S(2)}) collective-permute-start(f32[2,3,6144]{2,1,0:T(4,128)S(1)} %get-tuple-element.17), channel_id=1, source_target_pairs={{0,16},{16,32},{32,48},{48,64},{64,80},{80,96},{96,112},{112,128},... | collective-permute-start | bytes 442376 | tf_op jit(solution)/shard_map/ppermute | solution.py:116
  5.7 8.5 %collective-permute-start.1 = (f32[2,3,6144]{2,1,0:T(4,128)S(1)}, f32[2,3,6144]{2,1,0:T(4,128)S(1)}, u32[]{:S(2)}, u32[]{:S(2)}) collective-permute-start(f32[2,3,6144]{2,1,0:T(4,128)S(1)} %get-tuple-element.18), channel_id=1, source_target_pairs={{16,0},{32,16},{48,32},{64,48},{80,64},{96,80},{112,96},{128,112},... | collective-permute-start | bytes 442376 | tf_op jit(solution)/shard_map/ppermute | solution.py:117
  14.2 2.4 %shard_map.101 = f32[1,32,6144]{2,1,0:T(8,128)} custom-call(f32[1,8]{1,0:T(1,128)} %table_ref.3, s32[32,6144]{1,0:T(8,128)} %zone_ref.1), custom_call_target="tpu_custom_call" | custom-call | tf_op jit(solution)/shard_map/pallas_call | solution.py:47
  17.2 1.1 %collective-permute-done.1 = f32[2,3,6144]{2,1,0:T(4,128)S(1)} collective-permute-done((f32[2,3,6144]{2,1,0:T(4,128)S(1)}, f32[2,3,6144]{2,1,0:T(4,128)S(1)}, u32[]{:S(2)}, u32[]{:S(2)}) %collective-permute-start.1) | collective-permute-done | bytes 147488 | tf_op jit(solution)/shard_map/ppermute | solution.py:117
  18.4 0.7 maximum_convert_fusion.zone_ref
  19.1 1.7 %shard_map.100 = f32[1,6,6144]{2,1,0:T(8,128)} custom-call(f32[1,8]{1,0:T(1,128)} %table_ref.3, s32[6,6144]{1,0:T(8,128)} %maximum_convert_fusion.zone_ref), custom_call_target="tpu_custom_call" | custom-call | tf_op jit(solution)/shard_map/pallas_call | solution.py:47
  20.8 1.1 %slice_select_fusion.1 = (f32[1,3,6144]{2,1,0:T(4,128)S(1)}, f32[1,3,6144]{2,1,0:T(4,128)S(1)}) fusion(f32[1,6,6144]{2,1,0:T(8,128)} %shard_map.100, pred[]{:T(512)S(6)} %gt.3, pred[]{:T(512)S(6)} %lt.16), kind=kLoop, calls=%fused_computation.67 | loop fusion | flops 36864 | bytes 294914 | tf_op jit(solution)/shard_map/jit(_where)/select_n | solution.py:120
  22.1 0.7 fusion.39
  22.9 1.5 %add_add_fusion = (f32[1,38,6144]{2,1,0:T(8,128)S(1)}, f32[1,38,6144]{2,1,0:T(8,128)S(1)}, f32[1,38,6144]{2,1,0:T(8,128)S(1)}, f32[1,38,6144]{2,1,0:T(8,128)S(1)...) fusion(f32[1,38,6144]{2,1,0:T(8,128)S(1)} %slice.179, f32[1,3,6144]{2,1,0:T(4,128)S(1)} %get-tuple-element.32, ...), kind=kLoop, calls=%fused_computation.48 | loop fusion | flops 5603328 | bytes 12140240 | tf_op jit(solution)/shard_map/add | solution.py:29
  24.4 1.7 %fusion.32 = f32[1,38,6144]{2,1,0:T(8,128)S(1)} fusion(f32[1,38,6144]{2,1,0:T(8,128)S(1)} %get-tuple-element.16, f32[1,38,6144]{2,1,0:T(8,128)S(1)} %get-tuple-element.11, f32[1,38,6143]{2,1,0:T(8,128)S(1)} %get-tuple-element.14, f32[1,3,6144]{2,1,0:T(4,128)S(1)} %get-tuple-element.32, f32[1,3,6144]{2,1,0:T(4,128)S(1)} %get-tuple-element.33, ...), kind=kLoop, calls=%fused_computation.52 | loop fusion | flops 7004160 | bytes 9338614 | tf_op jit(solution)/shard_map/jit(_where)/select_n | solution.py:138
  26.5 0.9 fusion.31
  27.7 0.7 fusion.30
  29.0 0.8 copy.23
  29.8 9.7 %all-to-all-start = ((bf16[16,32,384]{2,1,0:T(8,128)(2,1)}), bf16[16,32,384]{2,1,0:T(8,128)(2,1)S(1)}, u32[]{:S(2)}, u32[]{:S(2)}) async-start(bf16[16,32,384]{2,1,0:T(8,128)(2,1)} %bitcast.20), calls=%async_computation | async-start | bytes 786432 | tf_op jit(solution)/shard_map/all_to_all | solution.py:143
  39.5 0.7 copy.15.w_in_ref
  40.3 0.7 copy.16.rate_ref
  41.5 0.6 broadcast_in_dim.45.b_mid_ref
  42.1 14.9 %all-to-all-done = bf16[16,32,384]{2,1,0:T(8,128)(2,1)S(1)} async-done(((bf16[16,32,384]{2,1,0:T(8,128)(2,1)}), bf16[16,32,384]{2,1,0:T(8,128)(2,1)S(1)}, u32[]{:S(2)}, u32[]{:S(2)}) %all-to-all-start) | async-done | bytes 393248 | tf_op jit(solution)/shard_map/all_to_all | solution.py:143
  57.0 0.9 copy.22
  57.9 14.4 %shard_map.102 = bf16[32,16,384]{2,1,0:T(8,128)(2,1)} custom-call(bf16[32,16,384]{2,1,0:T(8,128)(2,1)} %bitcast.21, bf16[384,16]{1,0:T(8,128)(2,1)} %copy.15.w_in_ref, f32[1,384]{1,0:T(1,128)} %broadcast_in_dim.44.b_in_ref, bf16[384,384]{1,0:T(8,128)(2,1)} %w_mid_ref.1, f32[1,384]{1,0:T(1,128)} %broadcast_in_dim.45.b_mid_ref, bf16[16,384]{1,0:T(8,128)(2,1)} %w_out_ref.1, ...), custom_call_target="tpu_custom_call" | custom-call | tf_op jit(solution)/shard_map/pallas_call | solution.py:89
  72.4 1.1 %copy.17 = bf16[16,32,384]{2,1,0:T(8,128)(2,1)S(1)} copy(bf16[16,32,384]{2,0,1:T(8,128)(2,1)} %bitcast.22) | data formatting | bytes 786432 | tf_op jit(solution)/shard_map/transpose | solution.py:155
  73.4 16.3 %all_to_all.10 = bf16[16,32,384]{2,1,0:T(8,128)(2,1)S(1)} all-to-all(bf16[16,32,384]{2,1,0:T(8,128)(2,1)S(1)} %copy.17), channel_id=1, replica_groups=mesh['space'=32,'field'=16] {'field'}, dimensions={0} | all-to-all | bytes 786432 | tf_op jit(solution)/shard_map/all_to_all | solution.py:155
  90.4 1.0 %add.85 = f32[1,32,6144]{2,1,0:T(8,128)} add(f32[1,32,6144]{2,1,0:T(8,128)S(1)} %get-tuple-element.6, f32[1,32,6144]{2,1,0:T(8,128)S(1)} %reshape.31) | non-fusion elementwise | flops 196608 | bytes 2359296 | tf_op jit(solution)/shard_map/add | solution.py:157
  (31 shorter events, 3.8 us)
Async XLA Ops:
  0.0 1.4 %copy-start.1 = (f32[1,32,6144]{2,1,0:T(8,128)S(1)}, f32[1,32,6144]{2,1,0:T(8,128)}, u32[]{:S(2)}) copy-start(f32[1,32,6144]{2,1,0:T(8,128)} %param.10) | copy-start | bytes 2359300
  1.5 15.7 %collective-permute-start = (f32[2,3,6144]{2,1,0:T(4,128)S(1)}, f32[2,3,6144]{2,1,0:T(4,128)S(1)}, u32[]{:S(2)}, u32[]{:S(2)}) collective-permute-start(f32[2,3,6144]{2,1,0:T(4,128)S(1)} %get-tuple-element.17), channel_id=1, source_target_pairs={{0,16},{16,32},{32,48},{48,64},{64,80},{80,96},{96,112},{112,128},... | collective-permute-start | bytes 442376 | tf_op jit(solution)/shard_map/ppermute | solution.py:116
  5.7 12.6 %collective-permute-start.1 = (f32[2,3,6144]{2,1,0:T(4,128)S(1)}, f32[2,3,6144]{2,1,0:T(4,128)S(1)}, u32[]{:S(2)}, u32[]{:S(2)}) collective-permute-start(f32[2,3,6144]{2,1,0:T(4,128)S(1)} %get-tuple-element.18), channel_id=1, source_target_pairs={{16,0},{32,16},{48,32},{64,48},{80,64},{96,80},{112,96},{128,112},... | collective-permute-start | bytes 442376 | tf_op jit(solution)/shard_map/ppermute | solution.py:117
  16.6 5.3 %copy-start = (f32[1,32,6144]{2,1,0:T(8,128)S(1)}, f32[1,32,6144]{2,1,0:T(8,128)}, u32[]{:S(2)}) copy-start(f32[1,32,6144]{2,1,0:T(8,128)} %shard_map.101) | copy-start | bytes 2359300
  28.9 10.6 %copy-start.2 = (bf16[384,16]{0,1:T(8,128)(2,1)S(1)}, bf16[384,16]{0,1:T(8,128)(2,1)}, u32[]{:S(2)}) copy-start(bf16[384,16]{0,1:T(8,128)(2,1)} %param.14) | copy-start | bytes 36868
  28.9 11.3 %copy-start.5 = (f32[15]{0:T(128)S(1)}, f32[15]{0:T(128)}, u32[]{:S(2)}) copy-start(f32[15]{0:T(128)} %param.13) | copy-start | bytes 184
  28.9 12.1 %copy-start.3 = (f32[384]{0:T(512)S(1)}, f32[384]{0:T(512)}, u32[]{:S(2)}) copy-start(f32[384]{0:T(512)} %param.15) | copy-start | bytes 4612
  28.9 12.6 %copy-start.4 = (f32[384]{0:T(512)S(1)}, f32[384]{0:T(512)}, u32[]{:S(2)}) copy-start(f32[384]{0:T(512)} %param.17) | copy-start | bytes 4612
  29.8 27.2 %all-to-all-start = ((bf16[16,32,384]{2,1,0:T(8,128)(2,1)}), bf16[16,32,384]{2,1,0:T(8,128)(2,1)S(1)}, u32[]{:S(2)}, u32[]{:S(2)}) async-start(bf16[16,32,384]{2,1,0:T(8,128)(2,1)} %bitcast.20), calls=%async_computation | async-start | bytes 786432 | tf_op jit(solution)/shard_map/all_to_all | solution.py:143

commit v10 on v8

--- a/solution.py
+++ b/solution.py
@@ -57,10 +57,13 @@
 
 def with_halo(block, axis, width):
     count = lax.axis_size(axis)
+    where = lax.axis_index(axis)
     head = block[:, :width]
     tail = block[:, -width:]
-    from_above = lax.ppermute(tail, axis, [(i, i + 1) for i in range(count - 1)])
-    from_below = lax.ppermute(head, axis, [(i + 1, i) for i in range(count - 1)])
+    from_above = lax.ppermute(tail, axis, [(i, (i + 1) % count) for i in range(count)])
+    from_below = lax.ppermute(head, axis, [((i + 1) % count, i) for i in range(count)])
+    from_above = jnp.where(where > 0, from_above, jnp.zeros_like(from_above))
+    from_below = jnp.where(where < count - 1, from_below, jnp.zeros_like(from_below))
     return jnp.concatenate([from_above, block, from_below], axis=1)
 
 

time: 88.8 us -> 94.8 us (1.068)
  the two profiles are of different devices: /device:TPU:8 before, /device:TPU:1 now
where the time goes in v10:
time: 94.8 us; the launch traced here: 94.4 us
  starting transfers between devices  25.2 us (27%)
  waiting for transfers between devices  20.2 us (21%)
  blocking collectives  18.2 us (19%)
  Pallas kernels  16.9 us (18%)
  local copies, waits for them, and re-layouts  7.6 us (8%)
  other arithmetic  6.09 us (6%)
    all_to_all x1, blocking collectives, on_device(): lax.all_to_all(delta.transpose(1, 0, 2), 'field', 0, 0, tiled=True)  18.2 us
    ppermute x1, starting transfers between devices, with_halo(): lax.ppermute(head, axis, [((i + 1) % count, i) for i in range(count)])  14.5 us
    pallas_call x1, Pallas kernels, surrogate_rows(): pl.pallas_call(mlp_kernel, grid=(rows // ROW_BLOCK,), in_specs=[pl.BlockS...  14.4 us
    all_to_all x1, waiting for transfers between devices, on_device(): incoming = lax.all_to_all(outgoing, 'field', 0, 0, tiled=True)  11.1 us
    all_to_all x1, starting transfers between devices, on_device(): incoming = lax.all_to_all(outgoing, 'field', 0, 0, tiled=True)  8.74 us
    ppermute x1, waiting for transfers between devices, with_halo(): lax.ppermute(tail, axis, [(i, (i + 1) % count) for i in range(count)])  7.66 us
    pallas_call x1, Pallas kernels, lookup(): pl.pallas_call(lookup_kernel, in_specs=[pl.BlockSpec(memory_space=pltpu.S...  2.43 us
    ppermute x1, starting transfers between devices, with_halo(): lax.ppermute(tail, axis, [(i, (i + 1) % count) for i in range(count)])  1.92 us
  transfers between devices with their start and end apart: 3, of which 3 were waited for; matrix products, arithmetic and copies ran while one was open for 3% of the time, Pallas kernels for 0%

profile of v10, /device:TPU:1, one launch (start us, length us, event | category | flops | bytes accessed | tf_op | source)
XLA Modules:
  0.0 94.4 jit_solution(6008249525667733141)
XLA Ops:
  0.0 2.4 %shard_map.100 = f32[1,32,6144]{2,1,0:T(8,128)} custom-call(f32[1,8]{1,0:T(1,128)} %table_ref.1, s32[32,6144]{1,0:T(8,128)} %zone_ref.1), custom_call_target="tpu_custom_call" | custom-call | tf_op jit(solution)/shard_map/pallas_call | solution.py:47
  2.4 1.2 %pad_maximum_fusion.14 = (f32[2,3,6144]{2,1,0:T(4,128)S(1)}, f32[2,3,6144]{2,1,0:T(4,128)S(1)}) fusion(f32[1,32,6144]{2,1,0:T(8,128)} %shard_map.100, f32[1,32,6144]{2,1,0:T(8,128)S(1)} %copy-done.1), kind=kLoop, calls=%fused_computation.55 | loop fusion | flops 73728 | bytes 1867776 | tf_op jit(solution)/shard_map/slice | solution.py:62
  3.6 14.5 %collective-permute-start.1 = (f32[2,3,6144]{2,1,0:T(4,128)S(1)}, f32[2,3,6144]{2,1,0:T(4,128)S(1)}, u32[]{:S(2)}, u32[]{:S(2)}) collective-permute-start(f32[2,3,6144]{2,1,0:T(4,128)S(1)} %get-tuple-element.18), channel_id=1, source_target_pairs={{16,0},{32,16},{48,32},{64,48},{80,64},{96,80},{112,96},{128,112},... | collective-permute-start | bytes 442376 | tf_op jit(solution)/shard_map/ppermute | solution.py:64
  18.1 1.9 %collective-permute-start = (f32[2,3,6144]{2,1,0:T(4,128)S(1)}, f32[2,3,6144]{2,1,0:T(4,128)S(1)}, u32[]{:S(2)}, u32[]{:S(2)}) collective-permute-start(f32[2,3,6144]{2,1,0:T(4,128)S(1)} %get-tuple-element.17), channel_id=1, source_target_pairs={{0,16},{16,32},{32,48},{48,64},{64,80},{80,96},{96,112},{112,128},... | collective-permute-start | bytes 442376 | tf_op jit(solution)/shard_map/ppermute | solution.py:63
  20.2 1.5 %collective-permute-done.1 = f32[2,3,6144]{2,1,0:T(4,128)S(1)} collective-permute-done((f32[2,3,6144]{2,1,0:T(4,128)S(1)}, f32[2,3,6144]{2,1,0:T(4,128)S(1)}, u32[]{:S(2)}, u32[]{:S(2)}) %collective-permute-start.1) | collective-permute-done | bytes 147488 | tf_op jit(solution)/shard_map/ppermute | solution.py:64
  21.7 7.7 %collective-permute-done = f32[2,3,6144]{2,1,0:T(4,128)S(1)} collective-permute-done((f32[2,3,6144]{2,1,0:T(4,128)S(1)}, f32[2,3,6144]{2,1,0:T(4,128)S(1)}, u32[]{:S(2)}, u32[]{:S(2)}) %collective-permute-start) | collective-permute-done | bytes 147488 | tf_op jit(solution)/shard_map/ppermute | solution.py:63
  29.7 0.7 fusion.31
  30.4 0.7 add_add_fusion
  31.1 0.8 fusion.24
  32.4 0.8 fusion.23
  33.6 0.7 fusion.22
  34.9 0.8 copy.23
  35.7 8.7 %all-to-all-start = ((bf16[16,32,384]{2,1,0:T(8,128)(2,1)}), bf16[16,32,384]{2,1,0:T(8,128)(2,1)S(1)}, u32[]{:S(2)}, u32[]{:S(2)}) async-start(bf16[16,32,384]{2,1,0:T(8,128)(2,1)} %bitcast.14), calls=%async_computation | async-start | bytes 786432 | tf_op jit(solution)/shard_map/all_to_all | solution.py:131
  44.4 0.8 copy.15.w_in_ref
  45.3 0.7 copy.16.rate_ref
  46.0 0.6 broadcast_in_dim.34.b_in_ref
  46.5 0.6 broadcast_in_dim.35.b_mid_ref
  47.1 11.1 %all-to-all-done = bf16[16,32,384]{2,1,0:T(8,128)(2,1)S(1)} async-done(((bf16[16,32,384]{2,1,0:T(8,128)(2,1)}), bf16[16,32,384]{2,1,0:T(8,128)(2,1)S(1)}, u32[]{:S(2)}, u32[]{:S(2)}) %all-to-all-start) | async-done | bytes 393248 | tf_op jit(solution)/shard_map/all_to_all | solution.py:131
  58.2 0.9 copy.22
  59.0 14.4 %shard_map.101 = bf16[32,16,384]{2,1,0:T(8,128)(2,1)} custom-call(bf16[32,16,384]{2,1,0:T(8,128)(2,1)} %bitcast.15, bf16[384,16]{1,0:T(8,128)(2,1)} %copy.15.w_in_ref, f32[1,384]{1,0:T(1,128)} %broadcast_in_dim.34.b_in_ref, bf16[384,384]{1,0:T(8,128)(2,1)} %w_mid_ref.1, f32[1,384]{1,0:T(1,128)} %broadcast_in_dim.35.b_mid_ref, bf16[16,384]{1,0:T(8,128)(2,1)} %w_out_ref.1, ...), custom_call_target="tpu_custom_call" | custom-call | tf_op jit(solution)/shard_map/pallas_call | solution.py:92
  73.5 1.1 %copy.17 = bf16[16,32,384]{2,1,0:T(8,128)(2,1)S(1)} copy(bf16[16,32,384]{2,0,1:T(8,128)(2,1)} %bitcast.16) | data formatting | bytes 786432 | tf_op jit(solution)/shard_map/transpose | solution.py:143
  74.6 18.2 %all_to_all.10 = bf16[16,32,384]{2,1,0:T(8,128)(2,1)S(1)} all-to-all(bf16[16,32,384]{2,1,0:T(8,128)(2,1)S(1)} %copy.17), channel_id=1, replica_groups=mesh['space'=32,'field'=16] {'field'}, dimensions={0} | all-to-all | bytes 786432 | tf_op jit(solution)/shard_map/all_to_all | solution.py:143
  92.9 0.5 copy.18
  93.5 1.0 %add.85 = f32[1,32,6144]{2,1,0:T(8,128)} add(f32[1,32,6144]{2,1,0:T(8,128)S(1)} %get-tuple-element.6, f32[1,32,6144]{2,1,0:T(8,128)S(1)} %reshape.29) | non-fusion elementwise | flops 196608 | bytes 2359296 | tf_op jit(solution)/shard_map/add | solution.py:145
  (27 shorter events, 2.1 us)
Async XLA Ops:
  0.0 2.4 %copy-start.1 = (f32[1,32,6144]{2,1,0:T(8,128)S(1)}, f32[1,32,6144]{2,1,0:T(8,128)}, u32[]{:S(2)}) copy-start(f32[1,32,6144]{2,1,0:T(8,128)} %param.10) | copy-start | bytes 2359300
  2.4 27.0 %copy-start = (f32[1,32,6144]{2,1,0:T(8,128)S(1)}, f32[1,32,6144]{2,1,0:T(8,128)}, u32[]{:S(2)}) copy-start(f32[1,32,6144]{2,1,0:T(8,128)} %shard_map.100) | copy-start | bytes 2359300
  3.6 18.1 %collective-permute-start.1 = (f32[2,3,6144]{2,1,0:T(4,128)S(1)}, f32[2,3,6144]{2,1,0:T(4,128)S(1)}, u32[]{:S(2)}, u32[]{:S(2)}) collective-permute-start(f32[2,3,6144]{2,1,0:T(4,128)S(1)} %get-tuple-element.18), channel_id=1, source_target_pairs={{16,0},{32,16},{48,32},{64,48},{80,64},{96,80},{112,96},{128,112},... | collective-permute-start | bytes 442376 | tf_op jit(solution)/shard_map/ppermute | solution.py:64
  18.1 11.3 %collective-permute-start = (f32[2,3,6144]{2,1,0:T(4,128)S(1)}, f32[2,3,6144]{2,1,0:T(4,128)S(1)}, u32[]{:S(2)}, u32[]{:S(2)}) collective-permute-start(f32[2,3,6144]{2,1,0:T(4,128)S(1)} %get-tuple-element.17), channel_id=1, source_target_pairs={{0,16},{16,32},{32,48},{48,64},{64,80},{80,96},{96,112},{112,128},... | collective-permute-start | bytes 442376 | tf_op jit(solution)/shard_map/ppermute | solution.py:63
  34.8 9.7 %copy-start.2 = (bf16[384,16]{0,1:T(8,128)(2,1)S(1)}, bf16[384,16]{0,1:T(8,128)(2,1)}, u32[]{:S(2)}) copy-start(bf16[384,16]{0,1:T(8,128)(2,1)} %param.14) | copy-start | bytes 36868
  34.8 10.4 %copy-start.5 = (f32[15]{0:T(128)S(1)}, f32[15]{0:T(128)}, u32[]{:S(2)}) copy-start(f32[15]{0:T(128)} %param.13) | copy-start | bytes 184
  34.8 11.2 %copy-start.3 = (f32[384]{0:T(512)S(1)}, f32[384]{0:T(512)}, u32[]{:S(2)}) copy-start(f32[384]{0:T(512)} %param.15) | copy-start | bytes 4612
  34.8 11.7 %copy-start.4 = (f32[384]{0:T(512)S(1)}, f32[384]{0:T(512)}, u32[]{:S(2)}) copy-start(f32[384]{0:T(512)} %param.17) | copy-start | bytes 4612
  35.7 22.5 %all-to-all-start = ((bf16[16,32,384]{2,1,0:T(8,128)(2,1)}), bf16[16,32,384]{2,1,0:T(8,128)(2,1)S(1)}, u32[]{:S(2)}, u32[]{:S(2)}) async-start(bf16[16,32,384]{2,1,0:T(8,128)(2,1)} %bitcast.14), calls=%async_computation | async-start | bytes 786432 | tf_op jit(solution)/shard_map/all_to_all | solution.py:131

commit v11 on v8

--- a/solution.py
+++ b/solution.py
@@ -9,7 +9,7 @@
 SWEEPS = 3
 HALO = SWEEPS
 CHUNK = 384
-ROW_BLOCK = 8
+ROW_BLOCK = 32
 NT = (((1,), (1,)), ((), ()))
 
 RELAX_WEIGHTS = (0.8, 1.25, 0.95)
@@ -65,8 +65,9 @@
 
 
 def mlp_kernel(x_ref, w_in_ref, b_in_ref, w_mid_ref, b_mid_ref, w_out_ref, b_out_ref, rate_ref, o_ref):
-    rows = x_ref.shape[0]
-    cells = jnp.concatenate([x_ref[r].astype(jnp.float32).T for r in range(rows)], axis=0)
+    rows = x_ref.shape[1]
+    block = x_ref[...].astype(jnp.float32)
+    cells = jnp.concatenate([block[:, r, :].T for r in range(rows)], axis=0)
     inputs = cells.astype(jnp.bfloat16)
     hidden = jax.nn.silu(lax.dot_general(inputs, w_in_ref[...], NT, preferred_element_type=jnp.float32) + b_in_ref[...])
     hidden = hidden.astype(jnp.bfloat16)
@@ -79,21 +80,29 @@
     factor = jnp.exp(rate_ref[...] * jnp.tanh(heat))
     scaled = (change * factor).astype(jnp.bfloat16)
     is_heat = lax.broadcasted_iota(jnp.int32, change.shape, 0) == FIELDS - 1
-    out = jnp.where(is_heat, change.astype(jnp.bfloat16), scaled)
-    for r in range(rows):
-        o_ref[r] = out[:, r * CHUNK : (r + 1) * CHUNK]
+    out = jnp.where(is_heat, change.astype(jnp.bfloat16), scaled).astype(jnp.float32)
+    rows_out = [out[:, r * CHUNK : (r + 1) * CHUNK] for r in range(rows)]
+    o_ref[...] = jnp.stack(rows_out, axis=1).astype(jnp.bfloat16)
+
 
 def surrogate_rows(x, weight_in, bias_in, weight_mid, bias_mid, weight_out, bias_out, rate):
-    rows = x.shape[0]
+    rows = x.shape[1]
     full = lambda shape: pl.BlockSpec(shape, lambda i: (0,) * len(shape))
     return pl.pallas_call(
         mlp_kernel,
         grid=(rows // ROW_BLOCK,),
-        in_specs=[pl.BlockSpec((ROW_BLOCK, FIELDS, CHUNK), lambda i: (i, 0, 0)),
-                  full(weight_in.shape), full(bias_in.shape), full(weight_mid.shape), full(bias_mid.shape),
-                  full(weight_out.shape), full(bias_out.shape), full(rate.shape)],
-        out_specs=pl.BlockSpec((ROW_BLOCK, FIELDS, CHUNK), lambda i: (i, 0, 0)),
-        out_shape=jax.ShapeDtypeStruct((rows, FIELDS, CHUNK), jnp.bfloat16),
+        in_specs=[
+            pl.BlockSpec((FIELDS, ROW_BLOCK, CHUNK), lambda i: (0, i, 0)),
+            full(weight_in.shape),
+            full(bias_in.shape),
+            full(weight_mid.shape),
+            full(bias_mid.shape),
+            full(weight_out.shape),
+            full(bias_out.shape),
+            full(rate.shape),
+        ],
+        out_specs=pl.BlockSpec((FIELDS, ROW_BLOCK, CHUNK), lambda i: (0, i, 0)),
+        out_shape=jax.ShapeDtypeStruct(x.shape, jnp.bfloat16),
     )(x, weight_in, bias_in, weight_mid, bias_mid, weight_out, bias_out, rate)
 
 
@@ -128,7 +137,7 @@
     incoming = lax.all_to_all(outgoing, "field", 0, 0, tiled=True)
     rate = jnp.concatenate([heat_rate, jnp.zeros((FIELDS - heat_rate.shape[0],), jnp.float32)])
     delta = surrogate_rows(
-        incoming.transpose(1, 0, 2),
+        incoming,
         weight_in,
         bias_in[None],
         weight_mid,
@@ -137,7 +146,7 @@
         bias_out[None],
         rate[:, None],
     )
-    returned = lax.all_to_all(delta.transpose(1, 0, 2), "field", 0, 0, tiled=True)
+    returned = lax.all_to_all(delta, "field", 0, 0, tiled=True)
     returned = returned.transpose(1, 0, 2).reshape(1, rows_here, columns)
     return state + returned.astype(jnp.float32)
 

time: 88.8 us -> 89.1 us (level)
  local copies, waits for them, and re-layouts: 7.6 us -> 6.4 us
  blocking collectives: 16.3 us -> 17.2 us
    transpose x1 -> x0, local copies, waits for them, and re-layouts: 1.07 us -> none  [on_device(): delta.transpose(1, 0, 2)]
    all_to_all x1, blocking collectives: 16.3 us -> 17.2 us  [on_device(): returned = lax.all_to_all(delta, 'field', 0, 0, tiled=True)]
where the time goes in v11:
time: 89.1 us; the launch traced here: 88.6 us
  starting transfers between devices  22.6 us (25%)
  waiting for transfers between devices  18.8 us (21%)
  Pallas kernels  17.5 us (20%)
  blocking collectives  17.2 us (19%)
  local copies, waits for them, and re-layouts  6.4 us (7%)
  other arithmetic  6 us (7%)
    all_to_all x1, blocking collectives, on_device(): returned = lax.all_to_all(delta, 'field', 0, 0, tiled=True)  17.2 us
    pallas_call x1, Pallas kernels, surrogate_rows(): pl.pallas_call(mlp_kernel, grid=(rows // ROW_BLOCK,), in_specs=[pl.BlockS...  15.1 us
    all_to_all x1, waiting for transfers between devices, on_device(): incoming = lax.all_to_all(outgoing, 'field', 0, 0, tiled=True)  14.7 us
    all_to_all x1, starting transfers between devices, on_device(): incoming = lax.all_to_all(outgoing, 'field', 0, 0, tiled=True)  9.85 us
    ppermute x1, starting transfers between devices, with_halo(): lax.ppermute(head, axis, [(i + 1, i) for i in range(count - 1)])  8.47 us
    ppermute x1, starting transfers between devices, with_halo(): lax.ppermute(tail, axis, [(i, i + 1) for i in range(count - 1)])  4.28 us
    ppermute x1, waiting for transfers between devices, with_halo(): lax.ppermute(tail, axis, [(i, i + 1) for i in range(count - 1)])  2.86 us
    pallas_call x1, Pallas kernels, lookup(): pl.pallas_call(lookup_kernel, in_specs=[pl.BlockSpec(memory_space=pltpu.S...  2.43 us
  transfers between devices with their start and end apart: 3, of which 3 were waited for; matrix products, arithmetic and copies ran while one was open for 3% of the time, Pallas kernels for 0%

profile of v11, /device:TPU:8, one launch (start us, length us, event | category | flops | bytes accessed | tf_op | source)
XLA Modules:
  0.0 88.6 jit_solution(14789250619442522515)
XLA Ops:
  0.0 2.4 %shard_map.100 = f32[1,32,6144]{2,1,0:T(8,128)} custom-call(f32[1,8]{1,0:T(1,128)} %table_ref.1, s32[32,6144]{1,0:T(8,128)} %zone_ref.1), custom_call_target="tpu_custom_call" | custom-call | tf_op jit(solution)/shard_map/pallas_call | solution.py:47
  2.4 1.2 %pad_maximum_fusion.14 = (f32[2,3,6144]{2,1,0:T(4,128)S(1)}, f32[2,3,6144]{2,1,0:T(4,128)S(1)}) fusion(f32[1,32,6144]{2,1,0:T(8,128)} %shard_map.100, f32[1,32,6144]{2,1,0:T(8,128)S(1)} %copy-done.1), kind=kLoop, calls=%fused_computation.54 | loop fusion | flops 73728 | bytes 1867776 | tf_op jit(solution)/shard_map/slice | solution.py:61
  3.6 4.3 %collective-permute-start = (f32[2,3,6144]{2,1,0:T(4,128)S(1)}, f32[2,3,6144]{2,1,0:T(4,128)S(1)}, u32[]{:S(2)}, u32[]{:S(2)}) collective-permute-start(f32[2,3,6144]{2,1,0:T(4,128)S(1)} %get-tuple-element.17), channel_id=1, source_target_pairs={{0,16},{16,32},{32,48},{48,64},{64,80},{80,96},{96,112},{112,128},... | collective-permute-start | bytes 442376 | tf_op jit(solution)/shard_map/ppermute | solution.py:62
  7.9 8.5 %collective-permute-start.1 = (f32[2,3,6144]{2,1,0:T(4,128)S(1)}, f32[2,3,6144]{2,1,0:T(4,128)S(1)}, u32[]{:S(2)}, u32[]{:S(2)}) collective-permute-start(f32[2,3,6144]{2,1,0:T(4,128)S(1)} %get-tuple-element.18), channel_id=1, source_target_pairs={{16,0},{32,16},{48,32},{64,48},{80,64},{96,80},{112,96},{128,112},... | collective-permute-start | bytes 442376 | tf_op jit(solution)/shard_map/ppermute | solution.py:63
  16.5 2.9 %collective-permute-done = f32[2,3,6144]{2,1,0:T(4,128)S(1)} collective-permute-done((f32[2,3,6144]{2,1,0:T(4,128)S(1)}, f32[2,3,6144]{2,1,0:T(4,128)S(1)}, u32[]{:S(2)}, u32[]{:S(2)}) %collective-permute-start) | collective-permute-done | bytes 147488 | tf_op jit(solution)/shard_map/ppermute | solution.py:62
  19.3 1.2 %collective-permute-done.1 = f32[2,3,6144]{2,1,0:T(4,128)S(1)} collective-permute-done((f32[2,3,6144]{2,1,0:T(4,128)S(1)}, f32[2,3,6144]{2,1,0:T(4,128)S(1)}, u32[]{:S(2)}, u32[]{:S(2)}) %collective-permute-start.1) | collective-permute-done | bytes 147488 | tf_op jit(solution)/shard_map/ppermute | solution.py:63
  20.7 0.7 fusion.31
  21.5 0.7 add_add_fusion
  22.2 0.8 fusion.24
  23.4 0.8 fusion.23
  24.7 0.7 fusion.22
  25.4 0.5 fusion.27
  25.9 0.8 copy.19
  26.8 9.8 %all-to-all-start = ((bf16[16,32,384]{2,1,0:T(8,128)(2,1)}), bf16[16,32,384]{2,1,0:T(8,128)(2,1)S(1)}, u32[]{:S(2)}, u32[]{:S(2)}) async-start(bf16[16,32,384]{2,1,0:T(8,128)(2,1)} %bitcast.10), calls=%async_computation | async-start | bytes 786432 | tf_op jit(solution)/shard_map/all_to_all | solution.py:137
  36.6 0.7 copy.14.w_in_ref
  37.4 0.7 copy.15.rate_ref
  38.1 0.6 broadcast_in_dim.34.b_in_ref
  38.7 0.6 broadcast_in_dim.35.b_mid_ref
  39.3 14.7 %all-to-all-done.x_ref = bf16[16,32,384]{2,1,0:T(8,128)(2,1)S(1)} async-done(((bf16[16,32,384]{2,1,0:T(8,128)(2,1)}), bf16[16,32,384]{2,1,0:T(8,128)(2,1)S(1)}, u32[]{:S(2)}, u32[]{:S(2)}) %all-to-all-start) | async-done | bytes 393248 | tf_op jit(solution)/shard_map/all_to_all | solution.py:137
  54.0 0.7 copy-done.2
  54.7 15.1 %shard_map.101 = bf16[16,32,384]{2,1,0:T(8,128)(2,1)} custom-call(bf16[16,32,384]{2,1,0:T(8,128)(2,1)} %copy-done.2, bf16[384,16]{1,0:T(8,128)(2,1)} %copy.14.w_in_ref, f32[1,384]{1,0:T(1,128)} %broadcast_in_dim.34.b_in_ref, bf16[384,384]{1,0:T(8,128)(2,1)} %w_mid_ref.1, f32[1,384]{1,0:T(1,128)} %broadcast_in_dim.35.b_mid_ref, bf16[16,384]{1,0:T(8,128)(2,1)} %w_out_ref.1, ...), custom_call_target="tpu_custom_call" | custom-call | tf_op jit(solution)/shard_map/pallas_call | solution.py:91
  69.8 17.2 %all_to_all.10 = bf16[16,32,384]{2,1,0:T(8,128)(2,1)S(1)} all-to-all(bf16[16,32,384]{2,1,0:T(8,128)(2,1)} %shard_map.101), channel_id=1, replica_groups=mesh['space'=32,'field'=16] {'field'}, dimensions={0} | all-to-all | bytes 786432 | tf_op jit(solution)/shard_map/all_to_all | solution.py:149
  87.1 0.5 copy.16
  87.7 1.0 %add.85 = f32[1,32,6144]{2,1,0:T(8,128)} add(f32[1,32,6144]{2,1,0:T(8,128)S(1)} %get-tuple-element.6, f32[1,32,6144]{2,1,0:T(8,128)S(1)} %reshape.29) | non-fusion elementwise | flops 196608 | bytes 2359296 | tf_op jit(solution)/shard_map/add | solution.py:151
  (25 shorter events, 1.5 us)
Async XLA Ops:
  0.0 2.4 %copy-start.1 = (f32[1,32,6144]{2,1,0:T(8,128)S(1)}, f32[1,32,6144]{2,1,0:T(8,128)}, u32[]{:S(2)}) copy-start(f32[1,32,6144]{2,1,0:T(8,128)} %param.10) | copy-start | bytes 2359300
  2.4 18.1 %copy-start = (f32[1,32,6144]{2,1,0:T(8,128)S(1)}, f32[1,32,6144]{2,1,0:T(8,128)}, u32[]{:S(2)}) copy-start(f32[1,32,6144]{2,1,0:T(8,128)} %shard_map.100) | copy-start | bytes 2359300
  3.6 15.7 %collective-permute-start = (f32[2,3,6144]{2,1,0:T(4,128)S(1)}, f32[2,3,6144]{2,1,0:T(4,128)S(1)}, u32[]{:S(2)}, u32[]{:S(2)}) collective-permute-start(f32[2,3,6144]{2,1,0:T(4,128)S(1)} %get-tuple-element.17), channel_id=1, source_target_pairs={{0,16},{16,32},{32,48},{48,64},{64,80},{80,96},{96,112},{112,128},... | collective-permute-start | bytes 442376 | tf_op jit(solution)/shard_map/ppermute | solution.py:62
  7.9 12.6 %collective-permute-start.1 = (f32[2,3,6144]{2,1,0:T(4,128)S(1)}, f32[2,3,6144]{2,1,0:T(4,128)S(1)}, u32[]{:S(2)}, u32[]{:S(2)}) collective-permute-start(f32[2,3,6144]{2,1,0:T(4,128)S(1)} %get-tuple-element.18), channel_id=1, source_target_pairs={{16,0},{32,16},{48,32},{64,48},{80,64},{96,80},{112,96},{128,112},... | collective-permute-start | bytes 442376 | tf_op jit(solution)/shard_map/ppermute | solution.py:63
  25.8 10.8 %copy-start.3 = (bf16[384,16]{0,1:T(8,128)(2,1)S(1)}, bf16[384,16]{0,1:T(8,128)(2,1)}, u32[]{:S(2)}) copy-start(bf16[384,16]{0,1:T(8,128)(2,1)} %param.14) | copy-start | bytes 36868
  25.8 11.5 %copy-start.6 = (f32[15]{0:T(128)S(1)}, f32[15]{0:T(128)}, u32[]{:S(2)}) copy-start(f32[15]{0:T(128)} %param.13) | copy-start | bytes 184
  25.8 12.3 %copy-start.4 = (f32[384]{0:T(512)S(1)}, f32[384]{0:T(512)}, u32[]{:S(2)}) copy-start(f32[384]{0:T(512)} %param.15) | copy-start | bytes 4612
  25.9 12.8 %copy-start.5 = (f32[384]{0:T(512)S(1)}, f32[384]{0:T(512)}, u32[]{:S(2)}) copy-start(f32[384]{0:T(512)} %param.17) | copy-start | bytes 4612
  26.8 27.2 %all-to-all-start = ((bf16[16,32,384]{2,1,0:T(8,128)(2,1)}), bf16[16,32,384]{2,1,0:T(8,128)(2,1)S(1)}, u32[]{:S(2)}, u32[]{:S(2)}) async-start(bf16[16,32,384]{2,1,0:T(8,128)(2,1)} %bitcast.10), calls=%async_computation | async-start | bytes 786432 | tf_op jit(solution)/shard_map/all_to_all | solution.py:137
  54.0 0.7 copy-start.2

commit v12 on v11

--- a/solution.py
+++ b/solution.py
@@ -9,7 +9,7 @@
 SWEEPS = 3
 HALO = SWEEPS
 CHUNK = 384
-ROW_BLOCK = 32
+ROW_BLOCK = 16
 NT = (((1,), (1,)), ((), ()))
 
 RELAX_WEIGHTS = (0.8, 1.25, 0.95)

time: 89.1 us -> 89.3 us (level)
  no operation moved by 1% of the time
where the time goes in v12:
time: 89.3 us; the launch traced here: 88.9 us
  starting transfers between devices  22.4 us (25%)
  waiting for transfers between devices  18.9 us (21%)
  Pallas kernels  17.7 us (20%)
  blocking collectives  17.2 us (19%)
  local copies, waits for them, and re-layouts  6.4 us (7%)
  other arithmetic  6 us (7%)
    all_to_all x1, blocking collectives, on_device(): returned = lax.all_to_all(delta, 'field', 0, 0, tiled=True)  17.2 us
    pallas_call x1, Pallas kernels, surrogate_rows(): pl.pallas_call(mlp_kernel, grid=(rows // ROW_BLOCK,), in_specs=[pl.BlockS...  15.3 us
    all_to_all x1, waiting for transfers between devices, on_device(): incoming = lax.all_to_all(outgoing, 'field', 0, 0, tiled=True)  14.9 us
    all_to_all x1, starting transfers between devices, on_device(): incoming = lax.all_to_all(outgoing, 'field', 0, 0, tiled=True)  9.67 us
    ppermute x1, starting transfers between devices, with_halo(): lax.ppermute(head, axis, [(i + 1, i) for i in range(count - 1)])  8.47 us
    ppermute x1, starting transfers between devices, with_halo(): lax.ppermute(tail, axis, [(i, i + 1) for i in range(count - 1)])  4.28 us
    ppermute x1, waiting for transfers between devices, with_halo(): lax.ppermute(tail, axis, [(i, i + 1) for i in range(count - 1)])  2.86 us
    pallas_call x1, Pallas kernels, lookup(): pl.pallas_call(lookup_kernel, in_specs=[pl.BlockSpec(memory_space=pltpu.S...  2.43 us
  transfers between devices with their start and end apart: 3, of which 3 were waited for; matrix products, arithmetic and copies ran while one was open for 3% of the time, Pallas kernels for 0%

profile of v12, /device:TPU:8, one launch (start us, length us, event | category | flops | bytes accessed | tf_op | source)
XLA Modules:
  0.0 88.9 jit_solution(12617085514274000995)
XLA Ops:
  0.0 2.4 %shard_map.100 = f32[1,32,6144]{2,1,0:T(8,128)} custom-call(f32[1,8]{1,0:T(1,128)} %table_ref.1, s32[32,6144]{1,0:T(8,128)} %zone_ref.1), custom_call_target="tpu_custom_call" | custom-call | tf_op jit(solution)/shard_map/pallas_call | solution.py:47
  2.4 1.2 %pad_maximum_fusion.14 = (f32[2,3,6144]{2,1,0:T(4,128)S(1)}, f32[2,3,6144]{2,1,0:T(4,128)S(1)}) fusion(f32[1,32,6144]{2,1,0:T(8,128)} %shard_map.100, f32[1,32,6144]{2,1,0:T(8,128)S(1)} %copy-done.1), kind=kLoop, calls=%fused_computation.54 | loop fusion | flops 73728 | bytes 1867776 | tf_op jit(solution)/shard_map/slice | solution.py:61
  3.6 4.3 %collective-permute-start = (f32[2,3,6144]{2,1,0:T(4,128)S(1)}, f32[2,3,6144]{2,1,0:T(4,128)S(1)}, u32[]{:S(2)}, u32[]{:S(2)}) collective-permute-start(f32[2,3,6144]{2,1,0:T(4,128)S(1)} %get-tuple-element.17), channel_id=1, source_target_pairs={{0,16},{16,32},{32,48},{48,64},{64,80},{80,96},{96,112},{112,128},... | collective-permute-start | bytes 442376 | tf_op jit(solution)/shard_map/ppermute | solution.py:62
  7.9 8.5 %collective-permute-start.1 = (f32[2,3,6144]{2,1,0:T(4,128)S(1)}, f32[2,3,6144]{2,1,0:T(4,128)S(1)}, u32[]{:S(2)}, u32[]{:S(2)}) collective-permute-start(f32[2,3,6144]{2,1,0:T(4,128)S(1)} %get-tuple-element.18), channel_id=1, source_target_pairs={{16,0},{32,16},{48,32},{64,48},{80,64},{96,80},{112,96},{128,112},... | collective-permute-start | bytes 442376 | tf_op jit(solution)/shard_map/ppermute | solution.py:63
  16.5 2.9 %collective-permute-done = f32[2,3,6144]{2,1,0:T(4,128)S(1)} collective-permute-done((f32[2,3,6144]{2,1,0:T(4,128)S(1)}, f32[2,3,6144]{2,1,0:T(4,128)S(1)}, u32[]{:S(2)}, u32[]{:S(2)}) %collective-permute-start) | collective-permute-done | bytes 147488 | tf_op jit(solution)/shard_map/ppermute | solution.py:62
  19.3 1.2 %collective-permute-done.1 = f32[2,3,6144]{2,1,0:T(4,128)S(1)} collective-permute-done((f32[2,3,6144]{2,1,0:T(4,128)S(1)}, f32[2,3,6144]{2,1,0:T(4,128)S(1)}, u32[]{:S(2)}, u32[]{:S(2)}) %collective-permute-start.1) | collective-permute-done | bytes 147488 | tf_op jit(solution)/shard_map/ppermute | solution.py:63
  20.7 0.7 fusion.31
  21.5 0.7 add_add_fusion
  22.2 0.8 fusion.24
  23.4 0.8 fusion.23
  24.7 0.7 fusion.22
  25.4 0.5 fusion.27
  25.9 0.8 copy.19
  26.8 9.7 %all-to-all-start = ((bf16[16,32,384]{2,1,0:T(8,128)(2,1)}), bf16[16,32,384]{2,1,0:T(8,128)(2,1)S(1)}, u32[]{:S(2)}, u32[]{:S(2)}) async-start(bf16[16,32,384]{2,1,0:T(8,128)(2,1)} %bitcast.10), calls=%async_computation | async-start | bytes 786432 | tf_op jit(solution)/shard_map/all_to_all | solution.py:137
  36.4 0.7 copy.14.w_in_ref
  37.3 0.7 copy.15.rate_ref
  37.9 0.6 broadcast_in_dim.34.b_in_ref
  38.5 0.6 broadcast_in_dim.35.b_mid_ref
  39.1 14.9 %all-to-all-done.x_ref = bf16[16,32,384]{2,1,0:T(8,128)(2,1)S(1)} async-done(((bf16[16,32,384]{2,1,0:T(8,128)(2,1)}), bf16[16,32,384]{2,1,0:T(8,128)(2,1)S(1)}, u32[]{:S(2)}, u32[]{:S(2)}) %all-to-all-start) | async-done | bytes 393248 | tf_op jit(solution)/shard_map/all_to_all | solution.py:137
  54.0 0.7 copy-done.2
  54.7 15.3 %shard_map.101 = bf16[16,32,384]{2,1,0:T(8,128)(2,1)} custom-call(bf16[16,32,384]{2,1,0:T(8,128)(2,1)} %copy-done.2, bf16[384,16]{1,0:T(8,128)(2,1)} %copy.14.w_in_ref, f32[1,384]{1,0:T(1,128)} %broadcast_in_dim.34.b_in_ref, bf16[384,384]{1,0:T(8,128)(2,1)} %w_mid_ref.1, f32[1,384]{1,0:T(1,128)} %broadcast_in_dim.35.b_mid_ref, bf16[16,384]{1,0:T(8,128)(2,1)} %w_out_ref.1, ...), custom_call_target="tpu_custom_call" | custom-call | tf_op jit(solution)/shard_map/pallas_call | solution.py:91
  70.0 17.2 %all_to_all.10 = bf16[16,32,384]{2,1,0:T(8,128)(2,1)S(1)} all-to-all(bf16[16,32,384]{2,1,0:T(8,128)(2,1)} %shard_map.101), channel_id=1, replica_groups=mesh['space'=32,'field'=16] {'field'}, dimensions={0} | all-to-all | bytes 786432 | tf_op jit(solution)/shard_map/all_to_all | solution.py:149
  87.3 0.5 copy.16
  87.9 1.0 %add.85 = f32[1,32,6144]{2,1,0:T(8,128)} add(f32[1,32,6144]{2,1,0:T(8,128)S(1)} %get-tuple-element.6, f32[1,32,6144]{2,1,0:T(8,128)S(1)} %reshape.29) | non-fusion elementwise | flops 196608 | bytes 2359296 | tf_op jit(solution)/shard_map/add | solution.py:151
  (25 shorter events, 1.5 us)
Async XLA Ops:
  0.0 2.4 %copy-start.1 = (f32[1,32,6144]{2,1,0:T(8,128)S(1)}, f32[1,32,6144]{2,1,0:T(8,128)}, u32[]{:S(2)}) copy-start(f32[1,32,6144]{2,1,0:T(8,128)} %param.10) | copy-start | bytes 2359300
  2.4 18.1 %copy-start = (f32[1,32,6144]{2,1,0:T(8,128)S(1)}, f32[1,32,6144]{2,1,0:T(8,128)}, u32[]{:S(2)}) copy-start(f32[1,32,6144]{2,1,0:T(8,128)} %shard_map.100) | copy-start | bytes 2359300
  3.6 15.7 %collective-permute-start = (f32[2,3,6144]{2,1,0:T(4,128)S(1)}, f32[2,3,6144]{2,1,0:T(4,128)S(1)}, u32[]{:S(2)}, u32[]{:S(2)}) collective-permute-start(f32[2,3,6144]{2,1,0:T(4,128)S(1)} %get-tuple-element.17), channel_id=1, source_target_pairs={{0,16},{16,32},{32,48},{48,64},{64,80},{80,96},{96,112},{112,128},... | collective-permute-start | bytes 442376 | tf_op jit(solution)/shard_map/ppermute | solution.py:62
  7.9 12.6 %collective-permute-start.1 = (f32[2,3,6144]{2,1,0:T(4,128)S(1)}, f32[2,3,6144]{2,1,0:T(4,128)S(1)}, u32[]{:S(2)}, u32[]{:S(2)}) collective-permute-start(f32[2,3,6144]{2,1,0:T(4,128)S(1)} %get-tuple-element.18), channel_id=1, source_target_pairs={{16,0},{32,16},{48,32},{64,48},{80,64},{96,80},{112,96},{128,112},... | collective-permute-start | bytes 442376 | tf_op jit(solution)/shard_map/ppermute | solution.py:63
  25.8 10.6 %copy-start.3 = (bf16[384,16]{0,1:T(8,128)(2,1)S(1)}, bf16[384,16]{0,1:T(8,128)(2,1)}, u32[]{:S(2)}) copy-start(bf16[384,16]{0,1:T(8,128)(2,1)} %param.14) | copy-start | bytes 36868
  25.8 11.3 %copy-start.6 = (f32[15]{0:T(128)S(1)}, f32[15]{0:T(128)}, u32[]{:S(2)}) copy-start(f32[15]{0:T(128)} %param.13) | copy-start | bytes 184
  25.8 12.1 %copy-start.4 = (f32[384]{0:T(512)S(1)}, f32[384]{0:T(512)}, u32[]{:S(2)}) copy-start(f32[384]{0:T(512)} %param.15) | copy-start | bytes 4612
  25.9 12.7 %copy-start.5 = (f32[384]{0:T(512)S(1)}, f32[384]{0:T(512)}, u32[]{:S(2)}) copy-start(f32[384]{0:T(512)} %param.17) | copy-start | bytes 4612
  26.8 27.2 %all-to-all-start = ((bf16[16,32,384]{2,1,0:T(8,128)(2,1)}), bf16[16,32,384]{2,1,0:T(8,128)(2,1)S(1)}, u32[]{:S(2)}, u32[]{:S(2)}) async-start(bf16[16,32,384]{2,1,0:T(8,128)(2,1)} %bitcast.10), calls=%async_computation | async-start | bytes 786432 | tf_op jit(solution)/shard_map/all_to_all | solution.py:137
  54.0 0.7 copy-start.2

commit v13 on v8

--- a/solution.py
+++ b/solution.py
@@ -32,7 +32,7 @@
     return middle + weight * (source - image) / diagonal
 
 
-def lookup_kernel(table_ref, zone_ref, o_ref):
+def lookup_kernel(table_ref, zone_ref, fields_ref, o_ref, head_ref, tail_ref):
     zone = zone_ref[...]
     level = [table_ref[0, number] for number in range(table_ref.shape[1])]
     bit = 1
@@ -40,25 +40,36 @@
         pick = (zone & bit) != 0
         level = [jnp.where(pick, level[k + 1], level[k]) for k in range(0, len(level), 2)]
         bit *= 2
-    o_ref[0] = level[0]
+    coef = level[0]
+    o_ref[0] = coef
+    width = head_ref.shape[1]
+    here = fields_ref[0]
+    head_ref[0] = here[:width]
+    head_ref[1] = coef[:width]
+    tail_ref[0] = here[-width:]
+    tail_ref[1] = coef[-width:]
 
 
-def lookup(zone_ids, diffusivity):
+def lookup(zone_ids, diffusivity, fields, width):
+    rows, cols = zone_ids.shape
     return pl.pallas_call(
         lookup_kernel,
         in_specs=[
             pl.BlockSpec(memory_space=pltpu.SMEM),
             pl.BlockSpec(memory_space=pltpu.VMEM),
+            pl.BlockSpec(memory_space=pltpu.VMEM),
         ],
-        out_specs=pl.BlockSpec(memory_space=pltpu.VMEM),
-        out_shape=jax.ShapeDtypeStruct((1,) + zone_ids.shape, jnp.float32),
-    )(diffusivity, zone_ids)
+        out_specs=[pl.BlockSpec(memory_space=pltpu.VMEM)] * 3,
+        out_shape=[
+            jax.ShapeDtypeStruct((1, rows, cols), jnp.float32),
+            jax.ShapeDtypeStruct((2, width, cols), jnp.float32),
+            jax.ShapeDtypeStruct((2, width, cols), jnp.float32),
+        ],
+    )(diffusivity, zone_ids, fields)
 
 
-def with_halo(block, axis, width):
+def with_halo(block, head, tail, axis):
     count = lax.axis_size(axis)
-    head = block[:, :width]
-    tail = block[:, -width:]
     from_above = lax.ppermute(tail, axis, [(i, i + 1) for i in range(count - 1)])
     from_below = lax.ppermute(head, axis, [(i + 1, i) for i in range(count - 1)])
     return jnp.concatenate([from_above, block, from_below], axis=1)
@@ -110,8 +121,8 @@
     bias_out,
 ):
     count_here, rows_here, columns = fields.shape
-    coefs = lookup(zone_ids, diffusivity)
-    stacked = with_halo(jnp.concatenate([fields, coefs], 0), "space", HALO)
+    coefs, head, tail = lookup(zone_ids, diffusivity, fields, HALO)
+    stacked = with_halo(jnp.concatenate([fields, coefs], 0), head, tail, "space")
     fields_ext = stacked[:count_here]
     coef_pad = pad_rows(stacked[count_here:])
     first_row = lax.axis_index("space") * rows_here - HALO

time: 88.8 us -> 90.5 us (1.019)
  local copies, waits for them, and re-layouts: 7.6 us -> 8.65 us
    slice x1 -> x0, other arithmetic: 1.16 us -> none  [with_halo(): tail = block[:, -width:]]
    concatenate x1, other arithmetic: 0.21 us -> 1.36 us  [with_halo(): return jnp.concatenate([from_above, block, from_below], axis=1)]
    unnamed x14, local copies, waits for them, and re-layouts: 0.83 us -> 1.88 us
where the time goes in v13:
time: 90.5 us; the launch traced here: 90 us
  starting transfers between devices  22.4 us (25%)
  waiting for transfers between devices  19.3 us (21%)
  Pallas kernels  17.2 us (19%)
  blocking collectives  16.3 us (18%)
  local copies, waits for them, and re-layouts  8.65 us (10%)
  other arithmetic  5.98 us (7%)
    all_to_all x1, blocking collectives, on_device(): lax.all_to_all(delta.transpose(1, 0, 2), 'field', 0, 0, tiled=True)  16.3 us
    all_to_all x1, waiting for transfers between devices, on_device(): incoming = lax.all_to_all(outgoing, 'field', 0, 0, tiled=True)  14.9 us
    pallas_call x1, Pallas kernels, surrogate_rows(): pl.pallas_call(mlp_kernel, grid=(rows // ROW_BLOCK,), in_specs=[pl.BlockS...  14.4 us
    all_to_all x1, starting transfers between devices, on_device(): incoming = lax.all_to_all(outgoing, 'field', 0, 0, tiled=True)  9.67 us
    ppermute x1, starting transfers between devices, with_halo(): lax.ppermute(head, axis, [(i + 1, i) for i in range(count - 1)])  8.47 us
    ppermute x1, starting transfers between devices, with_halo(): lax.ppermute(tail, axis, [(i, i + 1) for i in range(count - 1)])  4.27 us
    ppermute x1, waiting for transfers between devices, with_halo(): lax.ppermute(tail, axis, [(i, i + 1) for i in range(count - 1)])  3.07 us
    pallas_call x1, Pallas kernels, lookup(): pl.pallas_call(lookup_kernel, in_specs=[pl.BlockSpec(memory_space=pltpu.S...  2.74 us
  transfers between devices with their start and end apart: 3, of which 3 were waited for; matrix products, arithmetic and copies ran while one was open for 3% of the time, Pallas kernels for 0%

profile of v13, /device:TPU:8, one launch (start us, length us, event | category | flops | bytes accessed | tf_op | source)
XLA Modules:
  0.0 90.0 jit_solution(7357468928974865887)
XLA Ops:
  0.0 2.7 %shard_map.100 = (f32[1,32,6144]{2,1,0:T(8,128)}, f32[2,3,6144]{2,1,0:T(4,128)}, f32[2,3,6144]{2,1,0:T(4,128)}) custom-call(f32[1,8]{1,0:T(1,128)} %table_ref.1, s32[32,6144]{1,0:T(8,128)} %zone_ref.1, f32[1,32,6144]{2,1,0:T(8,128)} %fields_ref.1), custom_call_target="tpu_custom_call" | custom-call | tf_op jit(solution)/shard_map/pallas_call | solution.py:55
  2.7 4.3 %collective-permute-start = (f32[2,3,6144]{2,1,0:T(4,128)}, f32[2,3,6144]{2,1,0:T(4,128)S(1)}, u32[]{:S(2)}, u32[]{:S(2)}) collective-permute-start(f32[2,3,6144]{2,1,0:T(4,128)} %get-tuple-element.8), channel_id=1, source_target_pairs={{0,16},{16,32},{32,48},{48,64},{64,80},{80,96},{96,112},{112,128},... | collective-permute-start | bytes 442376 | tf_op jit(solution)/shard_map/ppermute | solution.py:73
  7.0 8.5 %collective-permute-start.1 = (f32[2,3,6144]{2,1,0:T(4,128)}, f32[2,3,6144]{2,1,0:T(4,128)S(1)}, u32[]{:S(2)}, u32[]{:S(2)}) collective-permute-start(f32[2,3,6144]{2,1,0:T(4,128)} %get-tuple-element.10), channel_id=1, source_target_pairs={{16,0},{32,16},{48,32},{64,48},{80,64},{96,80},{112,96},{128,112},... | collective-permute-start | bytes 442376 | tf_op jit(solution)/shard_map/ppermute | solution.py:74
  15.6 3.1 %collective-permute-done = f32[2,3,6144]{2,1,0:T(4,128)S(1)} collective-permute-done((f32[2,3,6144]{2,1,0:T(4,128)}, f32[2,3,6144]{2,1,0:T(4,128)S(1)}, u32[]{:S(2)}, u32[]{:S(2)}) %collective-permute-start) | collective-permute-done | bytes 147488 | tf_op jit(solution)/shard_map/ppermute | solution.py:73
  18.7 1.3 %collective-permute-done.1 = f32[2,3,6144]{2,1,0:T(4,128)S(1)} collective-permute-done((f32[2,3,6144]{2,1,0:T(4,128)}, f32[2,3,6144]{2,1,0:T(4,128)S(1)}, u32[]{:S(2)}, u32[]{:S(2)}) %collective-permute-start.1) | collective-permute-done | bytes 147488 | tf_op jit(solution)/shard_map/ppermute | solution.py:74
  20.0 1.4 %pad_maximum_fusion = f32[2,38,6144]{2,1,0:T(8,128)S(1)} fusion(f32[2,3,6144]{2,1,0:T(4,128)S(1)} %collective-permute-done.1, f32[1,32,6144]{2,1,0:T(8,128)} %get-tuple-element.9, f32[1,32,6144]{2,1,0:T(8,128)S(1)} %copy-done, f32[2,3,6144]{2,1,0:T(4,128)S(1)} %collective-permute-done), kind=kLoop, calls=%fused_computation | loop fusion | flops 1400832 | bytes 3735552 | tf_op jit(solution)/shard_map/concatenate | solution.py:75
  21.3 0.7 fusion.31
  22.1 1.1 %copy-done.1 = f32[1,32,6144]{2,1,0:T(8,128)S(1)} copy-done((f32[1,32,6144]{2,1,0:T(8,128)S(1)}, f32[1,32,6144]{2,1,0:T(8,128)}, u32[]{:S(2)}) %copy-start.1) | copy-done | bytes 786456
  23.1 0.7 add_add_fusion
  23.8 0.8 fusion.24
  25.1 0.8 fusion.23
  26.3 0.7 fusion.22
  27.6 0.8 copy.23
  28.4 9.7 %all-to-all-start = ((bf16[16,32,384]{2,1,0:T(8,128)(2,1)}), bf16[16,32,384]{2,1,0:T(8,128)(2,1)S(1)}, u32[]{:S(2)}, u32[]{:S(2)}) async-start(bf16[16,32,384]{2,1,0:T(8,128)(2,1)} %bitcast.14), calls=%async_computation | async-start | bytes 786432 | tf_op jit(solution)/shard_map/all_to_all | solution.py:139
  38.1 0.8 copy.15.w_in_ref
  38.9 0.7 copy.16.rate_ref
  39.6 0.6 broadcast_in_dim.34.b_in_ref
  40.2 0.6 broadcast_in_dim.35.b_mid_ref
  40.7 14.9 %all-to-all-done = bf16[16,32,384]{2,1,0:T(8,128)(2,1)S(1)} async-done(((bf16[16,32,384]{2,1,0:T(8,128)(2,1)}), bf16[16,32,384]{2,1,0:T(8,128)(2,1)S(1)}, u32[]{:S(2)}, u32[]{:S(2)}) %all-to-all-start) | async-done | bytes 393248 | tf_op jit(solution)/shard_map/all_to_all | solution.py:139
  55.6 0.9 copy.22
  56.5 14.4 %shard_map.101 = bf16[32,16,384]{2,1,0:T(8,128)(2,1)} custom-call(bf16[32,16,384]{2,1,0:T(8,128)(2,1)} %bitcast.15, bf16[384,16]{1,0:T(8,128)(2,1)} %copy.15.w_in_ref, f32[1,384]{1,0:T(1,128)} %broadcast_in_dim.34.b_in_ref, bf16[384,384]{1,0:T(8,128)(2,1)} %w_mid_ref.1, f32[1,384]{1,0:T(1,128)} %broadcast_in_dim.35.b_mid_ref, bf16[16,384]{1,0:T(8,128)(2,1)} %w_out_ref.1, ...), custom_call_target="tpu_custom_call" | custom-call | tf_op jit(solution)/shard_map/pallas_call | solution.py:100
  71.0 1.1 %copy.17 = bf16[16,32,384]{2,1,0:T(8,128)(2,1)S(1)} copy(bf16[16,32,384]{2,0,1:T(8,128)(2,1)} %bitcast.16) | data formatting | bytes 786432 | tf_op jit(solution)/shard_map/transpose | solution.py:151
  72.0 16.3 %all_to_all.10 = bf16[16,32,384]{2,1,0:T(8,128)(2,1)S(1)} all-to-all(bf16[16,32,384]{2,1,0:T(8,128)(2,1)S(1)} %copy.17), channel_id=1, replica_groups=mesh['space'=32,'field'=16] {'field'}, dimensions={0} | all-to-all | bytes 786432 | tf_op jit(solution)/shard_map/all_to_all | solution.py:151
  89.0 1.0 %add.85 = f32[1,32,6144]{2,1,0:T(8,128)} add(f32[1,32,6144]{2,1,0:T(8,128)S(1)} %get-tuple-element.12, f32[1,32,6144]{2,1,0:T(8,128)S(1)} %reshape.29) | non-fusion elementwise | flops 196608 | bytes 2359296 | tf_op jit(solution)/shard_map/add | solution.py:153
  (24 shorter events, 2.2 us)
Async XLA Ops:
  0.0 20.0 %copy-start = (f32[1,32,6144]{2,1,0:T(8,128)S(1)}, f32[1,32,6144]{2,1,0:T(8,128)}, u32[]{:S(2)}) copy-start(f32[1,32,6144]{2,1,0:T(8,128)} %fields_ref.1) | copy-start | bytes 2359300
  2.7 15.9 %collective-permute-start = (f32[2,3,6144]{2,1,0:T(4,128)}, f32[2,3,6144]{2,1,0:T(4,128)S(1)}, u32[]{:S(2)}, u32[]{:S(2)}) collective-permute-start(f32[2,3,6144]{2,1,0:T(4,128)} %get-tuple-element.8), channel_id=1, source_target_pairs={{0,16},{16,32},{32,48},{48,64},{64,80},{80,96},{96,112},{112,128},... | collective-permute-start | bytes 442376 | tf_op jit(solution)/shard_map/ppermute | solution.py:73
  7.0 12.9 %collective-permute-start.1 = (f32[2,3,6144]{2,1,0:T(4,128)}, f32[2,3,6144]{2,1,0:T(4,128)S(1)}, u32[]{:S(2)}, u32[]{:S(2)}) collective-permute-start(f32[2,3,6144]{2,1,0:T(4,128)} %get-tuple-element.10), channel_id=1, source_target_pairs={{16,0},{32,16},{48,32},{64,48},{80,64},{96,80},{112,96},{128,112},... | collective-permute-start | bytes 442376 | tf_op jit(solution)/shard_map/ppermute | solution.py:74
  22.0 1.1 %copy-start.1 = (f32[1,32,6144]{2,1,0:T(8,128)S(1)}, f32[1,32,6144]{2,1,0:T(8,128)}, u32[]{:S(2)}) copy-start(f32[1,32,6144]{2,1,0:T(8,128)} %get-tuple-element.9) | copy-start | bytes 2359300
  27.5 10.6 %copy-start.2 = (bf16[384,16]{0,1:T(8,128)(2,1)S(1)}, bf16[384,16]{0,1:T(8,128)(2,1)}, u32[]{:S(2)}) copy-start(bf16[384,16]{0,1:T(8,128)(2,1)} %param.14) | copy-start | bytes 36868
  27.5 11.4 %copy-start.5 = (f32[15]{0:T(128)S(1)}, f32[15]{0:T(128)}, u32[]{:S(2)}) copy-start(f32[15]{0:T(128)} %param.13) | copy-start | bytes 184
  27.5 12.1 %copy-start.3 = (f32[384]{0:T(512)S(1)}, f32[384]{0:T(512)}, u32[]{:S(2)}) copy-start(f32[384]{0:T(512)} %param.15) | copy-start | bytes 4612
  27.5 12.7 %copy-start.4 = (f32[384]{0:T(512)S(1)}, f32[384]{0:T(512)}, u32[]{:S(2)}) copy-start(f32[384]{0:T(512)} %param.17) | copy-start | bytes 4612
  28.4 27.2 %all-to-all-start = ((bf16[16,32,384]{2,1,0:T(8,128)(2,1)}), bf16[16,32,384]{2,1,0:T(8,128)(2,1)S(1)}, u32[]{:S(2)}, u32[]{:S(2)}) async-start(bf16[16,32,384]{2,1,0:T(8,128)(2,1)} %bitcast.14), calls=%async_computation | async-start | bytes 786432 | tf_op jit(solution)/shard_map/all_to_all | solution.py:139

commit v14 on v8

--- a/solution.py
+++ b/solution.py
@@ -9,7 +9,7 @@
 SWEEPS = 3
 HALO = SWEEPS
 CHUNK = 384
-ROW_BLOCK = 8
+ROW_BLOCK = 16
 NT = (((1,), (1,)), ((), ()))
 
 RELAX_WEIGHTS = (0.8, 1.25, 0.95)

time: 88.8 us -> 88.4 us (level)
  no operation moved by 1% of the time
where the time goes in v14:
time: 88.4 us; the launch traced here: 88 us
  starting transfers between devices  22.4 us (25%)
  waiting for transfers between devices  18.9 us (21%)
  Pallas kernels  16.5 us (19%)
  blocking collectives  16.3 us (18%)
  local copies, waits for them, and re-layouts  7.6 us (9%)
  other arithmetic  6 us (7%)
    all_to_all x1, blocking collectives, on_device(): lax.all_to_all(delta.transpose(1, 0, 2), 'field', 0, 0, tiled=True)  16.3 us
    all_to_all x1, waiting for transfers between devices, on_device(): incoming = lax.all_to_all(outgoing, 'field', 0, 0, tiled=True)  14.9 us
    pallas_call x1, Pallas kernels, surrogate_rows(): pl.pallas_call(mlp_kernel, grid=(rows // ROW_BLOCK,), in_specs=[pl.BlockS...  14.1 us
    all_to_all x1, starting transfers between devices, on_device(): incoming = lax.all_to_all(outgoing, 'field', 0, 0, tiled=True)  9.67 us
    ppermute x1, starting transfers between devices, with_halo(): lax.ppermute(head, axis, [(i + 1, i) for i in range(count - 1)])  8.47 us
    ppermute x1, starting transfers between devices, with_halo(): lax.ppermute(tail, axis, [(i, i + 1) for i in range(count - 1)])  4.28 us
    ppermute x1, waiting for transfers between devices, with_halo(): lax.ppermute(tail, axis, [(i, i + 1) for i in range(count - 1)])  2.86 us
    pallas_call x1, Pallas kernels, lookup(): pl.pallas_call(lookup_kernel, in_specs=[pl.BlockSpec(memory_space=pltpu.S...  2.43 us
  transfers between devices with their start and end apart: 3, of which 3 were waited for; matrix products, arithmetic and copies ran while one was open for 3% of the time, Pallas kernels for 0%

profile of v14, /device:TPU:8, one launch (start us, length us, event | category | flops | bytes accessed | tf_op | source)
XLA Modules:
  0.0 88.0 jit_solution(11642071191319874884)
XLA Ops:
  0.0 2.4 %shard_map.100 = f32[1,32,6144]{2,1,0:T(8,128)} custom-call(f32[1,8]{1,0:T(1,128)} %table_ref.1, s32[32,6144]{1,0:T(8,128)} %zone_ref.1), custom_call_target="tpu_custom_call" | custom-call | tf_op jit(solution)/shard_map/pallas_call | solution.py:47
  2.4 1.2 %pad_maximum_fusion.14 = (f32[2,3,6144]{2,1,0:T(4,128)S(1)}, f32[2,3,6144]{2,1,0:T(4,128)S(1)}) fusion(f32[1,32,6144]{2,1,0:T(8,128)} %shard_map.100, f32[1,32,6144]{2,1,0:T(8,128)S(1)} %copy-done.1), kind=kLoop, calls=%fused_computation.55 | loop fusion | flops 73728 | bytes 1867776 | tf_op jit(solution)/shard_map/slice | solution.py:61
  3.6 4.3 %collective-permute-start = (f32[2,3,6144]{2,1,0:T(4,128)S(1)}, f32[2,3,6144]{2,1,0:T(4,128)S(1)}, u32[]{:S(2)}, u32[]{:S(2)}) collective-permute-start(f32[2,3,6144]{2,1,0:T(4,128)S(1)} %get-tuple-element.17), channel_id=1, source_target_pairs={{0,16},{16,32},{32,48},{48,64},{64,80},{80,96},{96,112},{112,128},... | collective-permute-start | bytes 442376 | tf_op jit(solution)/shard_map/ppermute | solution.py:62
  7.9 8.5 %collective-permute-start.1 = (f32[2,3,6144]{2,1,0:T(4,128)S(1)}, f32[2,3,6144]{2,1,0:T(4,128)S(1)}, u32[]{:S(2)}, u32[]{:S(2)}) collective-permute-start(f32[2,3,6144]{2,1,0:T(4,128)S(1)} %get-tuple-element.18), channel_id=1, source_target_pairs={{16,0},{32,16},{48,32},{64,48},{80,64},{96,80},{112,96},{128,112},... | collective-permute-start | bytes 442376 | tf_op jit(solution)/shard_map/ppermute | solution.py:63
  16.5 2.9 %collective-permute-done = f32[2,3,6144]{2,1,0:T(4,128)S(1)} collective-permute-done((f32[2,3,6144]{2,1,0:T(4,128)S(1)}, f32[2,3,6144]{2,1,0:T(4,128)S(1)}, u32[]{:S(2)}, u32[]{:S(2)}) %collective-permute-start) | collective-permute-done | bytes 147488 | tf_op jit(solution)/shard_map/ppermute | solution.py:62
  19.3 1.2 %collective-permute-done.1 = f32[2,3,6144]{2,1,0:T(4,128)S(1)} collective-permute-done((f32[2,3,6144]{2,1,0:T(4,128)S(1)}, f32[2,3,6144]{2,1,0:T(4,128)S(1)}, u32[]{:S(2)}, u32[]{:S(2)}) %collective-permute-start.1) | collective-permute-done | bytes 147488 | tf_op jit(solution)/shard_map/ppermute | solution.py:63
  20.7 0.7 fusion.31
  21.5 0.7 add_add_fusion
  22.2 0.8 fusion.24
  23.4 0.8 fusion.23
  24.7 0.7 fusion.22
  25.4 0.5 fusion.27
  25.9 0.8 copy.23
  26.8 9.7 %all-to-all-start = ((bf16[16,32,384]{2,1,0:T(8,128)(2,1)}), bf16[16,32,384]{2,1,0:T(8,128)(2,1)S(1)}, u32[]{:S(2)}, u32[]{:S(2)}) async-start(bf16[16,32,384]{2,1,0:T(8,128)(2,1)} %bitcast.14), calls=%async_computation | async-start | bytes 786432 | tf_op jit(solution)/shard_map/all_to_all | solution.py:128
  36.4 0.8 copy.15.w_in_ref
  37.3 0.7 copy.16.rate_ref
  38.0 0.6 broadcast_in_dim.34.b_in_ref
  38.5 0.6 broadcast_in_dim.35.b_mid_ref
  39.1 14.9 %all-to-all-done = bf16[16,32,384]{2,1,0:T(8,128)(2,1)S(1)} async-done(((bf16[16,32,384]{2,1,0:T(8,128)(2,1)}), bf16[16,32,384]{2,1,0:T(8,128)(2,1)S(1)}, u32[]{:S(2)}, u32[]{:S(2)}) %all-to-all-start) | async-done | bytes 393248 | tf_op jit(solution)/shard_map/all_to_all | solution.py:128
  54.0 0.9 copy.22
  54.9 14.1 %shard_map.101 = bf16[32,16,384]{2,1,0:T(8,128)(2,1)} custom-call(bf16[32,16,384]{2,1,0:T(8,128)(2,1)} %bitcast.15, bf16[384,16]{1,0:T(8,128)(2,1)} %copy.15.w_in_ref, f32[1,384]{1,0:T(1,128)} %broadcast_in_dim.34.b_in_ref, bf16[384,384]{1,0:T(8,128)(2,1)} %w_mid_ref.1, f32[1,384]{1,0:T(1,128)} %broadcast_in_dim.35.b_mid_ref, bf16[16,384]{1,0:T(8,128)(2,1)} %w_out_ref.1, ...), custom_call_target="tpu_custom_call" | custom-call | tf_op jit(solution)/shard_map/pallas_call | solution.py:89
  69.0 1.1 %copy.17 = bf16[16,32,384]{2,1,0:T(8,128)(2,1)S(1)} copy(bf16[16,32,384]{2,0,1:T(8,128)(2,1)} %bitcast.16) | data formatting | bytes 786432 | tf_op jit(solution)/shard_map/transpose | solution.py:140
  70.1 16.3 %all_to_all.10 = bf16[16,32,384]{2,1,0:T(8,128)(2,1)S(1)} all-to-all(bf16[16,32,384]{2,1,0:T(8,128)(2,1)S(1)} %copy.17), channel_id=1, replica_groups=mesh['space'=32,'field'=16] {'field'}, dimensions={0} | all-to-all | bytes 786432 | tf_op jit(solution)/shard_map/all_to_all | solution.py:140
  87.0 1.0 %add.85 = f32[1,32,6144]{2,1,0:T(8,128)} add(f32[1,32,6144]{2,1,0:T(8,128)S(1)} %get-tuple-element.6, f32[1,32,6144]{2,1,0:T(8,128)S(1)} %reshape.29) | non-fusion elementwise | flops 196608 | bytes 2359296 | tf_op jit(solution)/shard_map/add | solution.py:142
  (25 shorter events, 2.0 us)
Async XLA Ops:
  0.0 2.4 %copy-start.1 = (f32[1,32,6144]{2,1,0:T(8,128)S(1)}, f32[1,32,6144]{2,1,0:T(8,128)}, u32[]{:S(2)}) copy-start(f32[1,32,6144]{2,1,0:T(8,128)} %param.10) | copy-start | bytes 2359300
  2.4 18.1 %copy-start = (f32[1,32,6144]{2,1,0:T(8,128)S(1)}, f32[1,32,6144]{2,1,0:T(8,128)}, u32[]{:S(2)}) copy-start(f32[1,32,6144]{2,1,0:T(8,128)} %shard_map.100) | copy-start | bytes 2359300
  3.6 15.7 %collective-permute-start = (f32[2,3,6144]{2,1,0:T(4,128)S(1)}, f32[2,3,6144]{2,1,0:T(4,128)S(1)}, u32[]{:S(2)}, u32[]{:S(2)}) collective-permute-start(f32[2,3,6144]{2,1,0:T(4,128)S(1)} %get-tuple-element.17), channel_id=1, source_target_pairs={{0,16},{16,32},{32,48},{48,64},{64,80},{80,96},{96,112},{112,128},... | collective-permute-start | bytes 442376 | tf_op jit(solution)/shard_map/ppermute | solution.py:62
  7.9 12.6 %collective-permute-start.1 = (f32[2,3,6144]{2,1,0:T(4,128)S(1)}, f32[2,3,6144]{2,1,0:T(4,128)S(1)}, u32[]{:S(2)}, u32[]{:S(2)}) collective-permute-start(f32[2,3,6144]{2,1,0:T(4,128)S(1)} %get-tuple-element.18), channel_id=1, source_target_pairs={{16,0},{32,16},{48,32},{64,48},{80,64},{96,80},{112,96},{128,112},... | collective-permute-start | bytes 442376 | tf_op jit(solution)/shard_map/ppermute | solution.py:63
  25.8 10.6 %copy-start.2 = (bf16[384,16]{0,1:T(8,128)(2,1)S(1)}, bf16[384,16]{0,1:T(8,128)(2,1)}, u32[]{:S(2)}) copy-start(bf16[384,16]{0,1:T(8,128)(2,1)} %param.14) | copy-start | bytes 36868
  25.8 11.4 %copy-start.5 = (f32[15]{0:T(128)S(1)}, f32[15]{0:T(128)}, u32[]{:S(2)}) copy-start(f32[15]{0:T(128)} %param.13) | copy-start | bytes 184
  25.8 12.1 %copy-start.3 = (f32[384]{0:T(512)S(1)}, f32[384]{0:T(512)}, u32[]{:S(2)}) copy-start(f32[384]{0:T(512)} %param.15) | copy-start | bytes 4612
  25.9 12.7 %copy-start.4 = (f32[384]{0:T(512)S(1)}, f32[384]{0:T(512)}, u32[]{:S(2)}) copy-start(f32[384]{0:T(512)} %param.17) | copy-start | bytes 4612
  26.8 27.2 %all-to-all-start = ((bf16[16,32,384]{2,1,0:T(8,128)(2,1)}), bf16[16,32,384]{2,1,0:T(8,128)(2,1)S(1)}, u32[]{:S(2)}, u32[]{:S(2)}) async-start(bf16[16,32,384]{2,1,0:T(8,128)(2,1)} %bitcast.14), calls=%async_computation | async-start | bytes 786432 | tf_op jit(solution)/shard_map/all_to_all | solution.py:128

commit v15 on v14

--- a/solution.py
+++ b/solution.py
@@ -9,7 +9,7 @@
 SWEEPS = 3
 HALO = SWEEPS
 CHUNK = 384
-ROW_BLOCK = 16
+ROW_BLOCK = 32
 NT = (((1,), (1,)), ((), ()))
 
 RELAX_WEIGHTS = (0.8, 1.25, 0.95)

time: 88.4 us -> 88.2 us (level)
  no operation moved by 1% of the time
where the time goes in v15:
time: 88.2 us; the launch traced here: 87.7 us
  starting transfers between devices  22.6 us (26%)
  waiting for transfers between devices  18.8 us (21%)
  Pallas kernels  16.3 us (18%)
  blocking collectives  16.3 us (18%)
  local copies, waits for them, and re-layouts  7.6 us (9%)
  other arithmetic  6 us (7%)
    all_to_all x1, blocking collectives, on_device(): lax.all_to_all(delta.transpose(1, 0, 2), 'field', 0, 0, tiled=True)  16.3 us
    all_to_all x1, waiting for transfers between devices, on_device(): incoming = lax.all_to_all(outgoing, 'field', 0, 0, tiled=True)  14.7 us
    pallas_call x1, Pallas kernels, surrogate_rows(): pl.pallas_call(mlp_kernel, grid=(rows // ROW_BLOCK,), in_specs=[pl.BlockS...  13.9 us
    all_to_all x1, starting transfers between devices, on_device(): incoming = lax.all_to_all(outgoing, 'field', 0, 0, tiled=True)  9.85 us
    ppermute x1, starting transfers between devices, with_halo(): lax.ppermute(head, axis, [(i + 1, i) for i in range(count - 1)])  8.47 us
    ppermute x1, starting transfers between devices, with_halo(): lax.ppermute(tail, axis, [(i, i + 1) for i in range(count - 1)])  4.28 us
    ppermute x1, waiting for transfers between devices, with_halo(): lax.ppermute(tail, axis, [(i, i + 1) for i in range(count - 1)])  2.86 us
    pallas_call x1, Pallas kernels, lookup(): pl.pallas_call(lookup_kernel, in_specs=[pl.BlockSpec(memory_space=pltpu.S...  2.43 us
  transfers between devices with their start and end apart: 3, of which 3 were waited for; matrix products, arithmetic and copies ran while one was open for 3% of the time, Pallas kernels for 0%

profile of v15, /device:TPU:8, one launch (start us, length us, event | category | flops | bytes accessed | tf_op | source)
XLA Modules:
  0.0 87.7 jit_solution(14058313238713847106)
XLA Ops:
  0.0 2.4 %shard_map.100 = f32[1,32,6144]{2,1,0:T(8,128)} custom-call(f32[1,8]{1,0:T(1,128)} %table_ref.1, s32[32,6144]{1,0:T(8,128)} %zone_ref.1), custom_call_target="tpu_custom_call" | custom-call | tf_op jit(solution)/shard_map/pallas_call | solution.py:47
  2.4 1.2 %pad_maximum_fusion.14 = (f32[2,3,6144]{2,1,0:T(4,128)S(1)}, f32[2,3,6144]{2,1,0:T(4,128)S(1)}) fusion(f32[1,32,6144]{2,1,0:T(8,128)} %shard_map.100, f32[1,32,6144]{2,1,0:T(8,128)S(1)} %copy-done.1), kind=kLoop, calls=%fused_computation.55 | loop fusion | flops 73728 | bytes 1867776 | tf_op jit(solution)/shard_map/slice | solution.py:61
  3.6 4.3 %collective-permute-start = (f32[2,3,6144]{2,1,0:T(4,128)S(1)}, f32[2,3,6144]{2,1,0:T(4,128)S(1)}, u32[]{:S(2)}, u32[]{:S(2)}) collective-permute-start(f32[2,3,6144]{2,1,0:T(4,128)S(1)} %get-tuple-element.17), channel_id=1, source_target_pairs={{0,16},{16,32},{32,48},{48,64},{64,80},{80,96},{96,112},{112,128},... | collective-permute-start | bytes 442376 | tf_op jit(solution)/shard_map/ppermute | solution.py:62
  7.9 8.5 %collective-permute-start.1 = (f32[2,3,6144]{2,1,0:T(4,128)S(1)}, f32[2,3,6144]{2,1,0:T(4,128)S(1)}, u32[]{:S(2)}, u32[]{:S(2)}) collective-permute-start(f32[2,3,6144]{2,1,0:T(4,128)S(1)} %get-tuple-element.18), channel_id=1, source_target_pairs={{16,0},{32,16},{48,32},{64,48},{80,64},{96,80},{112,96},{128,112},... | collective-permute-start | bytes 442376 | tf_op jit(solution)/shard_map/ppermute | solution.py:63
  16.5 2.9 %collective-permute-done = f32[2,3,6144]{2,1,0:T(4,128)S(1)} collective-permute-done((f32[2,3,6144]{2,1,0:T(4,128)S(1)}, f32[2,3,6144]{2,1,0:T(4,128)S(1)}, u32[]{:S(2)}, u32[]{:S(2)}) %collective-permute-start) | collective-permute-done | bytes 147488 | tf_op jit(solution)/shard_map/ppermute | solution.py:62
  19.3 1.2 %collective-permute-done.1 = f32[2,3,6144]{2,1,0:T(4,128)S(1)} collective-permute-done((f32[2,3,6144]{2,1,0:T(4,128)S(1)}, f32[2,3,6144]{2,1,0:T(4,128)S(1)}, u32[]{:S(2)}, u32[]{:S(2)}) %collective-permute-start.1) | collective-permute-done | bytes 147488 | tf_op jit(solution)/shard_map/ppermute | solution.py:63
  20.7 0.7 fusion.31
  21.5 0.7 add_add_fusion
  22.2 0.8 fusion.24
  23.4 0.8 fusion.23
  24.7 0.7 fusion.22
  25.4 0.5 fusion.27
  25.9 0.8 copy.23
  26.8 9.8 %all-to-all-start = ((bf16[16,32,384]{2,1,0:T(8,128)(2,1)}), bf16[16,32,384]{2,1,0:T(8,128)(2,1)S(1)}, u32[]{:S(2)}, u32[]{:S(2)}) async-start(bf16[16,32,384]{2,1,0:T(8,128)(2,1)} %bitcast.14), calls=%async_computation | async-start | bytes 786432 | tf_op jit(solution)/shard_map/all_to_all | solution.py:128
  36.6 0.8 copy.15.w_in_ref
  37.4 0.7 copy.16.rate_ref
  38.1 0.6 broadcast_in_dim.34.b_in_ref
  38.7 0.6 broadcast_in_dim.35.b_mid_ref
  39.3 14.7 %all-to-all-done = bf16[16,32,384]{2,1,0:T(8,128)(2,1)S(1)} async-done(((bf16[16,32,384]{2,1,0:T(8,128)(2,1)}), bf16[16,32,384]{2,1,0:T(8,128)(2,1)S(1)}, u32[]{:S(2)}, u32[]{:S(2)}) %all-to-all-start) | async-done | bytes 393248 | tf_op jit(solution)/shard_map/all_to_all | solution.py:128
  54.0 0.9 copy.22
  54.9 13.9 %shard_map.101 = bf16[32,16,384]{2,1,0:T(8,128)(2,1)} custom-call(bf16[32,16,384]{2,1,0:T(8,128)(2,1)} %bitcast.15, bf16[384,16]{1,0:T(8,128)(2,1)} %copy.15.w_in_ref, f32[1,384]{1,0:T(1,128)} %broadcast_in_dim.34.b_in_ref, bf16[384,384]{1,0:T(8,128)(2,1)} %w_mid_ref.1, f32[1,384]{1,0:T(1,128)} %broadcast_in_dim.35.b_mid_ref, bf16[16,384]{1,0:T(8,128)(2,1)} %w_out_ref.1, ...), custom_call_target="tpu_custom_call" | custom-call | tf_op jit(solution)/shard_map/pallas_call | solution.py:89
  68.7 1.1 %copy.17 = bf16[16,32,384]{2,1,0:T(8,128)(2,1)S(1)} copy(bf16[16,32,384]{2,0,1:T(8,128)(2,1)} %bitcast.16) | data formatting | bytes 786432 | tf_op jit(solution)/shard_map/transpose | solution.py:140
  69.8 16.3 %all_to_all.10 = bf16[16,32,384]{2,1,0:T(8,128)(2,1)S(1)} all-to-all(bf16[16,32,384]{2,1,0:T(8,128)(2,1)S(1)} %copy.17), channel_id=1, replica_groups=mesh['space'=32,'field'=16] {'field'}, dimensions={0} | all-to-all | bytes 786432 | tf_op jit(solution)/shard_map/all_to_all | solution.py:140
  86.8 1.0 %add.85 = f32[1,32,6144]{2,1,0:T(8,128)} add(f32[1,32,6144]{2,1,0:T(8,128)S(1)} %get-tuple-element.6, f32[1,32,6144]{2,1,0:T(8,128)S(1)} %reshape.29) | non-fusion elementwise | flops 196608 | bytes 2359296 | tf_op jit(solution)/shard_map/add | solution.py:142
  (25 shorter events, 2.0 us)
Async XLA Ops:
  0.0 2.4 %copy-start.1 = (f32[1,32,6144]{2,1,0:T(8,128)S(1)}, f32[1,32,6144]{2,1,0:T(8,128)}, u32[]{:S(2)}) copy-start(f32[1,32,6144]{2,1,0:T(8,128)} %param.10) | copy-start | bytes 2359300
  2.4 18.1 %copy-start = (f32[1,32,6144]{2,1,0:T(8,128)S(1)}, f32[1,32,6144]{2,1,0:T(8,128)}, u32[]{:S(2)}) copy-start(f32[1,32,6144]{2,1,0:T(8,128)} %shard_map.100) | copy-start | bytes 2359300
  3.6 15.7 %collective-permute-start = (f32[2,3,6144]{2,1,0:T(4,128)S(1)}, f32[2,3,6144]{2,1,0:T(4,128)S(1)}, u32[]{:S(2)}, u32[]{:S(2)}) collective-permute-start(f32[2,3,6144]{2,1,0:T(4,128)S(1)} %get-tuple-element.17), channel_id=1, source_target_pairs={{0,16},{16,32},{32,48},{48,64},{64,80},{80,96},{96,112},{112,128},... | collective-permute-start | bytes 442376 | tf_op jit(solution)/shard_map/ppermute | solution.py:62
  7.9 12.6 %collective-permute-start.1 = (f32[2,3,6144]{2,1,0:T(4,128)S(1)}, f32[2,3,6144]{2,1,0:T(4,128)S(1)}, u32[]{:S(2)}, u32[]{:S(2)}) collective-permute-start(f32[2,3,6144]{2,1,0:T(4,128)S(1)} %get-tuple-element.18), channel_id=1, source_target_pairs={{16,0},{32,16},{48,32},{64,48},{80,64},{96,80},{112,96},{128,112},... | collective-permute-start | bytes 442376 | tf_op jit(solution)/shard_map/ppermute | solution.py:63
  25.8 10.8 %copy-start.2 = (bf16[384,16]{0,1:T(8,128)(2,1)S(1)}, bf16[384,16]{0,1:T(8,128)(2,1)}, u32[]{:S(2)}) copy-start(bf16[384,16]{0,1:T(8,128)(2,1)} %param.14) | copy-start | bytes 36868
  25.8 11.5 %copy-start.5 = (f32[15]{0:T(128)S(1)}, f32[15]{0:T(128)}, u32[]{:S(2)}) copy-start(f32[15]{0:T(128)} %param.13) | copy-start | bytes 184
  25.8 12.3 %copy-start.3 = (f32[384]{0:T(512)S(1)}, f32[384]{0:T(512)}, u32[]{:S(2)}) copy-start(f32[384]{0:T(512)} %param.15) | copy-start | bytes 4612
  25.9 12.8 %copy-start.4 = (f32[384]{0:T(512)S(1)}, f32[384]{0:T(512)}, u32[]{:S(2)}) copy-start(f32[384]{0:T(512)} %param.17) | copy-start | bytes 4612
  26.8 27.2 %all-to-all-start = ((bf16[16,32,384]{2,1,0:T(8,128)(2,1)}), bf16[16,32,384]{2,1,0:T(8,128)(2,1)S(1)}, u32[]{:S(2)}, u32[]{:S(2)}) async-start(bf16[16,32,384]{2,1,0:T(8,128)(2,1)} %bitcast.14), calls=%async_computation | async-start | bytes 786432 | tf_op jit(solution)/shard_map/all_to_all | solution.py:128
